TPU v7x, 512 devices: a whole 4x8x8 slice. The times are simulated.
512 devices in a mesh: gx: 8 (over x, core), gy: 8 (over y), gz: 8 (over z).
Axes of the slice: x: 4, y: 8, z: 8, core: 2. Of those that a mesh axis runs over, the one named last changes fastest.
Arguments:
- features: bfloat16 [32, 16, 128, 1024], P(None, 'gx', 'gy', 'gz'), may hold values from -6 to 6
- voxel_slot: int32 [16, 128, 1024], P('gx', 'gy', 'gz'), may hold values from 0 to 1023
- conv_weight: bfloat16 [27, 32, 32], replicated, may hold values from -0.21875 to 0.21875
- conv_bias: float32 [32], replicated, may hold values from -3 to 3
- pair_owner: int32 [65536, 1], P(('gx', 'gy', 'gz')), may hold values from 0 to 63; in each aligned block of 128 rows (0 to 127, 128 to 255, ...) at most 5 rows name the same one
- pair_edge: int32 [65536], P(('gx', 'gy', 'gz')), may hold values from 0 to 63
- mlp_in: bfloat16 [256, 512], replicated, may hold values from -0.375 to 0.375
- mlp_in_bias: float32 [512], replicated, may hold values from -3 to 3
- mlp_mid: bfloat16 [512, 512], replicated, may hold values from -0.25 to 0.25
- mlp_mid_bias: float32 [512], replicated, may hold values from -3 to 3
- mlp_out: bfloat16 [512], replicated, may hold values from -0.25 to 0.25
Outputs:
- pair_scores: float32 [65536], P(('gx', 'gy', 'gz'))
Inputs may be any that keep to these rules, and one draw needn't show every extreme that they name: `pair_owner`: within each aligned block of 128 rows (the pairs of one brick) no owner is named by more than 5 rows, a bound that some block reaches.
All inputs are finite; a program needn't handle non-finite values.
Results may differ from a plain program's by a relative error of at most 0.011.
Values may be sent and summed in bfloat16 or wider, within the bound.
No kernel may reach another device: no remote copies, remote signals or barrier semaphores. Data moves between devices by JAX's collectives and lax.ppermute only.
A program may use at most 64 MiB of HBM per device.

v0:
```python
import jax
import jax.numpy as jnp
from jax import lax
from jax.sharding import PartitionSpec as P

BINS = 8
EDGE_DEV = 64


def extended(cells, sides, width):
    for axis, dim in sides:
        count = lax.axis_size(axis)
        ends = count - 1
        head = lax.slice_in_dim(cells, 0, width, axis=dim)
        tail = lax.slice_in_dim(cells, cells.shape[dim] - width, cells.shape[dim], axis=dim)
        cells = jnp.concatenate(
            [
                lax.ppermute(tail, axis, [(i, (i + 1) % count) for i in range(ends)]),
                cells,
                lax.ppermute(head, axis, [((i + 1) % count, i) for i in range(ends)]),
            ],
            axis=dim,
        )
    return cells


def body(
    features,
    voxel_slot,
    conv_weight,
    conv_bias,
    pair_owner,
    pair_edge,
    mlp_in,
    mlp_in_bias,
    mlp_mid,
    mlp_mid_bias,
    mlp_out,
):
    channels, extent_x, extent_y, extent_z = features.shape
    volume = extent_x * extent_y * extent_z
    padded = extended(features, (("gx", 1), ("gy", 2), ("gz", 3)), 1)
    total = jnp.zeros((channels, volume), jnp.float32)
    for offset in range(27):
        shift_x = offset // 9
        shift_y = offset // 3 % 3
        shift_z = offset % 3
        window = padded[
            :,
            shift_x : shift_x + extent_x,
            shift_y : shift_y + extent_y,
            shift_z : shift_z + extent_z,
        ].reshape(channels, volume)
        total = total + jnp.dot(conv_weight[offset], window, preferred_element_type=jnp.float32)
    fields = jnp.maximum(total + conv_bias[:, None], 0.0).astype(jnp.bfloat16)
    pair_count = pair_edge.shape[0]
    slot_count = pair_count * BINS
    slots_flat = voxel_slot.reshape(volume)
    block_width = 512
    pieces = []
    for block in range(slot_count // block_width):
        labels = block * block_width + lax.iota(jnp.int32, block_width)
        onehot = (slots_flat[:, None] == labels[None, :]).astype(jnp.bfloat16)
        pieces.append(jnp.dot(fields, onehot, preferred_element_type=jnp.float32))
    pooled = jnp.concatenate(pieces, axis=1) * (slot_count / volume)
    row_width = BINS * channels
    pair_rows = (
        pooled.reshape(channels, BINS, pair_count)
        .transpose(2, 1, 0)
        .reshape(pair_count, row_width)
        .astype(jnp.bfloat16)
    )
    size_gx = lax.axis_size("gx")
    size_gy = lax.axis_size("gy")
    groups = size_gx * size_gy
    capacity = max(2, (5 * pair_count + 2 * groups - 1) // (2 * groups))
    owners = pair_owner[:, 0]
    owner_marks = (owners[:, None] == lax.iota(jnp.int32, groups)[None, :]).astype(jnp.int32)
    earlier = jnp.cumsum(owner_marks, axis=0) - owner_marks
    slot_rank = jnp.sum(earlier * owner_marks, axis=1)
    target = owners * capacity + slot_rank
    send_rows = jnp.zeros((groups * capacity, row_width), jnp.bfloat16).at[target].set(pair_rows)
    send_ids = jnp.full((groups * capacity,), -1, jnp.int32).at[target].set(pair_edge)
    edge_count = EDGE_DEV
    recv_rows, recv_ids = (
        lax.all_to_all(
            send_rows.reshape(groups, capacity, row_width),
            ("gx", "gy"),
            split_axis=0,
            concat_axis=0,
            tiled=True,
        ),
        lax.all_to_all(
            send_ids.reshape(groups, capacity),
            ("gx", "gy"),
            split_axis=0,
            concat_axis=0,
            tiled=True,
        ),
    )
    flat_rows = recv_rows.reshape(groups * capacity, row_width)
    flat_ids = recv_ids.reshape(groups * capacity)
    edge_onehot = (lax.iota(jnp.int32, edge_count)[:, None] == flat_ids[None, :]).astype(
        jnp.bfloat16
    )
    edge_rows = jnp.dot(edge_onehot, flat_rows, preferred_element_type=jnp.float32).astype(
        jnp.bfloat16
    )
    first = jax.nn.silu(
        jnp.dot(edge_rows, mlp_in, preferred_element_type=jnp.float32) + mlp_in_bias
    ).astype(jnp.bfloat16)
    second = jax.nn.silu(
        jnp.dot(first, mlp_mid, preferred_element_type=jnp.float32) + mlp_mid_bias
    ).astype(jnp.bfloat16)
    edge_scores = jnp.dot(second, mlp_out, preferred_element_type=jnp.float32)
    owner_scores = jnp.take(edge_scores, jnp.clip(flat_ids, 0, edge_count - 1)).reshape(
        groups, capacity
    )
    returned = lax.all_to_all(owner_scores, ("gx", "gy"), split_axis=0, concat_axis=0, tiled=True)
    return returned.reshape(groups * capacity)[target]


def solution(mesh):
    placed = (
        P(None, "gx", "gy", "gz"),
        P("gx", "gy", "gz"),
        P(),
        P(),
        P(("gx", "gy", "gz"), None),
        P(("gx", "gy", "gz")),
        P(),
        P(),
        P(),
        P(),
        P(),
    )
    return jax.shard_map(
        body, mesh=mesh, in_specs=placed, out_specs=P(("gx", "gy", "gz")), check_vma=False
    )
```

profile of v0, /device:TPU:192, one launch (start us, length us, event | category | flops | bytes accessed | tf_op | source)
XLA Modules:
  0.0 166.2 jit_solution(17477800403513236115)
XLA Ops:
  0.0 1.1 fusion.169
  1.1 1.7 %collective-permute-start = (bf16[32,1,16,128]{3,2,1,0:T(8,128)(2,1)S(1)}, bf16[32,1,16,128]{3,2,1,0:T(8,128)(2,1)S(1)}, u32[]{:S(2)}, u32[]{:S(2)}) collective-permute-start(bf16[32,1,16,128]{3,2,1,0:T(8,128)(2,1)S(1)} %get-tuple-element.98), channel_id=1, source_target_pairs={{0,64},{64,128},{128,192},{192,256},{256,320},{320,384},{384,448},... | collective-permute-start | bytes 393224 | tf_op jit(solution)/shard_map/ppermute | solution.py:18
  2.8 1.3 collective-permute-start.1
  4.1 0.7 fusion.103
  5.0 0.8 select_reduce_fusion
  5.9 0.7 fusion.163
  6.5 1.1 scatter_custom_fusion
  7.7 0.7 all_to_all.13
  8.4 13.1 %all-to-all-start = ((s32[64,1,5]{2,1,0:T(1,128)}), s32[64,1,5]{2,1,0:T(1,128)S(1)}, u32[]{:S(2)}, u32[]{:S(2)}) async-start(s32[64,1,5]{2,1,0:T(1,128)} %bitcast.3), calls=%async_computation | async-start | bytes 65536 | tf_op jit(solution)/shard_map/all_to_all | solution.py:93
  21.5 0.6 iota_add_fusion
  22.1 0.8 pad_maximum_fusion.4
  23.1 3.5 %collective-permute-start.2 = (bf16[32,4,1,128]{3,0,2,1:T(8,128)(2,1)S(1)}, bf16[32,4,1,128]{3,0,2,1:T(8,128)(2,1)S(1)}, u32[]{:S(2)}, u32[]{:S(2)}) collective-permute-start(bf16[32,4,1,128]{3,0,2,1:T(8,128)(2,1)S(1)} %copy.285), channel_id=1, source_target_pairs={{0,8},{8,16},{16,24},{24,32},{32,40},{40,48},{48,56},{1,9},{9,17},... | collective-permute-start | bytes 98312 | tf_op jit(solution)/shard_map/ppermute | solution.py:18
  26.6 0.6 copy.284
  27.2 1.3 collective-permute-start.3
  28.5 1.7 %convolution_bitcast_fusion.4 = f32[32,4096]{1,0:T(8,128)} fusion(bf16[4,8,32,128]{3,2,1,0:T(8,128)(2,1)S(1)} %bitcast.343, bf16[27,32,32]{2,1,0:T(8,128)(2,1)} %param.13), kind=kOutput, calls=%fused_computation.40 | convolution fusion | flops 8388608 | bytes 794624 | tf_op jit(solution)/shard_map/dot_general | solution.py:54
  30.2 1.9 %copy.107 = bf16[32,4,16,128]{0,2,3,1:T(8,128)(2,1)S(1)} copy(bf16[32,4,16,128]{3,2,1,0:T(8,128)(2,1)S(1)} %constant_dynamic-update-slice_fusion) | data formatting | bytes 1048576 | tf_op jit(solution)/shard_map/concatenate | solution.py:16
  32.1 0.9 copy.106
  33.2 0.9 copy.108
  34.1 2.9 %pad_maximum_fusion = bf16[32,4,18,128]{0,2,3,1:T(8,128)(2,1)S(1)} fusion(bf16[32,4,1,128]{0,2,3,1:T(2,128)(2,1)} %copy.108, bf16[32,4,16,128]{0,2,3,1:T(8,128)(2,1)S(1)} %copy.107, bf16[32,4,1,128]{0,2,3,1:T(2,128)(2,1)} %copy.106), kind=kLoop, calls=%fused_computation.53 | loop fusion | flops 1769472 | bytes 1179648 | tf_op jit(solution)/shard_map/concatenate | solution.py:16
  36.9 0.7 fusion.165
  37.6 5.5 %collective-permute-start.4 = (bf16[32,4,18,1]{0,2,3,1:T(8,128)(2,1)}, bf16[32,4,18,1]{0,2,3,1:T(8,128)(2,1)S(1)}, u32[]{:S(2)}, u32[]{:S(2)}) collective-permute-start(bf16[32,4,18,1]{0,2,3,1:T(8,128)(2,1)} %get-tuple-element.64), channel_id=1, source_target_pairs={{0,1},{1,2},{2,3},{3,4},{4,5},{5,6},{6,7},{8,9},{9,10},{10,11},{11... | collective-permute-start | bytes 13832 | tf_op jit(solution)/shard_map/ppermute | solution.py:18
  43.1 0.4 constant_dynamic-update-slice_fusion.3
  43.9 0.9 convolution_bitcast_fusion.1
  44.9 0.9 convolution_bitcast_fusion.10
  46.0 1.7 %convolution_bitcast_fusion.7 = f32[32,4096]{1,0:T(8,128)} fusion(bf16[4,8,32,128]{3,2,1,0:T(8,128)(2,1)S(1)} %bitcast.357, bf16[27,32,32]{2,1,0:T(8,128)(2,1)} %param.13), kind=kOutput, calls=%fused_computation.43 | convolution fusion | flops 8388608 | bytes 794624 | tf_op jit(solution)/shard_map/dot_general | solution.py:54
  47.7 3.5 %copy.110 = bf16[32,4,18,128]{3,0,2,1:T(8,128)(2,1)S(1)} copy(bf16[32,4,18,128]{0,2,3,1:T(8,128)(2,1)} %copy-done.1) | data formatting | bytes 1179648 | tf_op jit(solution)/shard_map/concatenate | solution.py:16
  51.3 2.1 %collective-permute-start.5 = (bf16[32,4,18,1]{0,2,3,1:T(8,128)(2,1)}, bf16[32,4,18,1]{0,2,3,1:T(8,128)(2,1)S(1)}, u32[]{:S(2)}, u32[]{:S(2)}) collective-permute-start(bf16[32,4,18,1]{0,2,3,1:T(8,128)(2,1)} %get-tuple-element.65), channel_id=1, source_target_pairs={{1,0},{2,1},{3,2},{4,3},{5,4},{6,5},{7,6},{9,8},{10,9},{11,10},{12... | collective-permute-start | bytes 13832 | tf_op jit(solution)/shard_map/ppermute | solution.py:20
  53.4 0.8 copy.121
  54.2 0.8 copy.124
  55.1 0.5 copy.109
  55.6 2.1 %fusion.40 = (bf16[32,2,16,128]{3,0,2,1:T(8,128)(2,1)}, bf16[32,2,16,128]{3,0,2,1:T(8,128)(2,1)S(1)}, bf16[32,2,16,128]{3,0,2,1:T(8,128)(2,1)}, bf16[32,2,16,128...) fusion(bf16[32,4,18,1]{3,0,2,1:T(8,128)(2,1)S(1)} %copy.109, ...), kind=kLoop, calls=%fused_computation.105 | loop fusion | flops 4718592 | bytes 2953728 | tf_op jit(solution)/shard_map/concatenate | solution.py:16
  57.8 1.7 %fusion.95 = f32[4096,32]{0,1:T(8,128)} fusion(bf16[4,8,32,128]{3,2,1,0:T(8,128)(2,1)S(1)} %bitcast.358, bf16[27,32,32]{2,1,0:T(8,128)(2,1)} %param.13), kind=kOutput, calls=%fused_computation.160 | convolution fusion | flops 8388608 | bytes 794624 | tf_op jit(solution)/shard_map/dot_general | solution.py:54
  59.5 0.5 copy.115
  60.1 1.3 fusion.31
  61.7 0.6 copy-done.15
  62.9 0.5 copy-done.12
  64.1 0.4 copy-done.10
  66.9 0.5 copy-done.5
  68.0 0.5 copy-done.6
  69.2 0.5 copy-done.8
  70.4 0.5 copy-done.7
  71.6 0.6 copy-done.3
  72.3 0.6 fusion.19
  73.0 1.5 fusion.26
  74.6 1.5 fusion.23
  76.2 1.3 scatter_custom_fusion.1
  77.6 0.8 reshape.173
  78.3 12.4 %all-to-all-start.1 = ((bf16[64,5,256]{2,1,0:T(8,128)(2,1)}), bf16[64,5,256]{2,1,0:T(8,128)(2,1)S(1)}, u32[]{:S(2)}, u32[]{:S(2)}) async-start(bf16[64,5,256]{2,1,0:T(8,128)(2,1)} %reshape.173), calls=%async_computation.1 | async-start | bytes 524288 | tf_op jit(solution)/shard_map/all_to_all | solution.py:86
  90.7 0.5 broadcast.555
  91.3 0.7 reduce.122
  92.3 11.7 %all-to-all-done.1 = bf16[64,5,256]{2,1,0:T(8,128)(2,1)S(1)} async-done(((bf16[64,5,256]{2,1,0:T(8,128)(2,1)}), bf16[64,5,256]{2,1,0:T(8,128)(2,1)S(1)}, u32[]{:S(2)}, u32[]{:S(2)}) %all-to-all-start.1) | async-done | bytes 163872 | tf_op jit(solution)/shard_map/all_to_all | solution.py:86
  104.4 0.4 convolution_bitcast_fusion.13
  104.8 0.7 fusion.172
  105.5 0.7 fusion.173
  106.2 0.7 fusion.171
  106.9 0.7 fusion.170
  107.6 4.3 %fusion.160 = (f32[320]{0:T(512)S(1)}, s32[320,1]{0,1:T(1,128)S(1)}) fusion(f32[]{:T(128)} %bitcast.107, f32[]{:T(128)} %bitcast.108, f32[]{:T(128)} %bitcast.109, f32[]{:T(128)} %bitcast.110, f32[]{:T(128)} %bitcast.111, f32[]{:T(128)} %bitcast.113, f32[]{:T(128)} %bitcast.112, s32[320,1]{0,1:T(1,128)S(1)} %min.12), kind=kLoop, calls=%fused_computation.314 | loop fusion | flops 4800 | bytes 3868 | tf_op jit(solution)/shard_map/jit(_take)/gather | solution.py:116
  112.3 35.6 %select_select_fusion = f32[320]{0:T(512)S(1)} fusion(pred[320]{0:T(512)(128)(4,1)S(1)} %get-tuple-element.61, pred[320]{0:T(512)(128)(4,1)S(1)} %get-tuple-element.60, pred[320]{0:T(512)(128)(4,1)S(1)} %get-tuple-element.59, pred[320]{0:T(512)(128)(4,1)S(1)} %get-tuple-element.58, pred[320]{0:T(512)(128)(4,1)S(1)} %get-tuple-element.57, ...), kind=kLoop, calls=%fused_computation.312 | loop fusion | flops 18240 | bytes 21028 | tf_op jit(solution)/shard_map/jit(_take)/gather | solution.py:116
  148.0 0.6 and_select_fusion
  148.6 4.8 %all-to-all-start.2 = ((f32[64,1,5]{2,1,0:T(1,128)}), f32[64,1,5]{2,1,0:T(1,128)S(1)}, u32[]{:S(2)}, u32[]{:S(2)}) async-start(f32[64,1,5]{2,1,0:T(1,128)} %bitcast.114), calls=%async_computation.2 | async-start | bytes 65536 | tf_op jit(solution)/shard_map/all_to_all | solution.py:119
  153.5 9.6 %all-to-all-done.2 = f32[64,1,5]{2,1,0:T(1,128)S(1)} async-done(((f32[64,1,5]{2,1,0:T(1,128)}), f32[64,1,5]{2,1,0:T(1,128)S(1)}, u32[]{:S(2)}, u32[]{:S(2)}) %all-to-all-start.2) | async-done | bytes 1312 | tf_op jit(solution)/shard_map/all_to_all | solution.py:119
  163.1 0.5 broadcast.556
  163.6 0.7 reduce.123
  164.5 1.8 %gather_fusion = f32[128]{0:T(128)} fusion(f32[320]{0:T(512)S(1)} %reshape.175, s32[1024]{0:T(1024)S(1)} %pad_clamp_fusion), kind=kCustom, calls=%fused_computation | custom fusion | bytes 1536 | tf_op jit(solution)/shard_map/gather | solution.py:120
  (118 shorter events, 9.5 us)
Async XLA Ops:
  0.0 104.4 %copy-start = (bf16[512,512]{1,0:T(8,128)(2,1)S(1)}, bf16[512,512]{1,0:T(8,128)(2,1)}, u32[]{:S(2)}) copy-start(bf16[512,512]{1,0:T(8,128)(2,1)} %param.19) | copy-start | bytes 1572868
  0.0 22.1 %copy-start.2 = (bf16[32,2,16,128]{3,2,1,0:T(8,128)(2,1)S(1)}, bf16[32,2,16,128]{3,2,1,0:T(8,128)(2,1)}, u32[]{:S(2)}) copy-start(bf16[32,2,16,128]{3,2,1,0:T(8,128)(2,1)} %param.11) | copy-start | bytes 786436
  1.1 21.0 %collective-permute-start = (bf16[32,1,16,128]{3,2,1,0:T(8,128)(2,1)S(1)}, bf16[32,1,16,128]{3,2,1,0:T(8,128)(2,1)S(1)}, u32[]{:S(2)}, u32[]{:S(2)}) collective-permute-start(bf16[32,1,16,128]{3,2,1,0:T(8,128)(2,1)S(1)} %get-tuple-element.98), channel_id=1, source_target_pairs={{0,64},{64,128},{128,192},{192,256},{256,320},{320,384},{384,448},... | collective-permute-start | bytes 393224 | tf_op jit(solution)/shard_map/ppermute | solution.py:18
  2.8 19.3 %collective-permute-start.1 = (bf16[32,1,16,128]{3,2,1,0:T(8,128)(2,1)S(1)}, bf16[32,1,16,128]{3,2,1,0:T(8,128)(2,1)S(1)}, u32[]{:S(2)}, u32[]{:S(2)}) collective-permute-start(bf16[32,1,16,128]{3,2,1,0:T(8,128)(2,1)S(1)} %get-tuple-element.97), channel_id=1, source_target_pairs={{64,0},{128,64},{192,128},{256,192},{320,256},{384,320},{448,384},... | collective-permute-start | bytes 393224 | tf_op jit(solution)/shard_map/ppermute | solution.py:20
  6.5 15.6 %copy-start.21 = (s32[128]{0:T(128)}, s32[128]{0:T(128)S(1)}, u32[]{:S(2)}) copy-start(s32[128]{0:T(128)S(1)} %fusion.163) | copy-start | bytes 1540
  8.4 69.9 %all-to-all-start = ((s32[64,1,5]{2,1,0:T(1,128)}), s32[64,1,5]{2,1,0:T(1,128)S(1)}, u32[]{:S(2)}, u32[]{:S(2)}) async-start(s32[64,1,5]{2,1,0:T(1,128)} %bitcast.3), calls=%async_computation | async-start | bytes 65536 | tf_op jit(solution)/shard_map/all_to_all | solution.py:93
  23.1 9.0 %collective-permute-start.2 = (bf16[32,4,1,128]{3,0,2,1:T(8,128)(2,1)S(1)}, bf16[32,4,1,128]{3,0,2,1:T(8,128)(2,1)S(1)}, u32[]{:S(2)}, u32[]{:S(2)}) collective-permute-start(bf16[32,4,1,128]{3,0,2,1:T(8,128)(2,1)S(1)} %copy.285), channel_id=1, source_target_pairs={{0,8},{8,16},{16,24},{24,32},{32,40},{40,48},{48,56},{1,9},{9,17},... | collective-permute-start | bytes 98312 | tf_op jit(solution)/shard_map/ppermute | solution.py:18
  27.2 6.0 %collective-permute-start.3 = (bf16[32,4,1,128]{3,0,2,1:T(8,128)(2,1)}, bf16[32,4,1,128]{3,0,2,1:T(8,128)(2,1)S(1)}, u32[]{:S(2)}, u32[]{:S(2)}) collective-permute-start(bf16[32,4,1,128]{3,0,2,1:T(8,128)(2,1)} %copy.284), channel_id=1, source_target_pairs={{8,0},{16,8},{24,16},{32,24},{40,32},{48,40},{56,48},{9,1},{17,9},... | collective-permute-start | bytes 98312 | tf_op jit(solution)/shard_map/ppermute | solution.py:20
  36.9 6.7 %copy-start.1 = (bf16[32,4,18,128]{0,2,3,1:T(8,128)(2,1)}, bf16[32,4,18,128]{0,2,3,1:T(8,128)(2,1)S(1)}, u32[]{:S(2)}) copy-start(bf16[32,4,18,128]{0,2,3,1:T(8,128)(2,1)S(1)} %pad_maximum_fusion) | copy-start | bytes 1769476
  37.6 17.5 %collective-permute-start.4 = (bf16[32,4,18,1]{0,2,3,1:T(8,128)(2,1)}, bf16[32,4,18,1]{0,2,3,1:T(8,128)(2,1)S(1)}, u32[]{:S(2)}, u32[]{:S(2)}) collective-permute-start(bf16[32,4,18,1]{0,2,3,1:T(8,128)(2,1)} %get-tuple-element.64), channel_id=1, source_target_pairs={{0,1},{1,2},{2,3},{3,4},{4,5},{5,6},{6,7},{8,9},{9,10},{10,11},{11... | collective-permute-start | bytes 13832 | tf_op jit(solution)/shard_map/ppermute | solution.py:18
  51.3 8.2 %collective-permute-start.5 = (bf16[32,4,18,1]{0,2,3,1:T(8,128)(2,1)}, bf16[32,4,18,1]{0,2,3,1:T(8,128)(2,1)S(1)}, u32[]{:S(2)}, u32[]{:S(2)}) collective-permute-start(bf16[32,4,18,1]{0,2,3,1:T(8,128)(2,1)} %get-tuple-element.65), channel_id=1, source_target_pairs={{1,0},{2,1},{3,2},{4,3},{5,4},{6,5},{7,6},{9,8},{10,9},{11,10},{12... | collective-permute-start | bytes 13832 | tf_op jit(solution)/shard_map/ppermute | solution.py:20
  60.1 1.4 copy-start.16
  61.4 1.0 copy-start.15
  61.5 1.1 copy-start.14
  61.7 1.1 copy-start.13
  62.4 1.0 copy-start.12
  62.6 1.0 copy-start.17
  62.7 1.1 copy-start.11
  63.5 1.0 copy-start.10
  63.9 1.0 copy-start.9
  66.3 1.0 copy-start.5
  67.6 1.0 copy-start.6
  68.8 1.0 copy-start.8
  69.9 1.0 copy-start.7
  71.1 1.0 copy-start.3
  71.1 1.2 copy-start.4
  71.1 1.2 copy-start.20
  72.3 0.7 copy-start.24
  73.0 1.5 copy-start.18
  74.5 1.7 %copy-start.22 = (s32[128]{0:T(128)S(1)}, s32[128]{0:T(128)}, u32[]{:S(2)}) copy-start(s32[128]{0:T(128)} %copy-done.21) | copy-start | bytes 1540
  76.1 14.7 %copy-start.19 = (bf16[512]{0:T(512)(128)(2,1)S(1)}, bf16[512]{0:T(512)(128)(2,1)}, u32[]{:S(2)}) copy-start(bf16[512]{0:T(512)(128)(2,1)} %param.21) | copy-start | bytes 3076
  76.1 28.0 %copy-start.23 = (bf16[256,512]{1,0:T(8,128)(2,1)S(1)}, bf16[256,512]{1,0:T(8,128)(2,1)}, u32[]{:S(2)}) copy-start(bf16[256,512]{1,0:T(8,128)(2,1)} %param.17) | copy-start | bytes 786436
  76.1 28.0 %copy-start.25 = (f32[512]{0:T(512)S(1)}, f32[512]{0:T(512)}, u32[]{:S(2)}) copy-start(f32[512]{0:T(512)} %param.18) | copy-start | bytes 6148
  77.6 26.9 %copy-start.26 = (f32[512]{0:T(512)S(1)}, f32[512]{0:T(512)}, u32[]{:S(2)}) copy-start(f32[512]{0:T(512)} %param.20) | copy-start | bytes 6148
  78.3 25.6 %all-to-all-start.1 = ((bf16[64,5,256]{2,1,0:T(8,128)(2,1)}), bf16[64,5,256]{2,1,0:T(8,128)(2,1)S(1)}, u32[]{:S(2)}, u32[]{:S(2)}) async-start(bf16[64,5,256]{2,1,0:T(8,128)(2,1)} %reshape.173), calls=%async_computation.1 | async-start | bytes 524288 | tf_op jit(solution)/shard_map/all_to_all | solution.py:86
  148.6 14.5 %all-to-all-start.2 = ((f32[64,1,5]{2,1,0:T(1,128)}), f32[64,1,5]{2,1,0:T(1,128)S(1)}, u32[]{:S(2)}, u32[]{:S(2)}) async-start(f32[64,1,5]{2,1,0:T(1,128)} %bitcast.114), calls=%async_computation.2 | async-start | bytes 65536 | tf_op jit(solution)/shard_map/all_to_all | solution.py:119
where the time goes:
time: 168 us; the launch traced here: 166 us
  other arithmetic  52.4 us (31%)
  starting transfers between devices  45.7 us (27%)
  local copies, waits for them, and re-layouts  30 us (18%)
  waiting for transfers between devices  21.5 us (13%)
  matrix products  15.8 us (9%)
    gather x3, other arithmetic, body(): jnp.take(edge_scores, jnp.clip(flat_ids, 0, edge_count - 1))  40.2 us
    all_to_all x1, starting transfers between devices, body(): lax.all_to_all(send_ids.reshape(groups, capacity), ('gx', 'gy'), split_ax...  13.1 us
    all_to_all x1, starting transfers between devices, body(): lax.all_to_all(send_rows.reshape(groups, capacity, row_width), ('gx', 'gy...  12.4 us
    dot_general x27, matrix products, body(): jnp.dot(conv_weight[offset], window, preferred_element_type=jnp.float32)  12.1 us
    all_to_all x1, waiting for transfers between devices, body(): lax.all_to_all(send_rows.reshape(groups, capacity, row_width), ('gx', 'gy...  11.7 us
    ppermute x3, starting transfers between devices, extended(): lax.ppermute(tail, axis, [(i, (i + 1) % count) for i in range(ends)])  10.7 us
    all_to_all x1, waiting for transfers between devices, body(): lax.all_to_all(owner_scores, ('gx', 'gy'), split_axis=0, concat_axis=0, t...  9.62 us
    concatenate x4, other arithmetic, extended(): jnp.concatenate([lax.ppermute(tail, axis, [(i, (i + 1) % count) for i in...  7.05 us
  transfers between devices with their start and end apart: 9, of which 3 were waited for; matrix products, arithmetic and copies ran while one was open for 27% of the time, Pallas kernels for 0%

commit v1 on v0

--- a/solution.py
+++ b/solution.py
@@ -40,18 +40,15 @@
     channels, extent_x, extent_y, extent_z = features.shape
     volume = extent_x * extent_y * extent_z
     padded = extended(features, (("gx", 1), ("gy", 2), ("gz", 3)), 1)
-    total = jnp.zeros((channels, volume), jnp.float32)
-    for offset in range(27):
-        shift_x = offset // 9
-        shift_y = offset // 3 % 3
-        shift_z = offset % 3
-        window = padded[
-            :,
-            shift_x : shift_x + extent_x,
-            shift_y : shift_y + extent_y,
-            shift_z : shift_z + extent_z,
-        ].reshape(channels, volume)
-        total = total + jnp.dot(conv_weight[offset], window, preferred_element_type=jnp.float32)
+    kernel = conv_weight.reshape(3, 3, 3, channels, channels).transpose(3, 4, 0, 1, 2)
+    total = lax.conv_general_dilated(
+        padded[None],
+        kernel,
+        (1, 1, 1),
+        "VALID",
+        dimension_numbers=("NCDHW", "OIDHW", "NCDHW"),
+        preferred_element_type=jnp.float32,
+    )[0].reshape(channels, volume)
     fields = jnp.maximum(total + conv_bias[:, None], 0.0).astype(jnp.bfloat16)
     pair_count = pair_edge.shape[0]
     slot_count = pair_count * BINS
@@ -80,26 +77,15 @@
     slot_rank = jnp.sum(earlier * owner_marks, axis=1)
     target = owners * capacity + slot_rank
     send_rows = jnp.zeros((groups * capacity, row_width), jnp.bfloat16).at[target].set(pair_rows)
-    send_ids = jnp.full((groups * capacity,), -1, jnp.int32).at[target].set(pair_edge)
+    send_ids = jnp.full((groups * capacity,), -1, jnp.bfloat16).at[target].set(
+        pair_edge.astype(jnp.bfloat16)
+    )
+    id_row = jnp.pad(send_ids.reshape(groups, 1, capacity), ((0, 0), (0, 0), (0, row_width - capacity)))
+    send = jnp.concatenate([send_rows.reshape(groups, capacity, row_width), id_row], axis=1)
     edge_count = EDGE_DEV
-    recv_rows, recv_ids = (
-        lax.all_to_all(
-            send_rows.reshape(groups, capacity, row_width),
-            ("gx", "gy"),
-            split_axis=0,
-            concat_axis=0,
-            tiled=True,
-        ),
-        lax.all_to_all(
-            send_ids.reshape(groups, capacity),
-            ("gx", "gy"),
-            split_axis=0,
-            concat_axis=0,
-            tiled=True,
-        ),
-    )
-    flat_rows = recv_rows.reshape(groups * capacity, row_width)
-    flat_ids = recv_ids.reshape(groups * capacity)
+    recv = lax.all_to_all(send, ("gx", "gy"), split_axis=0, concat_axis=0, tiled=True)
+    flat_rows = recv[:, :capacity, :].reshape(groups * capacity, row_width)
+    flat_ids = recv[:, capacity, :capacity].reshape(groups * capacity).astype(jnp.int32)
     edge_onehot = (lax.iota(jnp.int32, edge_count)[:, None] == flat_ids[None, :]).astype(
         jnp.bfloat16
     )
@@ -113,11 +99,10 @@
         jnp.dot(first, mlp_mid, preferred_element_type=jnp.float32) + mlp_mid_bias
     ).astype(jnp.bfloat16)
     edge_scores = jnp.dot(second, mlp_out, preferred_element_type=jnp.float32)
-    owner_scores = jnp.take(edge_scores, jnp.clip(flat_ids, 0, edge_count - 1)).reshape(
-        groups, capacity
-    )
-    returned = lax.all_to_all(owner_scores, ("gx", "gy"), split_axis=0, concat_axis=0, tiled=True)
-    return returned.reshape(groups * capacity)[target]
+    plane_scores = lax.all_gather(edge_scores.reshape(1, edge_count), ("gx", "gy"), axis=0, tiled=True).reshape(groups * edge_count)
+    wanted = owners * edge_count + pair_edge
+    picks = wanted[:, None] == lax.iota(jnp.int32, groups * edge_count)[None, :]
+    return jnp.sum(jnp.where(picks, plane_scores[None, :], 0.0), axis=1)
 
 
 def solution(mesh):

time: 168 us -> 331 us (1.97)
  blocking collectives: 0 us -> 247 us
  other arithmetic: 52.4 us -> 8.5 us
  starting transfers between devices: 45.7 us -> 28.5 us
  matrix products: 15.8 us -> 6.96 us
  waiting for transfers between devices: 21.5 us -> 13.7 us
  local copies, waits for them, and re-layouts: 30 us -> 23.9 us
    unnamed x0 -> x1, blocking collectives: none -> 247 us
    gather x4 -> x0, other arithmetic: 40.2 us -> none  [the longest x3 40.2 us: body(): jnp.take(edge_scores, jnp.clip(flat_ids, 0, edge_count - 1))]
    all_to_all x3 -> x1, starting transfers between devices: 30.3 us -> 13.3 us  [body(): lax.all_to_all(send, ('gx', 'gy'), split_axis=0, concat_axis=0, tiled=True)]
    dot_general x27 -> x0, matrix products: 12.1 us -> none  [body(): jnp.dot(conv_weight[offset], window, preferred_element_type=jnp.float32)]
    all_to_all x3 -> x1, waiting for transfers between devices: 21.3 us -> 11.3 us  [body(): lax.all_to_all(send, ('gx', 'gy'), split_axis=0, concat_axis=0, tiled=True)]
    concatenate x4 -> x1, other arithmetic: 7.05 us -> 1.79 us  [extended(): jnp.concatenate([lax.ppermute(tail, axis, [(i, (i + 1) % count) for i in...]
    gather x6 -> x0, local copies, waits for them, and re-layouts: 4.76 us -> none  [the longest x5 2.99 us: body(): jnp.take(edge_scores, jnp.clip(flat_ids, 0, edge_count - 1))]
    unnamed x59 -> x29, local copies, waits for them, and re-layouts: 4.99 us -> 9.41 us
  transfers between devices with their start and end apart: 9 -> 7, of which waited for: 3 -> 2; matrix products, arithmetic and copies ran while one was open for 27% -> 4% of each run, Pallas kernels for 0% -> 0%
where the time goes in v1:
time: 331 us; the launch traced here: 330 us
  blocking collectives  247 us (75%)
  starting transfers between devices  28.5 us (9%)
  local copies, waits for them, and re-layouts  23.9 us (7%)
  waiting for transfers between devices  13.7 us (4%)
  other arithmetic  8.5 us (3%)
  matrix products  6.96 us (2%)
    unnamed x1, blocking collectives  247 us
    all_to_all x1, starting transfers between devices, body(): lax.all_to_all(send, ('gx', 'gy'), split_axis=0, concat_axis=0, tiled=True)  13.3 us
    all_to_all x1, waiting for transfers between devices, body(): lax.all_to_all(send, ('gx', 'gy'), split_axis=0, concat_axis=0, tiled=True)  11.3 us
    ppermute x3, starting transfers between devices, extended(): lax.ppermute(tail, axis, [(i, (i + 1) % count) for i in range(ends)])  10.7 us
    unnamed x29, local copies, waits for them, and re-layouts  9.41 us
  transfers between devices with their start and end apart: 7, of which 2 were waited for; matrix products, arithmetic and copies ran while one was open for 4% of the time, Pallas kernels for 0%

profile of v1, /device:TPU:192, one launch (start us, length us, event | category | flops | bytes accessed | tf_op | source)
XLA Modules:
  0.0 330.0 jit_solution(6236502940511893979)
XLA Ops:
  0.0 1.0 fusion.39
  1.1 1.7 collective-permute-start
  2.8 1.3 collective-permute-start.1
  4.1 0.7 fusion.26
  4.8 0.2 reduce_window_sum.11
  5.0 0.8 select_reduce_fusion.1
  5.9 0.7 multiply_add_fusion.1
  6.6 0.7 fusion.30
  7.3 0.0 collective-permute-done
  7.3 1.0 constant_dynamic-update-slice_fusion.1
  8.3 0.0 collective-permute-done.1
  8.3 0.1 fusion.38
  8.4 3.5 %collective-permute-start.2 = (bf16[32,4,1,128]{3,0,2,1:T(8,128)(2,1)S(1)}, bf16[32,4,1,128]{3,0,2,1:T(8,128)(2,1)S(1)}, u32[]{:S(2)}, u32[]{:S(2)}) collective-permute-start(bf16[32,4,1,128]{3,0,2,1:T(8,128)(2,1)S(1)} %copy.58), channel_id=1, source_target_pairs={{0,8},{8,16},{16,24},{24,32},{32,40},{40,48},{48,56},{1,9},{9,17},... | collective-permute-start | bytes 98312 | tf_op jit(solution)/shard_map/ppermute | solution.py:18
  11.9 1.3 collective-permute-start.3
  13.3 1.9 copy.46
  15.2 0.0 collective-permute-done.2
  15.2 0.2 copy.45
  15.4 2.4 collective-permute-done.3
  17.8 0.2 copy.47
  17.9 1.8 pad_maximum_fusion
  19.7 1.6 copy-done.1
  21.4 5.5 %collective-permute-start.4 = (bf16[32,4,18,1]{0,2,3,1:T(8,128)(2,1)S(1)}, bf16[32,4,18,1]{0,2,3,1:T(8,128)(2,1)S(1)}, u32[]{:S(2)}, u32[]{:S(2)}) collective-permute-start(bf16[32,4,18,1]{0,2,3,1:T(8,128)(2,1)S(1)} %get-tuple-element.5), channel_id=1, source_target_pairs={{0,1},{1,2},{2,3},{3,4},{4,5},{5,6},{6,7},{8,9},{9,10},{10,11},{11... | collective-permute-start | bytes 13832 | tf_op jit(solution)/shard_map/ppermute | solution.py:18
  26.9 1.9 collective-permute-start.5
  28.8 1.3 scatter_custom_fusion.1
  30.1 0.1 reshape.125
  30.3 3.7 %copy.49 = bf16[32,4,18,128]{3,0,2,1:T(8,128)(2,1)S(1)} copy(bf16[32,4,18,128]{0,2,3,1:T(8,128)(2,1)} %copy-done.1) | data formatting | bytes 1179648 | tf_op jit(solution)/shard_map/concatenate | solution.py:16
  34.0 0.0 collective-permute-done.4
  34.0 0.5 copy.48
  34.5 0.0 collective-permute-done.5
  34.6 0.5 copy.50
  35.1 1.7 maximum_bitcast_fusion
  36.8 4.8 %copy.60 = bf16[32,4,18,1,130]{0,1,4,2,3:T(4,128)(2,1)S(1)} copy(bf16[32,4,18,1,130]{4,0,2,1,3:T(8,128)(2,1)} %maximum_bitcast_fusion) | data formatting | bytes 1198080
  41.5 1.3 pad.5.clone
  42.8 0.0 copy-start.4
  42.8 0.0 copy-start.8
  42.8 0.0 copy-start.9
  42.9 0.3 copy.53
  43.2 0.1 slice.38
  43.3 0.5 copy-done.4
  43.8 3.2 maximum_convert_fusion
  47.0 0.1 copy.54
  47.1 0.0 copy-start.5
  47.1 0.2 slice_bitcast_fusion
  47.3 1.0 copy.55
  48.4 0.1 reshape.121
  48.5 1.5 fusion
  50.0 0.0 copy-start.3
  50.0 0.0 copy-start.6
  50.1 1.5 fusion.2
  51.6 0.1 copy.56
  51.7 1.3 scatter_custom_fusion
  53.0 0.1 reshape.81
  53.1 0.8 fusion.20
  53.9 13.3 %all-to-all-start = ((bf16[64,6,256]{2,1,0:T(8,128)(2,1)}), bf16[64,6,256]{2,1,0:T(8,128)(2,1)S(1)}, u32[]{:S(2)}, u32[]{:S(2)}) async-start(bf16[64,6,256]{2,1,0:T(8,128)(2,1)} %fusion.20), calls=%async_computation | async-start | bytes 524288 | tf_op jit(solution)/shard_map/all_to_all | solution.py:86
  67.3 1.3 dynamic-slice
  69.2 11.3 %all-to-all-done = bf16[64,6,256]{2,1,0:T(8,128)(2,1)S(1)} async-done(((bf16[64,6,256]{2,1,0:T(8,128)(2,1)}), bf16[64,6,256]{2,1,0:T(8,128)(2,1)S(1)}, u32[]{:S(2)}, u32[]{:S(2)}) %all-to-all-start) | async-done | bytes 196640 | tf_op jit(solution)/shard_map/all_to_all | solution.py:86
  80.5 0.1 reshape.83
  80.5 0.1 fusion.29
  80.7 0.1 reshape.92
  80.8 0.3 multiply_convert_fusion.1
  81.2 0.4 convolution_bitcast_fusion
  81.6 0.2 dynamic-update-slice
  81.8 247.3 %all-reduce.1 = f32[4096]{0:T(1024)S(1)} all-reduce(f32[4096]{0:T(1024)S(1)} %dynamic-update-slice), channel_id=2, replica_groups=mesh['gx'=8,'gy'=8,'gz'=8] {'gx','gy'}, use_global_device_ids=true, to_apply=%add.1 | all-reduce | flops 4096 | bytes 32768
  329.1 0.9 select_reduce_fusion
  (22 shorter events, 0.1 us)
Async XLA Ops:
  0.0 81.2 %copy-start = (bf16[512,512]{1,0:T(8,128)(2,1)S(1)}, bf16[512,512]{1,0:T(8,128)(2,1)}, u32[]{:S(2)}) copy-start(bf16[512,512]{1,0:T(8,128)(2,1)} %param.19) | copy-start | bytes 1572868
  1.1 6.2 %collective-permute-start = (bf16[32,1,16,128]{3,2,1,0:T(8,128)(2,1)S(1)}, bf16[32,1,16,128]{3,2,1,0:T(8,128)(2,1)S(1)}, u32[]{:S(2)}, u32[]{:S(2)}) collective-permute-start(bf16[32,1,16,128]{3,2,1,0:T(8,128)(2,1)S(1)} %get-tuple-element.10), channel_id=1, source_target_pairs={{0,64},{64,128},{128,192},{192,256},{256,320},{320,384},{384,448},... | collective-permute-start | bytes 393224 | tf_op jit(solution)/shard_map/ppermute | solution.py:18
  2.8 5.5 %collective-permute-start.1 = (bf16[32,1,16,128]{3,2,1,0:T(8,128)(2,1)S(1)}, bf16[32,1,16,128]{3,2,1,0:T(8,128)(2,1)S(1)}, u32[]{:S(2)}, u32[]{:S(2)}) collective-permute-start(bf16[32,1,16,128]{3,2,1,0:T(8,128)(2,1)S(1)} %get-tuple-element.9), channel_id=1, source_target_pairs={{64,0},{128,64},{192,128},{256,192},{320,256},{384,320},{448,384},... | collective-permute-start | bytes 393224 | tf_op jit(solution)/shard_map/ppermute | solution.py:20
  8.4 6.8 %collective-permute-start.2 = (bf16[32,4,1,128]{3,0,2,1:T(8,128)(2,1)S(1)}, bf16[32,4,1,128]{3,0,2,1:T(8,128)(2,1)S(1)}, u32[]{:S(2)}, u32[]{:S(2)}) collective-permute-start(bf16[32,4,1,128]{3,0,2,1:T(8,128)(2,1)S(1)} %copy.58), channel_id=1, source_target_pairs={{0,8},{8,16},{16,24},{24,32},{32,40},{40,48},{48,56},{1,9},{9,17},... | collective-permute-start | bytes 98312 | tf_op jit(solution)/shard_map/ppermute | solution.py:18
  11.9 5.8 %collective-permute-start.3 = (bf16[32,4,1,128]{3,0,2,1:T(8,128)(2,1)S(1)}, bf16[32,4,1,128]{3,0,2,1:T(8,128)(2,1)S(1)}, u32[]{:S(2)}, u32[]{:S(2)}) collective-permute-start(bf16[32,4,1,128]{3,0,2,1:T(8,128)(2,1)S(1)} %copy.59), channel_id=1, source_target_pairs={{8,0},{16,8},{24,16},{32,24},{40,32},{48,40},{56,48},{9,1},{17,9},... | collective-permute-start | bytes 98312 | tf_op jit(solution)/shard_map/ppermute | solution.py:20
  19.7 1.6 copy-start.1
  21.4 12.6 %collective-permute-start.4 = (bf16[32,4,18,1]{0,2,3,1:T(8,128)(2,1)S(1)}, bf16[32,4,18,1]{0,2,3,1:T(8,128)(2,1)S(1)}, u32[]{:S(2)}, u32[]{:S(2)}) collective-permute-start(bf16[32,4,18,1]{0,2,3,1:T(8,128)(2,1)S(1)} %get-tuple-element.5), channel_id=1, source_target_pairs={{0,1},{1,2},{2,3},{3,4},{4,5},{5,6},{6,7},{8,9},{9,10},{10,11},{11... | collective-permute-start | bytes 13832 | tf_op jit(solution)/shard_map/ppermute | solution.py:18
  26.9 7.7 %collective-permute-start.5 = (bf16[32,4,18,1]{0,2,3,1:T(8,128)(2,1)S(1)}, bf16[32,4,18,1]{0,2,3,1:T(8,128)(2,1)S(1)}, u32[]{:S(2)}, u32[]{:S(2)}) collective-permute-start(bf16[32,4,18,1]{0,2,3,1:T(8,128)(2,1)S(1)} %get-tuple-element.6), channel_id=1, source_target_pairs={{1,0},{2,1},{3,2},{4,3},{5,4},{6,5},{7,6},{9,8},{10,9},{11,10},{12... | collective-permute-start | bytes 13832 | tf_op jit(solution)/shard_map/ppermute | solution.py:20
  42.8 0.9 copy-start.4
  42.8 0.9 copy-start.8
  42.8 0.9 copy-start.9
  47.1 1.4 copy-start.5
  50.0 17.2 %copy-start.2 = (bf16[512]{0:T(512)(128)(2,1)S(1)}, bf16[512]{0:T(512)(128)(2,1)}, u32[]{:S(2)}) copy-start(bf16[512]{0:T(512)(128)(2,1)} %param.21) | copy-start | bytes 3076
  50.0 30.8 %copy-start.3 = (bf16[256,512]{1,0:T(8,128)(2,1)S(1)}, bf16[256,512]{1,0:T(8,128)(2,1)}, u32[]{:S(2)}) copy-start(bf16[256,512]{1,0:T(8,128)(2,1)} %param.17) | copy-start | bytes 786436
  50.0 30.8 %copy-start.6 = (f32[512]{0:T(512)S(1)}, f32[512]{0:T(512)}, u32[]{:S(2)}) copy-start(f32[512]{0:T(512)} %param.18) | copy-start | bytes 6148
  51.6 29.6 %copy-start.7 = (f32[512]{0:T(512)S(1)}, f32[512]{0:T(512)}, u32[]{:S(2)}) copy-start(f32[512]{0:T(512)} %param.20) | copy-start | bytes 6148
  53.9 26.5 %all-to-all-start = ((bf16[64,6,256]{2,1,0:T(8,128)(2,1)}), bf16[64,6,256]{2,1,0:T(8,128)(2,1)S(1)}, u32[]{:S(2)}, u32[]{:S(2)}) async-start(bf16[64,6,256]{2,1,0:T(8,128)(2,1)} %fusion.20), calls=%async_computation | async-start | bytes 524288 | tf_op jit(solution)/shard_map/all_to_all | solution.py:86

commit v2 on v1

--- a/solution.py
+++ b/solution.py
@@ -99,10 +99,13 @@
         jnp.dot(first, mlp_mid, preferred_element_type=jnp.float32) + mlp_mid_bias
     ).astype(jnp.bfloat16)
     edge_scores = jnp.dot(second, mlp_out, preferred_element_type=jnp.float32)
-    plane_scores = lax.all_gather(edge_scores.reshape(1, edge_count), ("gx", "gy"), axis=0, tiled=True).reshape(groups * edge_count)
-    wanted = owners * edge_count + pair_edge
-    picks = wanted[:, None] == lax.iota(jnp.int32, groups * edge_count)[None, :]
-    return jnp.sum(jnp.where(picks, plane_scores[None, :], 0.0), axis=1)
+    owner_picks = flat_ids[:, None] == lax.iota(jnp.int32, edge_count)[None, :]
+    owner_scores = jnp.sum(jnp.where(owner_picks, edge_scores[None, :], 0.0), axis=1)
+    returned = lax.all_to_all(
+        owner_scores.reshape(groups, capacity), ("gx", "gy"), split_axis=0, concat_axis=0, tiled=True
+    ).reshape(groups * capacity)
+    back_picks = target[:, None] == lax.iota(jnp.int32, groups * capacity)[None, :]
+    return jnp.sum(jnp.where(back_picks, returned[None, :], 0.0), axis=1)
 
 
 def solution(mesh):

time: 331 us -> 98 us (0.30)
  blocking collectives: 247 us -> 14.2 us
    unnamed x1 -> x0, blocking collectives: 247 us -> none
    all_to_all x0 -> x1, blocking collectives: none -> 14.2 us  [body(): lax.all_to_all(owner_scores.reshape(groups, capacity), ('gx', 'gy'), spli...]
    unnamed x29 -> x28, local copies, waits for them, and re-layouts: 9.41 us -> 7.96 us
  transfers between devices with their start and end apart: 7 -> 7, of which waited for: 2 -> 2; matrix products, arithmetic and copies ran while one was open for 4% -> 12% of each run, Pallas kernels for 0% -> 0%
where the time goes in v2:
time: 98 us; the launch traced here: 97.4 us
  starting transfers between devices  28.5 us (29%)
  local copies, waits for them, and re-layouts  23.3 us (24%)
  waiting for transfers between devices  15.6 us (16%)
  blocking collectives  14.2 us (14%)
  other arithmetic  8.3 us (8%)
  matrix products  6.95 us (7%)
    all_to_all x1, blocking collectives, body(): lax.all_to_all(owner_scores.reshape(groups, capacity), ('gx', 'gy'), spli...  14.2 us
    all_to_all x1, starting transfers between devices, body(): lax.all_to_all(send, ('gx', 'gy'), split_axis=0, concat_axis=0, tiled=True)  13.3 us
    all_to_all x1, waiting for transfers between devices, body(): lax.all_to_all(send, ('gx', 'gy'), split_axis=0, concat_axis=0, tiled=True)  13.2 us
    ppermute x3, starting transfers between devices, extended(): lax.ppermute(tail, axis, [(i, (i + 1) % count) for i in range(ends)])  10.7 us
    unnamed x28, local copies, waits for them, and re-layouts  7.96 us
    concatenate x3, local copies, waits for them, and re-layouts, extended(): jnp.concatenate([lax.ppermute(tail, axis, [(i, (i + 1) % count) for i in...  5.62 us
    ppermute x3, starting transfers between devices, extended(): lax.ppermute(head, axis, [((i + 1) % count, i) for i in range(ends)])  4.5 us
    conv_general_dilated x1, matrix products, body(): lax.conv_general_dilated(padded[None], kernel, (1, 1, 1), 'VALID', dimens...  3.18 us
  transfers between devices with their start and end apart: 7, of which 2 were waited for; matrix products, arithmetic and copies ran while one was open for 12% of the time, Pallas kernels for 0%

profile of v2, /device:TPU:192, one launch (start us, length us, event | category | flops | bytes accessed | tf_op | source)
XLA Modules:
  0.0 97.4 jit_solution(6656069576357746398)
XLA Ops:
  0.0 1.0 %fusion.40 = (bf16[32,1,16,128]{3,2,1,0:T(8,128)(2,1)S(1)}, bf16[32,1,16,128]{3,2,1,0:T(8,128)(2,1)S(1)}) fusion(bf16[32,2,16,128]{3,2,1,0:T(8,128)(2,1)} %param.11), kind=kLoop, calls=%fused_computation.66 | loop fusion | bytes 524288 | tf_op jit(solution)/shard_map/slice | solution.py:14
  1.1 1.7 %collective-permute-start = (bf16[32,1,16,128]{3,2,1,0:T(8,128)(2,1)S(1)}, bf16[32,1,16,128]{3,2,1,0:T(8,128)(2,1)S(1)}, u32[]{:S(2)}, u32[]{:S(2)}) collective-permute-start(bf16[32,1,16,128]{3,2,1,0:T(8,128)(2,1)S(1)} %get-tuple-element.10), channel_id=1, source_target_pairs={{0,64},{64,128},{128,192},{192,256},{256,320},{320,384},{384,448},... | collective-permute-start | bytes 393224 | tf_op jit(solution)/shard_map/ppermute | solution.py:18
  2.8 1.3 %collective-permute-start.1 = (bf16[32,1,16,128]{3,2,1,0:T(8,128)(2,1)S(1)}, bf16[32,1,16,128]{3,2,1,0:T(8,128)(2,1)S(1)}, u32[]{:S(2)}, u32[]{:S(2)}) collective-permute-start(bf16[32,1,16,128]{3,2,1,0:T(8,128)(2,1)S(1)} %get-tuple-element.9), channel_id=1, source_target_pairs={{64,0},{128,64},{192,128},{256,192},{320,256},{384,320},{448,384},... | collective-permute-start | bytes 393224 | tf_op jit(solution)/shard_map/ppermute | solution.py:20
  4.1 0.7 fusion.26
  4.8 0.2 reduce_window_sum.11
  5.0 0.8 select_reduce_fusion.2
  5.9 0.7 fusion.37
  6.5 1.0 %constant_dynamic-update-slice_fusion.1 = bf16[32,4,16,128]{3,2,1,0:T(8,128)(2,1)S(1)} fusion(bf16[32,4,16,128]{3,2,1,0:T(8,128)(2,1)S(1)} %constant_dynamic-update-slice_fusion.2, bf16[32,2,16,128]{3,2,1,0:T(8,128)(2,1)} %param.11), kind=kLoop, calls=%fused_computation.50 | loop fusion | bytes 524288
  7.5 0.0 collective-permute-done.1
  7.6 0.1 fusion.39
  7.7 3.5 %collective-permute-start.2 = (bf16[32,4,1,128]{3,0,2,1:T(8,128)(2,1)S(1)}, bf16[32,4,1,128]{3,0,2,1:T(8,128)(2,1)S(1)}, u32[]{:S(2)}, u32[]{:S(2)}) collective-permute-start(bf16[32,4,1,128]{3,0,2,1:T(8,128)(2,1)S(1)} %copy.61), channel_id=1, source_target_pairs={{0,8},{8,16},{16,24},{24,32},{32,40},{40,48},{48,56},{1,9},{9,17},... | collective-permute-start | bytes 98312 | tf_op jit(solution)/shard_map/ppermute | solution.py:18
  11.2 1.3 %collective-permute-start.3 = (bf16[32,4,1,128]{3,0,2,1:T(8,128)(2,1)S(1)}, bf16[32,4,1,128]{3,0,2,1:T(8,128)(2,1)S(1)}, u32[]{:S(2)}, u32[]{:S(2)}) collective-permute-start(bf16[32,4,1,128]{3,0,2,1:T(8,128)(2,1)S(1)} %copy.62), channel_id=1, source_target_pairs={{8,0},{16,8},{24,16},{32,24},{40,32},{48,40},{56,48},{9,1},{17,9},... | collective-permute-start | bytes 98312 | tf_op jit(solution)/shard_map/ppermute | solution.py:20
  12.5 1.9 %copy.48 = bf16[32,4,16,128]{0,2,3,1:T(8,128)(2,1)S(1)} copy(bf16[32,4,16,128]{3,2,1,0:T(8,128)(2,1)S(1)} %constant_dynamic-update-slice_fusion) | data formatting | bytes 1048576 | tf_op jit(solution)/shard_map/concatenate | solution.py:16
  14.5 0.2 copy.47
  14.6 2.4 %collective-permute-done.3 = bf16[32,4,1,128]{3,0,2,1:T(8,128)(2,1)S(1)} collective-permute-done((bf16[32,4,1,128]{3,0,2,1:T(8,128)(2,1)S(1)}, bf16[32,4,1,128]{3,0,2,1:T(8,128)(2,1)S(1)}, u32[]{:S(2)}, u32[]{:S(2)}) %collective-permute-start.3) | collective-permute-done | bytes 32800 | tf_op jit(solution)/shard_map/ppermute | solution.py:20
  17.0 0.2 copy.49
  17.2 0.0 copy-start.8
  17.2 1.8 %pad_maximum_fusion = bf16[32,4,18,128]{0,2,3,1:T(8,128)(2,1)S(1)} fusion(bf16[32,4,1,128]{0,2,3,1:T(2,128)(2,1)S(1)} %copy.49, bf16[32,4,16,128]{0,2,3,1:T(8,128)(2,1)S(1)} %copy.48, bf16[32,4,1,128]{0,2,3,1:T(2,128)(2,1)S(1)} %copy.47), kind=kLoop, calls=%fused_computation.12 | loop fusion | flops 1769472 | bytes 1179648 | tf_op jit(solution)/shard_map/concatenate | solution.py:16
  19.0 1.6 %copy-done.1 = bf16[32,4,18,128]{0,2,3,1:T(8,128)(2,1)} copy-done((bf16[32,4,18,128]{0,2,3,1:T(8,128)(2,1)}, bf16[32,4,18,128]{0,2,3,1:T(8,128)(2,1)S(1)}, u32[]{:S(2)}) %copy-start.1) | copy-done | bytes 589848
  20.7 5.5 %collective-permute-start.4 = (bf16[32,4,18,1]{0,2,3,1:T(8,128)(2,1)S(1)}, bf16[32,4,18,1]{0,2,3,1:T(8,128)(2,1)S(1)}, u32[]{:S(2)}, u32[]{:S(2)}) collective-permute-start(bf16[32,4,18,1]{0,2,3,1:T(8,128)(2,1)S(1)} %get-tuple-element.5), channel_id=1, source_target_pairs={{0,1},{1,2},{2,3},{3,4},{4,5},{5,6},{6,7},{8,9},{9,10},{10,11},{11... | collective-permute-start | bytes 13832 | tf_op jit(solution)/shard_map/ppermute | solution.py:18
  26.1 1.9 %collective-permute-start.5 = (bf16[32,4,18,1]{0,2,3,1:T(8,128)(2,1)S(1)}, bf16[32,4,18,1]{0,2,3,1:T(8,128)(2,1)S(1)}, u32[]{:S(2)}, u32[]{:S(2)}) collective-permute-start(bf16[32,4,18,1]{0,2,3,1:T(8,128)(2,1)S(1)} %get-tuple-element.6), channel_id=1, source_target_pairs={{1,0},{2,1},{3,2},{4,3},{5,4},{6,5},{7,6},{9,8},{10,9},{11,10},{12... | collective-permute-start | bytes 13832 | tf_op jit(solution)/shard_map/ppermute | solution.py:20
  28.1 1.3 %scatter_custom_fusion.1 = bf16[320]{0:T(512)(128)(2,1)S(1)} fusion(s32[128]{0:T(128)S(1)} %get-tuple-element.12, bf16[128]{0:T(256)(128)(2,1)S(1)} %convert_element_type.56, bf16[]{:T(256)} %constant.28.clone.1), kind=kCustom, calls=%fused_computation.57 | custom fusion | bytes 642 | tf_op jit(solution)/shard_map/scatter | solution.py:80
  29.5 0.1 reshape.125
  29.6 3.7 %copy.51 = bf16[32,4,18,128]{3,0,2,1:T(8,128)(2,1)S(1)} copy(bf16[32,4,18,128]{0,2,3,1:T(8,128)(2,1)} %copy-done.1) | data formatting | bytes 1179648 | tf_op jit(solution)/shard_map/concatenate | solution.py:16
  33.3 0.5 copy.50
  33.9 0.5 copy.52
  34.4 1.7 %maximum_bitcast_fusion = bf16[32,4,18,1,130]{4,0,2,1,3:T(8,128)(2,1)} fusion(bf16[32,4,18,1]{3,0,2,1:T(8,128)(2,1)S(1)} %copy.52, bf16[32,4,18,128]{3,0,2,1:T(8,128)(2,1)S(1)} %copy.51, bf16[32,4,18,1]{3,0,2,1:T(8,128)(2,1)S(1)} %copy.50), kind=kLoop, calls=%fused_computation.21 | loop fusion | flops 1797120 | bytes 1198080 | tf_op jit(solution)/shard_map/broadcast_in_dim | solution.py:45
  36.1 4.8 %copy.63 = bf16[32,4,18,1,130]{0,1,4,2,3:T(4,128)(2,1)S(1)} copy(bf16[32,4,18,1,130]{4,0,2,1,3:T(8,128)(2,1)} %maximum_bitcast_fusion) | data formatting | bytes 1198080
  40.8 1.3 %pad.5.clone = bf16[32,4,18,1,136]{0,1,4,2,3:T(4,128)(2,1)S(1)} pad(bf16[32,4,18,1,130]{0,1,4,2,3:T(4,128)(2,1)S(1)} %copy.63, bf16[]{:T(256)} %constant.12.clone.1), padding=0_0x0_0x0_0x0_0x0_6 | pad | bytes 1225730 | tf_op jit(solution)/shard_map/broadcast_in_dim | solution.py:45
  42.1 0.0 copy-start.4
  42.1 0.0 copy-start.9
  42.1 0.0 copy-start.10
  42.2 0.3 copy.55
  42.5 0.1 slice.38
  42.6 0.5 copy-done.4
  43.1 3.2 %maximum_convert_fusion = bf16[2,16,8,17,32]{4,2,3,1,0:T(8,128)(2,1)S(1)} fusion(bf16[3,3,3,32,32]{4,3,2,1,0:T(8,128)(2,1)S(1)} %bitcast.48, bf16[32,4,18,1,7,2]{0,4,5,2,1,3:T(8,128)(2,1)S(1)} %slice.38, bf16[32,4,18,1,8,17]{0,4,5,2,1,3:T(8,128)(2,1)S(1)} %copy.55, f32[32]{0:T(128)S(1)} %copy-done.9, pred[8,17]{0,1:T(8,128)(4,1)S(1)} %copy-done.10), kind=kOutput, calls=%fused_computation.19 | convolution fusion | flops 243306496 | bytes 1025288 | tf_op jit(solution)/shard_map/conv_general_dilated | solution.py:44
  46.3 0.1 copy.56
  46.4 0.0 copy-start.5
  46.4 0.2 slice_bitcast_fusion
  46.6 1.0 %copy.57 = bf16[1,32,2,16,128]{4,3,2,1,0:T(8,128)(2,1)S(1)} copy(bf16[1,32,2,16,128]{1,3,4,2,0:T(8,128)(2,1)S(1)} %slice_bitcast_fusion) | data formatting | bytes 524288 | tf_op jit(solution)/shard_map/convert_element_type | solution.py:52
  47.7 0.1 reshape.121
  47.8 1.5 %fusion = f32[32,4,128]{2,0,1:T(8,128)S(1)} fusion(bf16[32,4096,1]{1,0,2:T(8,128)(2,1)S(1)} %reshape.121, s32[4,128]{1,0:T(4,128)S(1)} %broadcast_add_fusion, s32[4096]{0:T(1024)S(1)} %bitcast.49), kind=kOutput, calls=%fused_computation.2 | convolution fusion | flops 136314880 | bytes 346112 | tf_op jit(solution)/shard_map/dot_general | solution.py:61
  49.3 0.0 copy-start.3
  49.3 0.0 copy-start.6
  49.4 0.0 copy-start.7
  49.4 1.5 %fusion.2 = f32[32,4,128]{2,0,1:T(8,128)S(1)} fusion(bf16[32,4096,1]{1,0,2:T(8,128)(2,1)S(1)} %reshape.121, s32[4,128]{1,0:T(4,128)S(1)} %multiply_add_fusion, s32[4096]{0:T(1024)S(1)} %bitcast.50), kind=kOutput, calls=%fused_computation.4 | convolution fusion | flops 136314880 | bytes 346112 | tf_op jit(solution)/shard_map/dot_general | solution.py:61
  50.9 0.1 copy.58
  51.0 1.3 %scatter_custom_fusion = bf16[320,256]{1,0:T(8,128)(2,1)S(1)} fusion(s32[128]{0:T(128)S(1)} %get-tuple-element.12, bf16[128,256]{1,0:T(8,128)(2,1)S(1)} %copy.58, bf16[]{:T(256)} %constant.12.clone.1), kind=kCustom, calls=%fused_computation.39 | custom fusion | bytes 163842 | tf_op jit(solution)/shard_map/scatter | solution.py:79
  52.4 0.1 reshape.89
  52.4 0.8 fusion.20
  53.2 13.3 %all-to-all-start = ((bf16[64,6,256]{2,1,0:T(8,128)(2,1)}), bf16[64,6,256]{2,1,0:T(8,128)(2,1)S(1)}, u32[]{:S(2)}, u32[]{:S(2)}) async-start(bf16[64,6,256]{2,1,0:T(8,128)(2,1)} %fusion.20), calls=%async_computation | async-start | bytes 524288 | tf_op jit(solution)/shard_map/all_to_all | solution.py:86
  66.6 13.2 %all-to-all-done = bf16[64,6,256]{2,1,0:T(8,128)(2,1)S(1)} async-done(((bf16[64,6,256]{2,1,0:T(8,128)(2,1)}), bf16[64,6,256]{2,1,0:T(8,128)(2,1)S(1)}, u32[]{:S(2)}, u32[]{:S(2)}) %all-to-all-start) | async-done | bytes 196640 | tf_op jit(solution)/shard_map/all_to_all | solution.py:86
  79.8 0.1 reshape.91
  79.8 0.1 fusion.29
  80.0 0.1 reshape.99
  80.1 0.3 multiply_convert_fusion.1
  80.5 0.4 convolution_bitcast_fusion
  80.9 0.1 select_reduce_fusion.1
  81.0 0.1 all_to_all.10
  81.1 14.2 %all_to_all.14 = f32[64,1,5]{2,1,0:T(1,128)S(1)} all-to-all(f32[64,1,5]{2,1,0:T(1,128)S(1)} %bitcast.45), channel_id=1, replica_groups=mesh['gx'=8,'gy'=8,'gz'=8] {'gx','gy'}, dimensions={0} | all-to-all | bytes 2560 | tf_op jit(solution)/shard_map/all_to_all | solution.py:104
  95.4 0.5 broadcast.113
  95.9 0.7 reduce.7
  96.6 0.1 broadcast_in_dim.55
  96.7 0.6 select_reduce_fusion
  (26 shorter events, 0.1 us)
Async XLA Ops:
  0.0 80.5 %copy-start = (bf16[512,512]{1,0:T(8,128)(2,1)S(1)}, bf16[512,512]{1,0:T(8,128)(2,1)}, u32[]{:S(2)}) copy-start(bf16[512,512]{1,0:T(8,128)(2,1)} %param.19) | copy-start | bytes 1572868
  1.1 5.5 %collective-permute-start = (bf16[32,1,16,128]{3,2,1,0:T(8,128)(2,1)S(1)}, bf16[32,1,16,128]{3,2,1,0:T(8,128)(2,1)S(1)}, u32[]{:S(2)}, u32[]{:S(2)}) collective-permute-start(bf16[32,1,16,128]{3,2,1,0:T(8,128)(2,1)S(1)} %get-tuple-element.10), channel_id=1, source_target_pairs={{0,64},{64,128},{128,192},{192,256},{256,320},{320,384},{384,448},... | collective-permute-start | bytes 393224 | tf_op jit(solution)/shard_map/ppermute | solution.py:18
  2.8 4.7 %collective-permute-start.1 = (bf16[32,1,16,128]{3,2,1,0:T(8,128)(2,1)S(1)}, bf16[32,1,16,128]{3,2,1,0:T(8,128)(2,1)S(1)}, u32[]{:S(2)}, u32[]{:S(2)}) collective-permute-start(bf16[32,1,16,128]{3,2,1,0:T(8,128)(2,1)S(1)} %get-tuple-element.9), channel_id=1, source_target_pairs={{64,0},{128,64},{192,128},{256,192},{320,256},{384,320},{448,384},... | collective-permute-start | bytes 393224 | tf_op jit(solution)/shard_map/ppermute | solution.py:20
  7.7 6.8 %collective-permute-start.2 = (bf16[32,4,1,128]{3,0,2,1:T(8,128)(2,1)S(1)}, bf16[32,4,1,128]{3,0,2,1:T(8,128)(2,1)S(1)}, u32[]{:S(2)}, u32[]{:S(2)}) collective-permute-start(bf16[32,4,1,128]{3,0,2,1:T(8,128)(2,1)S(1)} %copy.61), channel_id=1, source_target_pairs={{0,8},{8,16},{16,24},{24,32},{32,40},{40,48},{48,56},{1,9},{9,17},... | collective-permute-start | bytes 98312 | tf_op jit(solution)/shard_map/ppermute | solution.py:18
  11.2 5.8 %collective-permute-start.3 = (bf16[32,4,1,128]{3,0,2,1:T(8,128)(2,1)S(1)}, bf16[32,4,1,128]{3,0,2,1:T(8,128)(2,1)S(1)}, u32[]{:S(2)}, u32[]{:S(2)}) collective-permute-start(bf16[32,4,1,128]{3,0,2,1:T(8,128)(2,1)S(1)} %copy.62), channel_id=1, source_target_pairs={{8,0},{16,8},{24,16},{32,24},{40,32},{48,40},{56,48},{9,1},{17,9},... | collective-permute-start | bytes 98312 | tf_op jit(solution)/shard_map/ppermute | solution.py:20
  17.2 10.9 %copy-start.8 = (s32[128]{0:T(128)S(1)}, s32[128]{0:T(128)}, u32[]{:S(2)}) copy-start(s32[128]{0:T(128)} %param.16) | copy-start | bytes 1540
  19.0 1.7 %copy-start.1 = (bf16[32,4,18,128]{0,2,3,1:T(8,128)(2,1)}, bf16[32,4,18,128]{0,2,3,1:T(8,128)(2,1)S(1)}, u32[]{:S(2)}) copy-start(bf16[32,4,18,128]{0,2,3,1:T(8,128)(2,1)S(1)} %pad_maximum_fusion) | copy-start | bytes 1769476
  20.7 12.6 %collective-permute-start.4 = (bf16[32,4,18,1]{0,2,3,1:T(8,128)(2,1)S(1)}, bf16[32,4,18,1]{0,2,3,1:T(8,128)(2,1)S(1)}, u32[]{:S(2)}, u32[]{:S(2)}) collective-permute-start(bf16[32,4,18,1]{0,2,3,1:T(8,128)(2,1)S(1)} %get-tuple-element.5), channel_id=1, source_target_pairs={{0,1},{1,2},{2,3},{3,4},{4,5},{5,6},{6,7},{8,9},{9,10},{10,11},{11... | collective-permute-start | bytes 13832 | tf_op jit(solution)/shard_map/ppermute | solution.py:18
  26.1 7.7 %collective-permute-start.5 = (bf16[32,4,18,1]{0,2,3,1:T(8,128)(2,1)S(1)}, bf16[32,4,18,1]{0,2,3,1:T(8,128)(2,1)S(1)}, u32[]{:S(2)}, u32[]{:S(2)}) collective-permute-start(bf16[32,4,18,1]{0,2,3,1:T(8,128)(2,1)S(1)} %get-tuple-element.6), channel_id=1, source_target_pairs={{1,0},{2,1},{3,2},{4,3},{5,4},{6,5},{7,6},{9,8},{10,9},{11,10},{12... | collective-permute-start | bytes 13832 | tf_op jit(solution)/shard_map/ppermute | solution.py:20
  42.1 0.9 copy-start.4
  42.1 0.9 copy-start.9
  42.1 0.9 copy-start.10
  46.4 1.4 %copy-start.5 = (s32[2,16,128]{2,1,0:T(8,128)S(1)}, s32[2,16,128]{2,1,0:T(8,128)}, u32[]{:S(2)}) copy-start(s32[2,16,128]{2,1,0:T(8,128)} %param.12) | copy-start | bytes 49156
  49.3 17.2 %copy-start.2 = (bf16[512]{0:T(512)(128)(2,1)S(1)}, bf16[512]{0:T(512)(128)(2,1)}, u32[]{:S(2)}) copy-start(bf16[512]{0:T(512)(128)(2,1)} %param.21) | copy-start | bytes 3076
  49.3 30.8 %copy-start.3 = (bf16[256,512]{1,0:T(8,128)(2,1)S(1)}, bf16[256,512]{1,0:T(8,128)(2,1)}, u32[]{:S(2)}) copy-start(bf16[256,512]{1,0:T(8,128)(2,1)} %param.17) | copy-start | bytes 786436
  49.3 30.8 %copy-start.6 = (f32[512]{0:T(512)S(1)}, f32[512]{0:T(512)}, u32[]{:S(2)}) copy-start(f32[512]{0:T(512)} %param.18) | copy-start | bytes 6148
  49.4 31.2 %copy-start.7 = (f32[512]{0:T(512)S(1)}, f32[512]{0:T(512)}, u32[]{:S(2)}) copy-start(f32[512]{0:T(512)} %param.20) | copy-start | bytes 6148
  53.2 26.5 %all-to-all-start = ((bf16[64,6,256]{2,1,0:T(8,128)(2,1)}), bf16[64,6,256]{2,1,0:T(8,128)(2,1)S(1)}, u32[]{:S(2)}, u32[]{:S(2)}) async-start(bf16[64,6,256]{2,1,0:T(8,128)(2,1)} %fusion.20), calls=%async_computation | async-start | bytes 524288 | tf_op jit(solution)/shard_map/all_to_all | solution.py:86

commit v3 on v1

--- a/solution.py
+++ b/solution.py
@@ -67,29 +67,16 @@
         .reshape(pair_count, row_width)
         .astype(jnp.bfloat16)
     )
-    size_gx = lax.axis_size("gx")
-    size_gy = lax.axis_size("gy")
-    groups = size_gx * size_gy
-    capacity = max(2, (5 * pair_count + 2 * groups - 1) // (2 * groups))
     owners = pair_owner[:, 0]
-    owner_marks = (owners[:, None] == lax.iota(jnp.int32, groups)[None, :]).astype(jnp.int32)
-    earlier = jnp.cumsum(owner_marks, axis=0) - owner_marks
-    slot_rank = jnp.sum(earlier * owner_marks, axis=1)
-    target = owners * capacity + slot_rank
-    send_rows = jnp.zeros((groups * capacity, row_width), jnp.bfloat16).at[target].set(pair_rows)
-    send_ids = jnp.full((groups * capacity,), -1, jnp.bfloat16).at[target].set(
-        pair_edge.astype(jnp.bfloat16)
-    )
-    id_row = jnp.pad(send_ids.reshape(groups, 1, capacity), ((0, 0), (0, 0), (0, row_width - capacity)))
-    send = jnp.concatenate([send_rows.reshape(groups, capacity, row_width), id_row], axis=1)
-    edge_count = EDGE_DEV
-    recv = lax.all_to_all(send, ("gx", "gy"), split_axis=0, concat_axis=0, tiled=True)
-    flat_rows = recv[:, :capacity, :].reshape(groups * capacity, row_width)
-    flat_ids = recv[:, capacity, :capacity].reshape(groups * capacity).astype(jnp.int32)
-    edge_onehot = (lax.iota(jnp.int32, edge_count)[:, None] == flat_ids[None, :]).astype(
-        jnp.bfloat16
-    )
-    edge_rows = jnp.dot(edge_onehot, flat_rows, preferred_element_type=jnp.float32).astype(
+    labels = jnp.concatenate([owners, pair_edge]).astype(jnp.bfloat16).reshape(1, row_width)
+    send = jnp.concatenate([pair_rows, labels], axis=0)
+    gathered = lax.all_gather(send, ("gx", "gy"), axis=0, tiled=False)
+    all_rows = gathered[:, :pair_count, :].reshape(-1, row_width)
+    all_labels = gathered[:, pair_count, :].astype(jnp.int32)
+    all_keys = (all_labels[:, :pair_count] * EDGE_DEV + all_labels[:, pair_count:]).reshape(-1)
+    keys = owners * EDGE_DEV + pair_edge
+    edge_onehot = (keys[:, None] == all_keys[None, :]).astype(jnp.bfloat16)
+    edge_rows = jnp.dot(edge_onehot, all_rows, preferred_element_type=jnp.float32).astype(
         jnp.bfloat16
     )
     first = jax.nn.silu(
@@ -98,11 +85,7 @@
     second = jax.nn.silu(
         jnp.dot(first, mlp_mid, preferred_element_type=jnp.float32) + mlp_mid_bias
     ).astype(jnp.bfloat16)
-    edge_scores = jnp.dot(second, mlp_out, preferred_element_type=jnp.float32)
-    plane_scores = lax.all_gather(edge_scores.reshape(1, edge_count), ("gx", "gy"), axis=0, tiled=True).reshape(groups * edge_count)
-    wanted = owners * edge_count + pair_edge
-    picks = wanted[:, None] == lax.iota(jnp.int32, groups * edge_count)[None, :]
-    return jnp.sum(jnp.where(picks, plane_scores[None, :], 0.0), axis=1)
+    return jnp.dot(second, mlp_out, preferred_element_type=jnp.float32)
 
 
 def solution(mesh):

time: 331 us -> 166 us (0.50)
  the two profiles are of different devices: /device:TPU:192 before, /device:TPU:1 now
where the time goes in v3:
time: 166 us; the launch traced here: 165 us
  waiting for transfers between devices  92.5 us (56%)
  local copies, waits for them, and re-layouts  25.1 us (15%)
  starting transfers between devices  18.1 us (11%)
  between operations  13.8 us (8%)
  matrix products  10.3 us (6%)
  other arithmetic  5.58 us (3%)
    all_gather x1, waiting for transfers between devices, body(): gathered = lax.all_gather(send, ('gx', 'gy'), axis=0, tiled=False)  91.2 us
    ppermute x3, starting transfers between devices, extended(): lax.ppermute(tail, axis, [(i, (i + 1) % count) for i in range(ends)])  9.99 us
    ppermute x3, starting transfers between devices, extended(): lax.ppermute(head, axis, [((i + 1) % count, i) for i in range(ends)])  8.13 us
    unnamed x26, local copies, waits for them, and re-layouts  8.13 us
    concatenate x3, local copies, waits for them, and re-layouts, extended(): jnp.concatenate([lax.ppermute(tail, axis, [(i, (i + 1) % count) for i in...  5.44 us
    slice x1, local copies, waits for them, and re-layouts, body(): all_rows = gathered[:, :pair_count, :].reshape(-1, row_width)  4.76 us
  transfers between devices with their start and end apart: 7, of which 2 were waited for; matrix products, arithmetic and copies ran while one was open for 5% of the time, Pallas kernels for 0%

profile of v3, /device:TPU:1, one launch (start us, length us, event | category | flops | bytes accessed | tf_op | source)
XLA Modules:
  0.0 165.4 jit_solution(14005155769820954690)
XLA Ops:
  6.5 0.0 copy-start
  6.5 0.0 all-gather.4.cloned.1.call-start
  6.5 1.0 fusion.41
  7.6 4.5 %collective-permute-start = (bf16[32,1,16,128]{3,2,1,0:T(8,128)(2,1)S(1)}, bf16[32,1,16,128]{3,2,1,0:T(8,128)(2,1)S(1)}, u32[]{:S(2)}, u32[]{:S(2)}) collective-permute-start(bf16[32,1,16,128]{3,2,1,0:T(8,128)(2,1)S(1)} %get-tuple-element.10), channel_id=1, source_target_pairs={{0,64},{64,128},{128,192},{192,256},{256,320},{320,384},{384,448},... | collective-permute-start | bytes 393224 | tf_op jit(solution)/shard_map/ppermute | solution.py:18
  12.1 5.5 %collective-permute-start.1 = (bf16[32,1,16,128]{3,2,1,0:T(8,128)(2,1)S(1)}, bf16[32,1,16,128]{3,2,1,0:T(8,128)(2,1)S(1)}, u32[]{:S(2)}, u32[]{:S(2)}) collective-permute-start(bf16[32,1,16,128]{3,2,1,0:T(8,128)(2,1)S(1)} %get-tuple-element.9), channel_id=1, source_target_pairs={{64,0},{128,64},{192,128},{256,192},{320,256},{384,320},{448,384},... | collective-permute-start | bytes 393224 | tf_op jit(solution)/shard_map/ppermute | solution.py:20
  17.6 0.7 bitcast_add_fusion
  18.4 0.7 convert_bitcast_fusion.1
  19.0 0.0 collective-permute-done
  19.1 1.0 constant_dynamic-update-slice_fusion.1
  20.1 0.0 collective-permute-done.1
  20.1 0.1 fusion.40
  20.2 1.5 collective-permute-start.2
  21.8 1.3 collective-permute-start.3
  23.1 1.9 %copy.53 = bf16[32,4,16,128]{0,2,3,1:T(8,128)(2,1)S(1)} copy(bf16[32,4,16,128]{3,2,1,0:T(8,128)(2,1)S(1)} %constant_dynamic-update-slice_fusion) | data formatting | bytes 1048576 | tf_op jit(solution)/shard_map/concatenate | solution.py:16
  25.0 0.0 collective-permute-done.2
  25.0 0.2 copy.52
  25.2 1.2 collective-permute-done.3
  26.4 0.2 copy.54
  26.6 1.8 %pad_maximum_fusion = bf16[32,4,18,128]{0,2,3,1:T(8,128)(2,1)S(1)} fusion(bf16[32,4,1,128]{0,2,3,1:T(2,128)(2,1)S(1)} %copy.54, bf16[32,4,16,128]{0,2,3,1:T(8,128)(2,1)S(1)} %copy.53, bf16[32,4,1,128]{0,2,3,1:T(2,128)(2,1)S(1)} %copy.52), kind=kLoop, calls=%fused_computation.12 | loop fusion | flops 1769472 | bytes 1179648 | tf_op jit(solution)/shard_map/concatenate | solution.py:16
  28.4 0.0 copy-start.1
  28.4 1.6 copy-done.1
  30.0 4.0 %collective-permute-start.4 = (bf16[32,4,18,1]{0,2,3,1:T(8,128)(2,1)S(1)}, bf16[32,4,18,1]{0,2,3,1:T(8,128)(2,1)S(1)}, u32[]{:S(2)}, u32[]{:S(2)}) collective-permute-start(bf16[32,4,18,1]{0,2,3,1:T(8,128)(2,1)S(1)} %get-tuple-element.5), channel_id=1, source_target_pairs={{0,1},{1,2},{2,3},{3,4},{4,5},{5,6},{6,7},{8,9},{9,10},{10,11},{11... | collective-permute-start | bytes 13832 | tf_op jit(solution)/shard_map/ppermute | solution.py:18
  34.0 1.3 collective-permute-start.5
  35.3 3.5 %copy.56 = bf16[32,4,18,128]{3,0,2,1:T(8,128)(2,1)S(1)} copy(bf16[32,4,18,128]{0,2,3,1:T(8,128)(2,1)} %copy-done.1) | data formatting | bytes 1179648 | tf_op jit(solution)/shard_map/concatenate | solution.py:16
  38.8 0.0 collective-permute-done.4
  38.9 0.5 copy.55
  39.4 0.0 collective-permute-done.5
  39.4 0.5 copy.57
  40.0 1.7 %maximum_bitcast_fusion = bf16[32,4,18,1,130]{4,0,2,1,3:T(8,128)(2,1)} fusion(bf16[32,4,18,1]{3,0,2,1:T(8,128)(2,1)S(1)} %copy.57, bf16[32,4,18,128]{3,0,2,1:T(8,128)(2,1)S(1)} %copy.56, bf16[32,4,18,1]{3,0,2,1:T(8,128)(2,1)S(1)} %copy.55), kind=kLoop, calls=%fused_computation.23 | loop fusion | flops 1797120 | bytes 1198080 | tf_op jit(solution)/shard_map/broadcast_in_dim | solution.py:45
  41.7 4.9 %copy.68 = bf16[32,4,18,1,130]{0,1,4,2,3:T(4,128)(2,1)S(1)} copy(bf16[32,4,18,1,130]{4,0,2,1,3:T(8,128)(2,1)} %maximum_bitcast_fusion) | data formatting | bytes 1198080
  46.6 1.3 pad.clone
  47.9 0.0 copy-start.4
  47.9 0.0 copy-start.8
  47.9 0.0 copy-start.9
  47.9 0.3 copy.60
  48.2 0.1 slice.46
  48.3 0.5 copy-done.4
  48.8 0.0 copy-done.8
  48.8 0.0 copy-done.9
  48.8 3.2 %maximum_convert_fusion = bf16[2,16,8,17,32]{4,2,3,1,0:T(8,128)(2,1)S(1)} fusion(bf16[3,3,3,32,32]{4,3,2,1,0:T(8,128)(2,1)S(1)} %bitcast.48, bf16[32,4,18,1,7,2]{0,4,5,2,1,3:T(8,128)(2,1)S(1)} %slice.46, bf16[32,4,18,1,8,17]{0,4,5,2,1,3:T(8,128)(2,1)S(1)} %copy.60, f32[32]{0:T(128)S(1)} %copy-done.8, pred[8,17]{0,1:T(8,128)(4,1)S(1)} %copy-done.9), kind=kOutput, calls=%fused_computation.19 | convolution fusion | flops 243306496 | bytes 1025288 | tf_op jit(solution)/shard_map/conv_general_dilated | solution.py:44
  52.0 0.0 copy-start.5
  52.0 0.1 copy.61
  52.2 0.2 slice_bitcast_fusion
  52.4 1.0 copy.62
  53.4 0.1 reshape.119
  53.5 0.0 copy-done.5
  53.5 0.0 copy-start.2
  53.6 1.5 fusion
  55.1 1.5 fusion.2
  56.7 0.1 copy.63
  56.8 0.6 maximum_bitcast_fusion.1
  57.4 0.0 all-gather.4.cloned.1.call-update
  57.4 0.0 copy-done.2
  57.5 91.2 %all-gather.4.cloned.1.call-done = bf16[64,129,256]{2,1,0:T(8,128)(2,1)} async-done(((bf16[1,129,256]{2,1,0:T(8,128)(2,1)}), bf16[64,129,256]{2,1,0:T(8,128)(2,1)}) %all-gather.4.cloned.1.call-update) | async-done | bytes 4227088 | tf_op jit(solution)/shard_map/all_gather | solution.py:73
  148.7 1.0 slice.48
  149.7 0.0 copy-start.3
  149.7 0.0 copy-start.6
  149.7 4.8 %slice.51 = bf16[64,128,256]{2,1,0:T(8,128)(2,1)} slice(bf16[64,129,256]{2,1,0:T(8,128)(2,1)} %all-gather.4.cloned.1.call-done), slice={[0:64], [0:128], [0:256]} | slice | bytes 8388608 | tf_op jit(solution)/shard_map/slice | solution.py:74
  154.5 0.0 copy-done.3
  154.5 0.0 copy-done.6
  154.5 3.2 %multiply_convert_fusion.1 = bf16[128,512]{1,0:T(8,128)(2,1)S(1)} fusion(bf16[256,512]{1,0:T(8,128)(2,1)S(1)} %copy-done.3, bf16[8192,256]{1,0:T(8,128)(2,1)} %bitcast.46, s32[8192]{0:T(1024)S(1)} %fusion.33, s32[128]{0:T(128)S(1)} %get-tuple-element.11, f32[512]{0:T(512)S(1)} %copy-done.6), kind=kOutput, calls=%fused_computation.30 | convolution fusion | flops 571899904 | bytes 4622848 | tf_op jit(solution)/shard_map/dot_general | solution.py:83
  157.7 0.0 copy-done
  157.7 0.0 copy-done.7
  157.7 0.9 convolution_bitcast_fusion
  (12 shorter events, 0.1 us)
Async XLA Ops:
  6.5 151.1 %copy-start = (bf16[512,512]{1,0:T(8,128)(2,1)S(1)}, bf16[512,512]{1,0:T(8,128)(2,1)}, u32[]{:S(2)}) copy-start(bf16[512,512]{1,0:T(8,128)(2,1)} %param.19) | copy-start | bytes 1572868
  6.5 142.1 %all-gather.4.cloned.1.call-start = ((), (), s32[]{:S(2)}) async-start(), calls=%async_computation | async-start | bytes 4526080 | tf_op jit(solution)/shard_map/all_gather | solution.py:73
  7.6 11.5 %collective-permute-start = (bf16[32,1,16,128]{3,2,1,0:T(8,128)(2,1)S(1)}, bf16[32,1,16,128]{3,2,1,0:T(8,128)(2,1)S(1)}, u32[]{:S(2)}, u32[]{:S(2)}) collective-permute-start(bf16[32,1,16,128]{3,2,1,0:T(8,128)(2,1)S(1)} %get-tuple-element.10), channel_id=1, source_target_pairs={{0,64},{64,128},{128,192},{192,256},{256,320},{320,384},{384,448},... | collective-permute-start | bytes 393224 | tf_op jit(solution)/shard_map/ppermute | solution.py:18
  12.1 8.0 %collective-permute-start.1 = (bf16[32,1,16,128]{3,2,1,0:T(8,128)(2,1)S(1)}, bf16[32,1,16,128]{3,2,1,0:T(8,128)(2,1)S(1)}, u32[]{:S(2)}, u32[]{:S(2)}) collective-permute-start(bf16[32,1,16,128]{3,2,1,0:T(8,128)(2,1)S(1)} %get-tuple-element.9), channel_id=1, source_target_pairs={{64,0},{128,64},{192,128},{256,192},{320,256},{384,320},{448,384},... | collective-permute-start | bytes 393224 | tf_op jit(solution)/shard_map/ppermute | solution.py:20
  20.2 4.8 %collective-permute-start.2 = (bf16[32,4,1,128]{3,0,2,1:T(8,128)(2,1)S(1)}, bf16[32,4,1,128]{3,0,2,1:T(8,128)(2,1)S(1)}, u32[]{:S(2)}, u32[]{:S(2)}) collective-permute-start(bf16[32,4,1,128]{3,0,2,1:T(8,128)(2,1)S(1)} %copy.65), channel_id=1, source_target_pairs={{0,8},{8,16},{16,24},{24,32},{32,40},{40,48},{48,56},{1,9},{9,17},... | collective-permute-start | bytes 98312 | tf_op jit(solution)/shard_map/ppermute | solution.py:18
  21.8 4.7 %collective-permute-start.3 = (bf16[32,4,1,128]{3,0,2,1:T(8,128)(2,1)S(1)}, bf16[32,4,1,128]{3,0,2,1:T(8,128)(2,1)S(1)}, u32[]{:S(2)}, u32[]{:S(2)}) collective-permute-start(bf16[32,4,1,128]{3,0,2,1:T(8,128)(2,1)S(1)} %copy.66), channel_id=1, source_target_pairs={{8,0},{16,8},{24,16},{32,24},{40,32},{48,40},{56,48},{9,1},{17,9},... | collective-permute-start | bytes 98312 | tf_op jit(solution)/shard_map/ppermute | solution.py:20
  28.4 1.6 copy-start.1
  30.0 8.8 %collective-permute-start.4 = (bf16[32,4,18,1]{0,2,3,1:T(8,128)(2,1)S(1)}, bf16[32,4,18,1]{0,2,3,1:T(8,128)(2,1)S(1)}, u32[]{:S(2)}, u32[]{:S(2)}) collective-permute-start(bf16[32,4,18,1]{0,2,3,1:T(8,128)(2,1)S(1)} %get-tuple-element.5), channel_id=1, source_target_pairs={{0,1},{1,2},{2,3},{3,4},{4,5},{5,6},{6,7},{8,9},{9,10},{10,11},{11... | collective-permute-start | bytes 13832 | tf_op jit(solution)/shard_map/ppermute | solution.py:18
  34.0 5.4 %collective-permute-start.5 = (bf16[32,4,18,1]{0,2,3,1:T(8,128)(2,1)S(1)}, bf16[32,4,18,1]{0,2,3,1:T(8,128)(2,1)S(1)}, u32[]{:S(2)}, u32[]{:S(2)}) collective-permute-start(bf16[32,4,18,1]{0,2,3,1:T(8,128)(2,1)S(1)} %get-tuple-element.6), channel_id=1, source_target_pairs={{1,0},{2,1},{3,2},{4,3},{5,4},{6,5},{7,6},{9,8},{10,9},{11,10},{12... | collective-permute-start | bytes 13832 | tf_op jit(solution)/shard_map/ppermute | solution.py:20
  47.9 0.9 copy-start.4
  47.9 0.9 copy-start.8
  47.9 0.9 copy-start.9
  52.0 1.5 copy-start.5
  53.5 3.9 %copy-start.2 = (bf16[512]{0:T(512)(128)(2,1)S(1)}, bf16[512]{0:T(512)(128)(2,1)}, u32[]{:S(2)}) copy-start(bf16[512]{0:T(512)(128)(2,1)} %param.21) | copy-start | bytes 3076
  149.7 4.8 %copy-start.3 = (bf16[256,512]{1,0:T(8,128)(2,1)S(1)}, bf16[256,512]{1,0:T(8,128)(2,1)}, u32[]{:S(2)}) copy-start(bf16[256,512]{1,0:T(8,128)(2,1)} %param.17) | copy-start | bytes 786436
  149.7 4.8 %copy-start.6 = (f32[512]{0:T(512)S(1)}, f32[512]{0:T(512)}, u32[]{:S(2)}) copy-start(f32[512]{0:T(512)} %param.18) | copy-start | bytes 6148
  154.5 3.2 %copy-start.7 = (f32[512]{0:T(512)S(1)}, f32[512]{0:T(512)}, u32[]{:S(2)}) copy-start(f32[512]{0:T(512)} %param.20) | copy-start | bytes 6148
Sparse Core Ops, SparseCore 0:
  57.6 91.0 all-gather.3

commit v4 on v2

--- a/solution.py
+++ b/solution.py
@@ -39,31 +39,29 @@
 ):
     channels, extent_x, extent_y, extent_z = features.shape
     volume = extent_x * extent_y * extent_z
-    padded = extended(features, (("gx", 1), ("gy", 2), ("gz", 3)), 1)
-    kernel = conv_weight.reshape(3, 3, 3, channels, channels).transpose(3, 4, 0, 1, 2)
+    cells = features.transpose(1, 2, 3, 0)
+    padded = extended(cells, (("gx", 0), ("gy", 1), ("gz", 2)), 1)
+    kernel = conv_weight.reshape(3, 3, 3, channels, channels).transpose(0, 1, 2, 4, 3)
     total = lax.conv_general_dilated(
         padded[None],
         kernel,
         (1, 1, 1),
         "VALID",
-        dimension_numbers=("NCDHW", "OIDHW", "NCDHW"),
+        dimension_numbers=("NDHWC", "DHWIO", "NDHWC"),
         preferred_element_type=jnp.float32,
-    )[0].reshape(channels, volume)
-    fields = jnp.maximum(total + conv_bias[:, None], 0.0).astype(jnp.bfloat16)
+    )[0].reshape(volume, channels)
+    fields = jnp.maximum(total + conv_bias[None, :], 0.0).astype(jnp.bfloat16)
     pair_count = pair_edge.shape[0]
     slot_count = pair_count * BINS
     slots_flat = voxel_slot.reshape(volume)
-    block_width = 512
-    pieces = []
-    for block in range(slot_count // block_width):
-        labels = block * block_width + lax.iota(jnp.int32, block_width)
-        onehot = (slots_flat[:, None] == labels[None, :]).astype(jnp.bfloat16)
-        pieces.append(jnp.dot(fields, onehot, preferred_element_type=jnp.float32))
-    pooled = jnp.concatenate(pieces, axis=1) * (slot_count / volume)
+    onehot = (slots_flat[:, None] == lax.iota(jnp.int32, slot_count)[None, :]).astype(jnp.bfloat16)
+    pooled = lax.dot_general(
+        onehot, fields, (((0,), (0,)), ((), ())), preferred_element_type=jnp.float32
+    ) * (slot_count / volume)
     row_width = BINS * channels
     pair_rows = (
-        pooled.reshape(channels, BINS, pair_count)
-        .transpose(2, 1, 0)
+        pooled.reshape(BINS, pair_count, channels)
+        .transpose(1, 0, 2)
         .reshape(pair_count, row_width)
         .astype(jnp.bfloat16)
     )

time: 98 us -> 94.1 us (0.960)
  local copies, waits for them, and re-layouts: 23.3 us -> 16.3 us
  waiting for transfers between devices: 15.6 us -> 21.8 us
  other arithmetic: 8.3 us -> 5.94 us
    ppermute x3, waiting for transfers between devices: 2.38 us -> 8.58 us  [extended(): lax.ppermute(head, axis, [((i + 1) % count, i) for i in range(ends)])]
    concatenate x3 -> x0, local copies, waits for them, and re-layouts: 5.62 us -> none  [extended(): jnp.concatenate([lax.ppermute(tail, axis, [(i, (i + 1) % count) for i in...]
    concatenate x1, other arithmetic: 1.79 us -> 0.11 us  [extended(): jnp.concatenate([lax.ppermute(tail, axis, [(i, (i + 1) % count) for i in...]
    conv_general_dilated x2 -> x5, local copies, waits for them, and re-layouts: 0.41 us -> 1.98 us  [body(): lax.conv_general_dilated(padded[None], kernel, (1, 1, 1), 'VALID', dimens...]
    convert_element_type x5 -> x2, local copies, waits for them, and re-layouts: 1.59 us -> 0.12 us  [body(): pair_rows = pooled.reshape(BINS, pair_count, channels).transpose(1, 0, 2)...]
    slice x1 -> x0, local copies, waits for them, and re-layouts: 1.04 us -> none  [extended(): head = lax.slice_in_dim(cells, 0, width, axis=dim)]
    unnamed x28 -> x27, local copies, waits for them, and re-layouts: 7.96 us -> 7.44 us
    dot_general x2 -> x1, matrix products: 3.07 us -> 2.85 us  [body(): lax.dot_general(onehot, fields, (((0,), (0,)), ((), ())), preferred_eleme...]
  transfers between devices with their start and end apart: 7 -> 7, of which waited for: 2 -> 4; matrix products, arithmetic and copies ran while one was open for 12% -> 5% of each run, Pallas kernels for 0% -> 0%
where the time goes in v4:
time: 94.1 us; the launch traced here: 93.6 us
  starting transfers between devices  28 us (30%)
  waiting for transfers between devices  21.8 us (23%)
  local copies, waits for them, and re-layouts  16.3 us (17%)
  blocking collectives  14.2 us (15%)
  matrix products  6.9 us (7%)
  other arithmetic  5.94 us (6%)
    all_to_all x1, blocking collectives, body(): lax.all_to_all(owner_scores.reshape(groups, capacity), ('gx', 'gy'), spli...  14.2 us
    all_to_all x1, waiting for transfers between devices, body(): lax.all_to_all(send, ('gx', 'gy'), split_axis=0, concat_axis=0, tiled=True)  13.2 us
    all_to_all x1, starting transfers between devices, body(): lax.all_to_all(send, ('gx', 'gy'), split_axis=0, concat_axis=0, tiled=True)  12.7 us
    ppermute x3, starting transfers between devices, extended(): lax.ppermute(tail, axis, [(i, (i + 1) % count) for i in range(ends)])  10.7 us
    ppermute x3, waiting for transfers between devices, extended(): lax.ppermute(head, axis, [((i + 1) % count, i) for i in range(ends)])  8.58 us
    unnamed x27, local copies, waits for them, and re-layouts  7.44 us
    ppermute x3, starting transfers between devices, extended(): lax.ppermute(head, axis, [((i + 1) % count, i) for i in range(ends)])  4.5 us
    conv_general_dilated x1, matrix products, body(): lax.conv_general_dilated(padded[None], kernel, (1, 1, 1), 'VALID', dimens...  3.35 us
  transfers between devices with their start and end apart: 7, of which 4 were waited for; matrix products, arithmetic and copies ran while one was open for 5% of the time, Pallas kernels for 0%

profile of v4, /device:TPU:192, one launch (start us, length us, event | category | flops | bytes accessed | tf_op | source)
XLA Modules:
  0.0 93.6 jit_solution(15824406301769893312)
XLA Ops:
  0.0 1.1 %copy.69 = bf16[32,2,16,128]{3,0,2,1:T(8,128)(2,1)S(1)} copy(bf16[32,2,16,128]{3,2,1,0:T(8,128)(2,1)} %param.11) | data formatting | bytes 524288 | tf_op args[0]
  1.1 1.7 %collective-permute-start = (bf16[1,16,128,32]{2,3,1,0:T(8,128)(2,1)S(1)}, bf16[1,16,128,32]{2,3,1,0:T(8,128)(2,1)S(1)}, u32[]{:S(2)}, u32[]{:S(2)}) collective-permute-start(bf16[1,16,128,32]{2,3,1,0:T(8,128)(2,1)S(1)} %get-tuple-element.9), channel_id=1, source_target_pairs={{0,64},{64,128},{128,192},{192,256},{256,320},{320,384},{384,448},... | collective-permute-start | bytes 393224 | tf_op jit(solution)/shard_map/ppermute | solution.py:18
  2.9 1.3 %collective-permute-start.1 = (bf16[1,16,128,32]{2,3,1,0:T(8,128)(2,1)S(1)}, bf16[1,16,128,32]{2,3,1,0:T(8,128)(2,1)S(1)}, u32[]{:S(2)}, u32[]{:S(2)}) collective-permute-start(bf16[1,16,128,32]{2,3,1,0:T(8,128)(2,1)S(1)} %get-tuple-element.10), channel_id=1, source_target_pairs={{64,0},{128,64},{192,128},{256,192},{320,256},{384,320},{448,384},... | collective-permute-start | bytes 393224 | tf_op jit(solution)/shard_map/ppermute | solution.py:20
  4.2 0.7 fusion.25
  4.9 0.2 reduce_window_sum.11
  5.1 0.0 collective-permute-done
  5.1 2.3 %collective-permute-done.1 = bf16[1,16,128,32]{2,3,1,0:T(8,128)(2,1)S(1)} collective-permute-done((bf16[1,16,128,32]{2,3,1,0:T(8,128)(2,1)S(1)}, bf16[1,16,128,32]{2,3,1,0:T(8,128)(2,1)S(1)}, u32[]{:S(2)}, u32[]{:S(2)}) %collective-permute-start.1) | collective-permute-done | bytes 131104 | tf_op jit(solution)/shard_map/ppermute | solution.py:20
  7.4 3.5 %collective-permute-start.2 = (bf16[4,1,128,32]{2,3,1,0:T(8,128)(2,1)S(1)}, bf16[4,1,128,32]{2,3,1,0:T(8,128)(2,1)S(1)}, u32[]{:S(2)}, u32[]{:S(2)}) collective-permute-start(bf16[4,1,128,32]{2,3,1,0:T(8,128)(2,1)S(1)} %get-tuple-element.7), channel_id=1, source_target_pairs={{0,8},{8,16},{16,24},{24,32},{32,40},{40,48},{48,56},{1,9},{9,17},... | collective-permute-start | bytes 98312 | tf_op jit(solution)/shard_map/ppermute | solution.py:18
  10.9 1.3 %collective-permute-start.3 = (bf16[4,1,128,32]{2,3,1,0:T(8,128)(2,1)S(1)}, bf16[4,1,128,32]{2,3,1,0:T(8,128)(2,1)S(1)}, u32[]{:S(2)}, u32[]{:S(2)}) collective-permute-start(bf16[4,1,128,32]{2,3,1,0:T(8,128)(2,1)S(1)} %get-tuple-element.8), channel_id=1, source_target_pairs={{8,0},{16,8},{24,16},{32,24},{40,32},{48,40},{56,48},{9,1},{17,9},... | collective-permute-start | bytes 98312 | tf_op jit(solution)/shard_map/ppermute | solution.py:20
  12.2 0.8 select_reduce_fusion.2
  13.0 0.0 copy-start.1
  13.1 0.0 copy-start.8
  13.1 0.0 collective-permute-done.2
  13.1 3.6 %collective-permute-done.3 = bf16[4,1,128,32]{2,3,1,0:T(8,128)(2,1)S(1)} collective-permute-done((bf16[4,1,128,32]{2,3,1,0:T(8,128)(2,1)S(1)}, bf16[4,1,128,32]{2,3,1,0:T(8,128)(2,1)S(1)}, u32[]{:S(2)}, u32[]{:S(2)}) %collective-permute-start.3) | collective-permute-done | bytes 32800 | tf_op jit(solution)/shard_map/ppermute | solution.py:20
  16.7 0.1 pad_maximum_fusion
  16.8 0.2 fusion.38
  17.1 0.5 copy.63
  17.6 5.5 %collective-permute-start.4 = (bf16[4,18,1,32]{3,0,2,1:T(4,128)(2,1)S(1)}, bf16[4,18,1,32]{3,0,2,1:T(4,128)(2,1)S(1)}, u32[]{:S(2)}, u32[]{:S(2)}) collective-permute-start(bf16[4,18,1,32]{3,0,2,1:T(4,128)(2,1)S(1)} %copy.63), channel_id=1, source_target_pairs={{0,1},{1,2},{2,3},{3,4},{4,5},{5,6},{6,7},{8,9},{9,10},{10,11},{11... | collective-permute-start | bytes 13832 | tf_op jit(solution)/shard_map/ppermute | solution.py:18
  23.1 0.5 copy.64
  23.6 1.9 %collective-permute-start.5 = (bf16[4,18,1,32]{3,0,2,1:T(4,128)(2,1)S(1)}, bf16[4,18,1,32]{3,0,2,1:T(4,128)(2,1)S(1)}, u32[]{:S(2)}, u32[]{:S(2)}) collective-permute-start(bf16[4,18,1,32]{3,0,2,1:T(4,128)(2,1)S(1)} %copy.64), channel_id=1, source_target_pairs={{1,0},{2,1},{3,2},{4,3},{5,4},{6,5},{7,6},{9,8},{10,9},{11,10},{12... | collective-permute-start | bytes 13832 | tf_op jit(solution)/shard_map/ppermute | solution.py:20
  25.5 1.5 %scatter_custom_fusion.1 = bf16[320]{0:T(512)(128)(2,1)S(1)} fusion(s32[128]{0:T(128)S(1)} %get-tuple-element.12, bf16[128]{0:T(256)(128)(2,1)S(1)} %convert_element_type.54, bf16[]{:T(256)} %constant.23.clone.1), kind=kCustom, calls=%fused_computation.55 | custom fusion | bytes 642 | tf_op jit(solution)/shard_map/scatter | solution.py:78
  27.1 0.1 reshape.78
  27.2 0.0 collective-permute-done.4
  27.2 0.5 copy.52
  27.8 2.6 %collective-permute-done.5 = bf16[4,18,1,32]{3,0,2,1:T(4,128)(2,1)S(1)} collective-permute-done((bf16[4,18,1,32]{3,0,2,1:T(4,128)(2,1)S(1)}, bf16[4,18,1,32]{3,0,2,1:T(4,128)(2,1)S(1)}, u32[]{:S(2)}, u32[]{:S(2)}) %collective-permute-start.5) | collective-permute-done | bytes 4640 | tf_op jit(solution)/shard_map/ppermute | solution.py:20
  30.4 0.5 copy.53
  31.0 1.7 %maximum_bitcast_fusion = bf16[4,18,1,130,32]{3,4,1,0,2:T(8,128)(2,1)} fusion(bf16[4,18,1,32]{2,3,1,0:T(8,128)(2,1)S(1)} %copy.53, bf16[4,1,128,32]{2,3,1,0:T(8,128)(2,1)S(1)} %collective-permute-done.3, bf16[1,16,128,32]{2,3,1,0:T(8,128)(2,1)S(1)} %collective-permute-done.1, bf16[2,16,128,32]{2,3,1,0:T(8,128)(2,1)S(1)} %bitcast.52, ...), kind=kLoop, calls=%fused_computation.15 | loop fusion | flops 4193280 | bytes 1198080 | tf_op jit(solution)/shard_map/broadcast_in_dim | solution.py:46
  32.7 4.8 %copy.65 = bf16[4,18,1,130,32]{4,0,3,1,2:T(4,128)(2,1)S(1)} copy(bf16[4,18,1,130,32]{3,4,1,0,2:T(8,128)(2,1)} %maximum_bitcast_fusion) | data formatting | bytes 1198080
  37.4 1.3 %pad.5.clone = bf16[4,18,1,136,32]{4,0,3,1,2:T(4,128)(2,1)S(1)} pad(bf16[4,18,1,130,32]{4,0,3,1,2:T(4,128)(2,1)S(1)} %copy.65, bf16[]{:T(256)} %constant.6.clone.1), padding=0_0x0_0x0_0x0_6x0_0 | pad | bytes 1225730 | tf_op jit(solution)/shard_map/broadcast_in_dim | solution.py:46
  38.7 0.0 copy-start.4
  38.7 0.0 copy-start.10
  38.7 0.3 copy.56
  39.1 0.1 slice.38
  39.1 0.5 copy-done.4
  39.6 3.4 %fusion.10 = f32[2,16,8,17,32]{4,2,3,1,0:T(8,128)S(1)} fusion(bf16[3,3,3,32,32]{4,3,2,1,0:T(8,128)(2,1)S(1)} %bitcast.58, bf16[4,18,1,7,2,32]{5,3,4,1,0,2:T(8,128)(2,1)S(1)} %slice.38, bf16[4,18,1,8,17,32]{5,3,4,1,0,2:T(8,128)(2,1)S(1)} %copy.56, pred[8,17]{0,1:T(8,128)(4,1)S(1)} %copy-done.10), kind=kOutput, calls=%fused_computation.13 | convolution fusion | flops 242888704 | bytes 1303688 | tf_op jit(solution)/shard_map/conv_general_dilated | solution.py:45
  43.0 0.4 copy.57
  43.4 0.1 slice.39
  43.6 0.0 copy-start.5
  43.6 0.0 copy-start.9
  43.6 1.0 %copy.58 = f32[2,16,1,128,32]{3,1,0,4,2:T(8,128)S(1)} copy(f32[2,16,1,128,32]{4,1,3,0,2:T(8,128)S(1)} %slice.39) | data formatting | bytes 1048576 | tf_op jit(solution)/shard_map/conv_general_dilated | solution.py:45
  44.6 0.1 reshape_squeeze.4
  44.8 0.0 copy-start.2
  44.8 2.8 %fusion.16 = bf16[4,8,8,128]{3,2,1,0:T(8,128)(2,1)S(1)} fusion(s32[4096]{0:T(1024)S(1)} %bitcast.59, f32[4096,32]{0,1:T(8,128)S(1)} %reshape_squeeze.4, f32[32]{0:T(128)S(1)} %copy-done.9), kind=kOutput, calls=%fused_computation.20 | convolution fusion | flops 273088512 | bytes 606336 | tf_op jit(solution)/shard_map/dot_general | solution.py:58
  47.6 0.0 copy-start.3
  47.6 0.0 copy-start.6
  47.7 0.0 copy-start.7
  47.7 0.1 copy.60
  47.8 1.3 %scatter_custom_fusion = bf16[320,256]{1,0:T(8,128)(2,1)S(1)} fusion(s32[128]{0:T(128)S(1)} %get-tuple-element.12, bf16[128,256]{1,0:T(8,128)(2,1)S(1)} %copy.60, bf16[]{:T(256)} %constant.6.clone.1), kind=kCustom, calls=%fused_computation.38 | custom fusion | bytes 163842 | tf_op jit(solution)/shard_map/scatter | solution.py:77
  49.1 0.1 reshape.42
  49.2 0.8 fusion.18
  50.0 12.7 %all-to-all-start = ((bf16[64,6,256]{2,1,0:T(8,128)(2,1)}), bf16[64,6,256]{2,1,0:T(8,128)(2,1)S(1)}, u32[]{:S(2)}, u32[]{:S(2)}) async-start(bf16[64,6,256]{2,1,0:T(8,128)(2,1)} %fusion.18), calls=%async_computation | async-start | bytes 524288 | tf_op jit(solution)/shard_map/all_to_all | solution.py:84
  62.8 13.2 %all-to-all-done = bf16[64,6,256]{2,1,0:T(8,128)(2,1)S(1)} async-done(((bf16[64,6,256]{2,1,0:T(8,128)(2,1)}), bf16[64,6,256]{2,1,0:T(8,128)(2,1)S(1)}, u32[]{:S(2)}, u32[]{:S(2)}) %all-to-all-start) | async-done | bytes 196640 | tf_op jit(solution)/shard_map/all_to_all | solution.py:84
  76.0 0.1 reshape.44
  76.1 0.1 fusion.28
  76.2 0.1 reshape.52
  76.3 0.3 multiply_convert_fusion.1
  76.7 0.4 convolution_bitcast_fusion
  77.1 0.1 select_reduce_fusion.1
  77.2 0.1 all_to_all.10
  77.3 14.2 %all_to_all.14 = f32[64,1,5]{2,1,0:T(1,128)S(1)} all-to-all(f32[64,1,5]{2,1,0:T(1,128)S(1)} %bitcast.55), channel_id=1, replica_groups=mesh['gx'=8,'gy'=8,'gz'=8] {'gx','gy'}, dimensions={0} | all-to-all | bytes 2560 | tf_op jit(solution)/shard_map/all_to_all | solution.py:102
  91.6 0.5 broadcast.54
  92.1 0.7 reduce.7
  92.8 0.1 broadcast_in_dim.54
  92.9 0.6 select_reduce_fusion
  (17 shorter events, 0.1 us)
Async XLA Ops:
  0.0 76.7 %copy-start = (bf16[512,512]{1,0:T(8,128)(2,1)S(1)}, bf16[512,512]{1,0:T(8,128)(2,1)}, u32[]{:S(2)}) copy-start(bf16[512,512]{1,0:T(8,128)(2,1)} %param.19) | copy-start | bytes 1572868
  1.1 4.0 %collective-permute-start = (bf16[1,16,128,32]{2,3,1,0:T(8,128)(2,1)S(1)}, bf16[1,16,128,32]{2,3,1,0:T(8,128)(2,1)S(1)}, u32[]{:S(2)}, u32[]{:S(2)}) collective-permute-start(bf16[1,16,128,32]{2,3,1,0:T(8,128)(2,1)S(1)} %get-tuple-element.9), channel_id=1, source_target_pairs={{0,64},{64,128},{128,192},{192,256},{256,320},{320,384},{384,448},... | collective-permute-start | bytes 393224 | tf_op jit(solution)/shard_map/ppermute | solution.py:18
  2.9 4.5 %collective-permute-start.1 = (bf16[1,16,128,32]{2,3,1,0:T(8,128)(2,1)S(1)}, bf16[1,16,128,32]{2,3,1,0:T(8,128)(2,1)S(1)}, u32[]{:S(2)}, u32[]{:S(2)}) collective-permute-start(bf16[1,16,128,32]{2,3,1,0:T(8,128)(2,1)S(1)} %get-tuple-element.10), channel_id=1, source_target_pairs={{64,0},{128,64},{192,128},{256,192},{320,256},{384,320},{448,384},... | collective-permute-start | bytes 393224 | tf_op jit(solution)/shard_map/ppermute | solution.py:20
  7.4 5.6 %collective-permute-start.2 = (bf16[4,1,128,32]{2,3,1,0:T(8,128)(2,1)S(1)}, bf16[4,1,128,32]{2,3,1,0:T(8,128)(2,1)S(1)}, u32[]{:S(2)}, u32[]{:S(2)}) collective-permute-start(bf16[4,1,128,32]{2,3,1,0:T(8,128)(2,1)S(1)} %get-tuple-element.7), channel_id=1, source_target_pairs={{0,8},{8,16},{16,24},{24,32},{32,40},{40,48},{48,56},{1,9},{9,17},... | collective-permute-start | bytes 98312 | tf_op jit(solution)/shard_map/ppermute | solution.py:18
  10.9 5.8 %collective-permute-start.3 = (bf16[4,1,128,32]{2,3,1,0:T(8,128)(2,1)S(1)}, bf16[4,1,128,32]{2,3,1,0:T(8,128)(2,1)S(1)}, u32[]{:S(2)}, u32[]{:S(2)}) collective-permute-start(bf16[4,1,128,32]{2,3,1,0:T(8,128)(2,1)S(1)} %get-tuple-element.8), channel_id=1, source_target_pairs={{8,0},{16,8},{24,16},{32,24},{40,32},{48,40},{56,48},{9,1},{17,9},... | collective-permute-start | bytes 98312 | tf_op jit(solution)/shard_map/ppermute | solution.py:20
  13.0 12.5 %copy-start.1 = (s32[128,1]{0,1:T(1,128)S(1)}, s32[128,1]{0,1:T(1,128)}, u32[]{:S(2)}) copy-start(s32[128,1]{0,1:T(1,128)} %param.15) | copy-start | bytes 1540
  13.1 12.5 %copy-start.8 = (s32[128]{0:T(128)S(1)}, s32[128]{0:T(128)}, u32[]{:S(2)}) copy-start(s32[128]{0:T(128)} %param.16) | copy-start | bytes 1540
  17.6 9.7 %collective-permute-start.4 = (bf16[4,18,1,32]{3,0,2,1:T(4,128)(2,1)S(1)}, bf16[4,18,1,32]{3,0,2,1:T(4,128)(2,1)S(1)}, u32[]{:S(2)}, u32[]{:S(2)}) collective-permute-start(bf16[4,18,1,32]{3,0,2,1:T(4,128)(2,1)S(1)} %copy.63), channel_id=1, source_target_pairs={{0,1},{1,2},{2,3},{3,4},{4,5},{5,6},{6,7},{8,9},{9,10},{10,11},{11... | collective-permute-start | bytes 13832 | tf_op jit(solution)/shard_map/ppermute | solution.py:18
  23.6 6.9 %collective-permute-start.5 = (bf16[4,18,1,32]{3,0,2,1:T(4,128)(2,1)S(1)}, bf16[4,18,1,32]{3,0,2,1:T(4,128)(2,1)S(1)}, u32[]{:S(2)}, u32[]{:S(2)}) collective-permute-start(bf16[4,18,1,32]{3,0,2,1:T(4,128)(2,1)S(1)} %copy.64), channel_id=1, source_target_pairs={{1,0},{2,1},{3,2},{4,3},{5,4},{6,5},{7,6},{9,8},{10,9},{11,10},{12... | collective-permute-start | bytes 13832 | tf_op jit(solution)/shard_map/ppermute | solution.py:20
  38.7 0.9 %copy-start.4 = (bf16[27,32,32]{2,1,0:T(8,128)(2,1)S(1)}, bf16[27,32,32]{2,1,0:T(8,128)(2,1)}, u32[]{:S(2)}) copy-start(bf16[27,32,32]{2,1,0:T(8,128)(2,1)} %param.13) | copy-start | bytes 165892
  38.7 0.9 copy-start.10
  43.6 1.1 %copy-start.5 = (s32[2,16,128]{2,1,0:T(8,128)S(1)}, s32[2,16,128]{2,1,0:T(8,128)}, u32[]{:S(2)}) copy-start(s32[2,16,128]{2,1,0:T(8,128)} %param.12) | copy-start | bytes 49156
  43.6 1.1 %copy-start.9 = (f32[32]{0:T(128)S(1)}, f32[32]{0:T(128)}, u32[]{:S(2)}) copy-start(f32[32]{0:T(128)} %param.14) | copy-start | bytes 388
  44.8 18.0 %copy-start.2 = (bf16[512]{0:T(512)(128)(2,1)S(1)}, bf16[512]{0:T(512)(128)(2,1)}, u32[]{:S(2)}) copy-start(bf16[512]{0:T(512)(128)(2,1)} %param.21) | copy-start | bytes 3076
  47.6 28.7 %copy-start.3 = (bf16[256,512]{1,0:T(8,128)(2,1)S(1)}, bf16[256,512]{1,0:T(8,128)(2,1)}, u32[]{:S(2)}) copy-start(bf16[256,512]{1,0:T(8,128)(2,1)} %param.17) | copy-start | bytes 786436
  47.6 28.7 %copy-start.6 = (f32[512]{0:T(512)S(1)}, f32[512]{0:T(512)}, u32[]{:S(2)}) copy-start(f32[512]{0:T(512)} %param.18) | copy-start | bytes 6148
  47.7 29.1 %copy-start.7 = (f32[512]{0:T(512)S(1)}, f32[512]{0:T(512)}, u32[]{:S(2)}) copy-start(f32[512]{0:T(512)} %param.20) | copy-start | bytes 6148
  50.0 26.0 %all-to-all-start = ((bf16[64,6,256]{2,1,0:T(8,128)(2,1)}), bf16[64,6,256]{2,1,0:T(8,128)(2,1)S(1)}, u32[]{:S(2)}, u32[]{:S(2)}) async-start(bf16[64,6,256]{2,1,0:T(8,128)(2,1)} %fusion.18), calls=%async_computation | async-start | bytes 524288 | tf_op jit(solution)/shard_map/all_to_all | solution.py:84

commit v5 on v4

--- a/solution.py
+++ b/solution.py
@@ -1,4 +1,5 @@
 import jax
+import numpy as np
 import jax.numpy as jnp
 from jax import lax
 from jax.sharding import PartitionSpec as P
@@ -24,6 +25,40 @@
     return cells
 
 
+def band_selector():
+    sel = np.zeros((3, 4, 4, 3), np.float32)
+    sel[0, 3, 0, 0] = 1.0
+    for zi in range(4):
+        for zo in range(4):
+            if abs(zi - zo) <= 1:
+                sel[1, zi, zo, zi - zo + 1] = 1.0
+    sel[2, 0, 3, 2] = 1.0
+    return sel
+
+
+def banded_weight(conv_weight, channels):
+    taps = conv_weight.astype(jnp.float32).reshape(3, 3, 3, channels, channels).transpose(0, 1, 2, 4, 3)
+    full = jnp.einsum("pizd,xydco->xypiczo", band_selector(), taps, precision=lax.Precision.HIGHEST)
+    return full.reshape(27 * 4 * channels, 4 * channels).astype(jnp.bfloat16)
+
+
+def conv_lane_dense(padded_xy, low, high, conv_weight, channels):
+    px, py, lanes = padded_xy.shape
+    chunk = 4 * channels
+    nchunk = lanes // chunk
+    low_chunk = jnp.pad(low, ((0, 0), (0, 0), (chunk - channels, 0)))[:, :, None]
+    high_chunk = jnp.pad(high, ((0, 0), (0, 0), (0, chunk - channels)))[:, :, None]
+    full = jnp.concatenate([low_chunk, padded_xy.reshape(px, py, nchunk, chunk), high_chunk], axis=2)
+    slabs = [
+        full[dx : dx + px - 2, dy : dy + py - 2, p : p + nchunk, :]
+        for dx in range(3)
+        for dy in range(3)
+        for p in range(3)
+    ]
+    stacked = jnp.concatenate(slabs, axis=3)
+    return jnp.dot(stacked, banded_weight(conv_weight, channels), preferred_element_type=jnp.float32)
+
+
 def body(
     features,
     voxel_slot,
@@ -39,17 +74,16 @@
 ):
     channels, extent_x, extent_y, extent_z = features.shape
     volume = extent_x * extent_y * extent_z
-    cells = features.transpose(1, 2, 3, 0)
-    padded = extended(cells, (("gx", 0), ("gy", 1), ("gz", 2)), 1)
-    kernel = conv_weight.reshape(3, 3, 3, channels, channels).transpose(0, 1, 2, 4, 3)
-    total = lax.conv_general_dilated(
-        padded[None],
-        kernel,
-        (1, 1, 1),
-        "VALID",
-        dimension_numbers=("NDHWC", "DHWIO", "NDHWC"),
-        preferred_element_type=jnp.float32,
-    )[0].reshape(volume, channels)
+    cells = features.transpose(1, 2, 3, 0).reshape(extent_x, extent_y, extent_z * channels)
+    padded = extended(cells, (("gx", 0), ("gy", 1)), 1)
+    count_z = lax.axis_size("gz")
+    low = lax.ppermute(
+        padded[:, :, -channels:], "gz", [(i, i + 1) for i in range(count_z - 1)]
+    )
+    high = lax.ppermute(
+        padded[:, :, :channels], "gz", [(i + 1, i) for i in range(count_z - 1)]
+    )
+    total = conv_lane_dense(padded, low, high, conv_weight, channels).reshape(volume, channels)
     fields = jnp.maximum(total + conv_bias[None, :], 0.0).astype(jnp.bfloat16)
     pair_count = pair_edge.shape[0]
     slot_count = pair_count * BINS

time: 94.1 us -> 105 us (1.12)
  local copies, waits for them, and re-layouts: 16.3 us -> 23.8 us
  matrix products: 6.9 us -> 13 us
  waiting for transfers between devices: 21.8 us -> 17.9 us
  starting transfers between devices: 28 us -> 30.6 us
  other arithmetic: 5.94 us -> 4.25 us
    convert_element_type x0 -> x2, local copies, waits for them, and re-layouts: none -> 11.5 us  [banded_weight(): return full.reshape(27 * 4 * channels, 4 * channels).astype(jnp.bfloat16)]
    dot_general x0 -> x2, matrix products: none -> 8.83 us  [the longest x1 6.84 us: banded_weight(): jnp.einsum('pizd,xydco->xypiczo', band_selector(), taps, precision=lax.Pr...]
    ppermute x3 -> x2, waiting for transfers between devices: 8.58 us -> 0.01 us  [extended(): lax.ppermute(head, axis, [((i + 1) % count, i) for i in range(ends)])]
    ppermute x0 -> x2, starting transfers between devices: none -> 7.4 us  [the longest x1 5.48 us: body(): lax.ppermute(padded[:, :, -channels:], 'gz', [(i, i + 1) for i in range(c...]
    unnamed x27 -> x41, local copies, waits for them, and re-layouts: 7.44 us -> 1.61 us
    ppermute x3 -> x2, starting transfers between devices: 10.7 us -> 5.23 us  [extended(): lax.ppermute(tail, axis, [(i, (i + 1) % count) for i in range(ends)])]
    ppermute x0 -> x2, waiting for transfers between devices: none -> 4.71 us  [the longest x1 4.7 us: body(): lax.ppermute(padded[:, :, :channels], 'gz', [(i + 1, i) for i in range(co...]
    conv_general_dilated x1 -> x0, matrix products: 3.35 us -> none  [body(): lax.conv_general_dilated(padded[None], kernel, (1, 1, 1), 'VALID', dimens...]
  transfers between devices with their start and end apart: 7 -> 7, of which waited for: 4 -> 2; matrix products, arithmetic and copies ran while one was open for 5% -> 23% of each run, Pallas kernels for 0% -> 0%
where the time goes in v5:
time: 105 us; the launch traced here: 104 us
  starting transfers between devices  30.6 us (29%)
  local copies, waits for them, and re-layouts  23.8 us (23%)
  waiting for transfers between devices  17.9 us (17%)
  blocking collectives  14.2 us (14%)
  matrix products  13 us (12%)
  other arithmetic  4.25 us (4%)
    all_to_all x1, starting transfers between devices, body(): lax.all_to_all(send, ('gx', 'gy'), split_axis=0, concat_axis=0, tiled=True)  15.4 us
    all_to_all x1, blocking collectives, body(): lax.all_to_all(owner_scores.reshape(groups, capacity), ('gx', 'gy'), spli...  14.2 us
    all_to_all x1, waiting for transfers between devices, body(): lax.all_to_all(send, ('gx', 'gy'), split_axis=0, concat_axis=0, tiled=True)  13.2 us
    convert_element_type x2, local copies, waits for them, and re-layouts, banded_weight(): return full.reshape(27 * 4 * channels, 4 * channels).astype(jnp.bfloat16)  11.5 us
    dot_general x1, matrix products, banded_weight(): jnp.einsum('pizd,xydco->xypiczo', band_selector(), taps, precision=lax.Pr...  6.84 us
    ppermute x1, starting transfers between devices, body(): lax.ppermute(padded[:, :, -channels:], 'gz', [(i, i + 1) for i in range(c...  5.48 us
    ppermute x2, starting transfers between devices, extended(): lax.ppermute(tail, axis, [(i, (i + 1) % count) for i in range(ends)])  5.23 us
    ppermute x1, waiting for transfers between devices, body(): lax.ppermute(padded[:, :, :channels], 'gz', [(i + 1, i) for i in range(co...  4.7 us
  transfers between devices with their start and end apart: 7, of which 2 were waited for; matrix products, arithmetic and copies ran while one was open for 23% of the time, Pallas kernels for 0%

profile of v5, /device:TPU:192, one launch (start us, length us, event | category | flops | bytes accessed | tf_op | source)
XLA Modules:
  0.0 104.4 jit_solution(1473938096690627714)
XLA Ops:
  0.0 1.1 %fusion.46 = (bf16[1,16,128,32]{2,1,0,3:T(8,128)(2,1)S(1)}, bf16[1,16,128,32]{2,1,0,3:T(8,128)(2,1)S(1)}) fusion(bf16[2,16,128,32]{2,1,0,3:T(8,128)(2,1)} %bitcast.61), kind=kLoop, calls=%fused_computation.111 | loop fusion | bytes 524288 | tf_op jit(solution)/shard_map/slice | solution.py:15
  1.1 0.3 copy.88
  1.4 0.5 slice.130
  1.9 1.7 %collective-permute-start = (bf16[1,16,4096]{2,1,0:T(8,128)(2,1)S(1)}, bf16[1,16,4096]{2,1,0:T(8,128)(2,1)S(1)}, u32[]{:S(2)}, u32[]{:S(2)}) collective-permute-start(bf16[1,16,4096]{2,1,0:T(8,128)(2,1)S(1)} %slice.130), channel_id=1, source_target_pairs={{0,64},{64,128},{128,192},{192,256},{256,320},{320,384},{384,448},... | collective-permute-start | bytes 393224 | tf_op jit(solution)/shard_map/ppermute | solution.py:19
  3.7 0.3 copy.90
  4.0 0.5 slice.132
  4.5 1.3 %collective-permute-start.1 = (bf16[1,16,4096]{2,1,0:T(8,128)(2,1)S(1)}, bf16[1,16,4096]{2,1,0:T(8,128)(2,1)S(1)}, u32[]{:S(2)}, u32[]{:S(2)}) collective-permute-start(bf16[1,16,4096]{2,1,0:T(8,128)(2,1)S(1)} %slice.132), channel_id=1, source_target_pairs={{64,0},{128,64},{192,128},{256,192},{320,256},{384,320},{448,384},... | collective-permute-start | bytes 393224 | tf_op jit(solution)/shard_map/ppermute | solution.py:21
  5.8 1.1 %copy.107 = bf16[3,3,3,32,32]{3,2,4,1,0:T(4,128)(2,1)S(1)} copy(bf16[3,3,3,32,32]{4,3,2,1,0:T(8,128)(2,1)} %bitcast.64) | data formatting | bytes 110592 | tf_op jit(solution)/shard_map/reshape | solution.py:40
  7.0 6.8 %fusion.2 = bf16[3,3,3,4,32,4,32]{6,5,4,1,0,3,2:T(4,128)(2,1)} fusion(f32[3,4,4,3,1,1,1]{3,2,6,5,4,1,0:T(4,128)} %constant.38, bf16[3,3,3,32,32]{3,2,4,1,0:T(4,128)(2,1)S(1)} %copy.107), kind=kOutput, calls=%fused_computation.6 | convolution fusion | flops 16367616 | bytes 940608 | tf_op jit(solution)/shard_map/pizd,xydco->xypiczo/dot_general | solution.py:41
  13.8 0.1 fusion.34
  13.9 0.5 copy.89
  14.5 1.1 %reshape.54 = bf16[2,16,4096]{2,1,0:T(8,128)(2,1)S(1)} reshape(bf16[2,16,128,32]{3,2,1,0:T(8,128)(2,1)S(1)} %copy.89) | data formatting | bytes 524288 | tf_op jit(solution)/shard_map/reshape | solution.py:77
  15.6 0.2 reduce_window_sum.11
  15.7 0.2 select_reduce_fusion.2
  16.0 0.1 fusion.45
  16.1 3.5 %collective-permute-start.2 = (bf16[4,1,4096]{2,1,0:T(2,128)(2,1)S(1)}, bf16[4,1,4096]{2,1,0:T(2,128)(2,1)S(1)}, u32[]{:S(2)}, u32[]{:S(2)}) collective-permute-start(bf16[4,1,4096]{2,1,0:T(2,128)(2,1)S(1)} %get-tuple-element.7), channel_id=1, source_target_pairs={{0,8},{8,16},{16,24},{24,32},{32,40},{40,48},{48,56},{1,9},{9,17},... | collective-permute-start | bytes 98312 | tf_op jit(solution)/shard_map/ppermute | solution.py:19
  19.6 1.3 %collective-permute-start.3 = (bf16[4,1,4096]{2,1,0:T(2,128)(2,1)S(1)}, bf16[4,1,4096]{2,1,0:T(2,128)(2,1)S(1)}, u32[]{:S(2)}, u32[]{:S(2)}) collective-permute-start(bf16[4,1,4096]{2,1,0:T(2,128)(2,1)S(1)} %get-tuple-element.8), channel_id=1, source_target_pairs={{8,0},{16,8},{24,16},{32,24},{40,32},{48,40},{56,48},{9,1},{17,9},... | collective-permute-start | bytes 98312 | tf_op jit(solution)/shard_map/ppermute | solution.py:21
  20.9 6.9 %copy.108 = bf16[3,3,3,4,32,4,32]{6,5,4,3,2,1,0:T(4,128)(2,1)} copy(bf16[3,3,3,4,32,4,32]{6,5,4,1,0,3,2:T(4,128)(2,1)} %fusion.2) | data formatting | bytes 1769472 | tf_op jit(solution)/shard_map/convert_element_type | solution.py:42
  27.8 4.6 %reshape.80 = bf16[3456,128,1,1]{1,0,2,3:T(8,128)(2,1)S(1)} reshape(bf16[3,3,3,4,32,4,32]{6,5,4,3,2,1,0:T(4,128)(2,1)} %copy.108) | data formatting | bytes 1769472 | tf_op jit(solution)/shard_map/convert_element_type | solution.py:42
  32.4 1.5 %scatter_custom_fusion.1 = bf16[320]{0:T(512)(128)(2,1)S(1)} fusion(s32[128]{0:T(128)S(1)} %get-tuple-element.12, bf16[128]{0:T(256)(128)(2,1)S(1)} %convert_element_type.71, bf16[]{:T(256)} %constant.25.clone.1), kind=kCustom, calls=%fused_computation.104 | custom fusion | bytes 642 | tf_op jit(solution)/shard_map/scatter | solution.py:112
  33.9 0.1 reshape.85
  34.1 0.3 pad_maximum_fusion
  34.4 0.3 reshape.83
  34.8 0.1 fusion.44
  34.8 5.5 %collective-permute-start.4 = (bf16[4,18,32]{2,1,0:T(8,128)(2,1)S(1)}, bf16[4,18,32]{2,1,0:T(8,128)(2,1)S(1)}, u32[]{:S(2)}, u32[]{:S(2)}) collective-permute-start(bf16[4,18,32]{2,1,0:T(8,128)(2,1)S(1)} %get-tuple-element.6), channel_id=1, source_target_pairs={{0,1},{1,2},{2,3},{3,4},{4,5},{5,6},{6,7},{8,9},{9,10},{10,11},{11... | collective-permute-start | bytes 13832 | tf_op jit(solution)/shard_map/ppermute | solution.py:80
  40.4 1.9 %collective-permute-start.5 = (bf16[4,18,32]{2,1,0:T(8,128)(2,1)S(1)}, bf16[4,18,32]{2,1,0:T(8,128)(2,1)S(1)}, u32[]{:S(2)}, u32[]{:S(2)}) collective-permute-start(bf16[4,18,32]{2,1,0:T(8,128)(2,1)S(1)} %get-tuple-element.5), channel_id=1, source_target_pairs={{1,0},{2,1},{3,2},{4,3},{5,4},{6,5},{7,6},{9,8},{10,9},{11,10},{12... | collective-permute-start | bytes 13832 | tf_op jit(solution)/shard_map/ppermute | solution.py:83
  42.4 0.1 fusion.16
  42.6 4.7 %collective-permute-done.5 = bf16[4,18,32]{2,1,0:T(8,128)(2,1)S(1)} collective-permute-done((bf16[4,18,32]{2,1,0:T(8,128)(2,1)S(1)}, bf16[4,18,32]{2,1,0:T(8,128)(2,1)S(1)}, u32[]{:S(2)}, u32[]{:S(2)}) %collective-permute-start.5) | collective-permute-done | bytes 4640 | tf_op jit(solution)/shard_map/ppermute | solution.py:83
  47.4 0.1 slice_dynamic-update-slice_fusion.16
  47.5 0.1 fusion.18
  47.7 0.1 slice_dynamic-update-slice_fusion.14
  47.8 0.1 fusion.20
  48.0 0.1 slice_dynamic-update-slice_fusion.12
  48.1 0.1 fusion.22
  48.3 0.1 slice_dynamic-update-slice_fusion.10
  48.5 0.1 fusion.24
  48.7 0.1 slice_dynamic-update-slice_fusion.8
  48.8 0.1 fusion.26
  49.0 0.1 slice_dynamic-update-slice_fusion.6
  49.1 0.1 fusion.28
  49.3 0.1 slice_dynamic-update-slice_fusion.4
  49.4 0.1 fusion.14
  49.6 0.1 slice_dynamic-update-slice_fusion.2
  49.7 0.1 fusion.29
  49.9 0.1 slice_dynamic-update-slice_fusion
  50.1 2.0 %fusion.8 = f32[2,16,32,128]{3,2,1,0:T(8,128)S(1)} fusion(bf16[2,16,32,3456]{3,2,1,0:T(8,128)(2,1)S(1)} %slice_dynamic-update-slice_fusion, bf16[3456,128,1,1]{1,0,2,3:T(8,128)(2,1)S(1)} %reshape.80), kind=kOutput, calls=%fused_computation.25 | convolution fusion | flops 905969664 | bytes 8486912 | tf_op jit(solution)/shard_map/dot_general | solution.py:59
  52.1 0.5 reshape.57
  52.6 3.4 %fusion.5 = bf16[4,8,8,128]{3,2,1,0:T(8,128)(2,1)S(1)} fusion(s32[4096]{0:T(1024)S(1)} %bitcast.68, f32[4096,32]{1,0:T(8,128)S(1)} %reshape.57, f32[32]{0:T(128)S(1)} %copy-done.9), kind=kOutput, calls=%fused_computation.20 | convolution fusion | flops 273088512 | bytes 606336 | tf_op jit(solution)/shard_map/dot_general | solution.py:92
  56.1 0.1 copy.110
  56.2 1.1 %scatter_custom_fusion = bf16[320,256]{1,0:T(8,128)(2,1)S(1)} fusion(s32[128]{0:T(128)S(1)} %get-tuple-element.12, bf16[128,256]{1,0:T(8,128)(2,1)S(1)} %copy.110, bf16[]{:T(256)} %constant.7.clone.1), kind=kCustom, calls=%fused_computation.83 | custom fusion | bytes 163842 | tf_op jit(solution)/shard_map/scatter | solution.py:111
  57.4 0.8 fusion.12
  58.2 15.4 %all-to-all-start = ((bf16[64,6,256]{2,1,0:T(8,128)(2,1)}), bf16[64,6,256]{2,1,0:T(8,128)(2,1)S(1)}, u32[]{:S(2)}, u32[]{:S(2)}) async-start(bf16[64,6,256]{2,1,0:T(8,128)(2,1)} %fusion.12), calls=%async_computation | async-start | bytes 524288 | tf_op jit(solution)/shard_map/all_to_all | solution.py:118
  73.6 13.2 %all-to-all-done = bf16[64,6,256]{2,1,0:T(8,128)(2,1)S(1)} async-done(((bf16[64,6,256]{2,1,0:T(8,128)(2,1)}), bf16[64,6,256]{2,1,0:T(8,128)(2,1)S(1)}, u32[]{:S(2)}, u32[]{:S(2)}) %all-to-all-start) | async-done | bytes 196640 | tf_op jit(solution)/shard_map/all_to_all | solution.py:118
  86.9 0.1 fusion.37
  87.0 0.1 reshape.61
  87.2 0.3 multiply_convert_fusion.1
  87.5 0.4 convolution_bitcast_fusion
  87.9 0.1 select_reduce_fusion.1
  88.0 0.1 all_to_all.10
  88.1 14.2 %all_to_all.14 = f32[64,1,5]{2,1,0:T(1,128)S(1)} all-to-all(f32[64,1,5]{2,1,0:T(1,128)S(1)} %bitcast.65), channel_id=1, replica_groups=mesh['gx'=8,'gy'=8,'gz'=8] {'gx','gy'}, dimensions={0} | all-to-all | bytes 2560 | tf_op jit(solution)/shard_map/all_to_all | solution.py:136
  102.4 0.5 broadcast.42
  102.9 0.7 reduce.7
  103.6 0.1 broadcast_in_dim.58
  103.8 0.6 select_reduce_fusion
  (48 shorter events, 1.1 us)
Async XLA Ops:
  0.0 87.5 %copy-start = (bf16[512,512]{1,0:T(8,128)(2,1)S(1)}, bf16[512,512]{1,0:T(8,128)(2,1)}, u32[]{:S(2)}) copy-start(bf16[512,512]{1,0:T(8,128)(2,1)} %param.20) | copy-start | bytes 1572868
  0.0 13.9 %copy-start.1 = (bf16[32,2,16,128]{3,2,1,0:T(8,128)(2,1)S(1)}, bf16[32,2,16,128]{3,2,1,0:T(8,128)(2,1)}, u32[]{:S(2)}) copy-start(bf16[32,2,16,128]{3,2,1,0:T(8,128)(2,1)} %param.12) | copy-start | bytes 786436
  0.0 13.8 %copy-start.2 = (s32[128,1]{0,1:T(1,128)S(1)}, s32[128,1]{0,1:T(1,128)}, u32[]{:S(2)}) copy-start(s32[128,1]{0,1:T(1,128)} %param.16) | copy-start | bytes 1540
  1.9 14.0 %collective-permute-start = (bf16[1,16,4096]{2,1,0:T(8,128)(2,1)S(1)}, bf16[1,16,4096]{2,1,0:T(8,128)(2,1)S(1)}, u32[]{:S(2)}, u32[]{:S(2)}) collective-permute-start(bf16[1,16,4096]{2,1,0:T(8,128)(2,1)S(1)} %slice.130), channel_id=1, source_target_pairs={{0,64},{64,128},{128,192},{192,256},{256,320},{320,384},{384,448},... | collective-permute-start | bytes 393224 | tf_op jit(solution)/shard_map/ppermute | solution.py:19
  4.5 11.4 %collective-permute-start.1 = (bf16[1,16,4096]{2,1,0:T(8,128)(2,1)S(1)}, bf16[1,16,4096]{2,1,0:T(8,128)(2,1)S(1)}, u32[]{:S(2)}, u32[]{:S(2)}) collective-permute-start(bf16[1,16,4096]{2,1,0:T(8,128)(2,1)S(1)} %slice.132), channel_id=1, source_target_pairs={{64,0},{128,64},{192,128},{256,192},{320,256},{384,320},{448,384},... | collective-permute-start | bytes 393224 | tf_op jit(solution)/shard_map/ppermute | solution.py:21
  14.4 17.9 %copy-start.8 = (s32[128]{0:T(128)S(1)}, s32[128]{0:T(128)}, u32[]{:S(2)}) copy-start(s32[128]{0:T(128)} %param.17) | copy-start | bytes 1540
  16.1 18.0 %collective-permute-start.2 = (bf16[4,1,4096]{2,1,0:T(2,128)(2,1)S(1)}, bf16[4,1,4096]{2,1,0:T(2,128)(2,1)S(1)}, u32[]{:S(2)}, u32[]{:S(2)}) collective-permute-start(bf16[4,1,4096]{2,1,0:T(2,128)(2,1)S(1)} %get-tuple-element.7), channel_id=1, source_target_pairs={{0,8},{8,16},{16,24},{24,32},{32,40},{40,48},{48,56},{1,9},{9,17},... | collective-permute-start | bytes 98312 | tf_op jit(solution)/shard_map/ppermute | solution.py:19
  19.6 14.5 %collective-permute-start.3 = (bf16[4,1,4096]{2,1,0:T(2,128)(2,1)S(1)}, bf16[4,1,4096]{2,1,0:T(2,128)(2,1)S(1)}, u32[]{:S(2)}, u32[]{:S(2)}) collective-permute-start(bf16[4,1,4096]{2,1,0:T(2,128)(2,1)S(1)} %get-tuple-element.8), channel_id=1, source_target_pairs={{8,0},{16,8},{24,16},{32,24},{40,32},{48,40},{56,48},{9,1},{17,9},... | collective-permute-start | bytes 98312 | tf_op jit(solution)/shard_map/ppermute | solution.py:21
  34.8 7.5 %collective-permute-start.4 = (bf16[4,18,32]{2,1,0:T(8,128)(2,1)S(1)}, bf16[4,18,32]{2,1,0:T(8,128)(2,1)S(1)}, u32[]{:S(2)}, u32[]{:S(2)}) collective-permute-start(bf16[4,18,32]{2,1,0:T(8,128)(2,1)S(1)} %get-tuple-element.6), channel_id=1, source_target_pairs={{0,1},{1,2},{2,3},{3,4},{4,5},{5,6},{6,7},{8,9},{9,10},{10,11},{11... | collective-permute-start | bytes 13832 | tf_op jit(solution)/shard_map/ppermute | solution.py:80
  40.4 6.9 %collective-permute-start.5 = (bf16[4,18,32]{2,1,0:T(8,128)(2,1)S(1)}, bf16[4,18,32]{2,1,0:T(8,128)(2,1)S(1)}, u32[]{:S(2)}, u32[]{:S(2)}) collective-permute-start(bf16[4,18,32]{2,1,0:T(8,128)(2,1)S(1)} %get-tuple-element.5), channel_id=1, source_target_pairs={{1,0},{2,1},{3,2},{4,3},{5,4},{6,5},{7,6},{9,8},{10,9},{11,10},{12... | collective-permute-start | bytes 13832 | tf_op jit(solution)/shard_map/ppermute | solution.py:83
  50.1 2.5 %copy-start.5 = (s32[2,16,128]{2,1,0:T(8,128)S(1)}, s32[2,16,128]{2,1,0:T(8,128)}, u32[]{:S(2)}) copy-start(s32[2,16,128]{2,1,0:T(8,128)} %param.13) | copy-start | bytes 49156
  50.1 2.5 %copy-start.9 = (f32[32]{0:T(128)S(1)}, f32[32]{0:T(128)}, u32[]{:S(2)}) copy-start(f32[32]{0:T(128)} %param.15) | copy-start | bytes 388
  52.1 21.5 %copy-start.3 = (bf16[512]{0:T(512)(128)(2,1)S(1)}, bf16[512]{0:T(512)(128)(2,1)}, u32[]{:S(2)}) copy-start(bf16[512]{0:T(512)(128)(2,1)} %param.22) | copy-start | bytes 3076
  52.1 35.1 %copy-start.6 = (f32[512]{0:T(512)S(1)}, f32[512]{0:T(512)}, u32[]{:S(2)}) copy-start(f32[512]{0:T(512)} %param.19) | copy-start | bytes 6148
  52.6 34.6 %copy-start.4 = (bf16[256,512]{1,0:T(8,128)(2,1)S(1)}, bf16[256,512]{1,0:T(8,128)(2,1)}, u32[]{:S(2)}) copy-start(bf16[256,512]{1,0:T(8,128)(2,1)} %param.18) | copy-start | bytes 786436
  52.6 34.9 %copy-start.7 = (f32[512]{0:T(512)S(1)}, f32[512]{0:T(512)}, u32[]{:S(2)}) copy-start(f32[512]{0:T(512)} %param.21) | copy-start | bytes 6148
  58.2 28.6 %all-to-all-start = ((bf16[64,6,256]{2,1,0:T(8,128)(2,1)}), bf16[64,6,256]{2,1,0:T(8,128)(2,1)S(1)}, u32[]{:S(2)}, u32[]{:S(2)}) async-start(bf16[64,6,256]{2,1,0:T(8,128)(2,1)} %fusion.12), calls=%async_computation | async-start | bytes 524288 | tf_op jit(solution)/shard_map/all_to_all | solution.py:118

commit v6 on v5

--- a/solution.py
+++ b/solution.py
@@ -42,22 +42,23 @@
     return full.reshape(27 * 4 * channels, 4 * channels).astype(jnp.bfloat16)
 
 
-def conv_lane_dense(padded_xy, low, high, conv_weight, channels):
-    px, py, lanes = padded_xy.shape
-    chunk = 4 * channels
-    nchunk = lanes // chunk
+def conv_lane_dense(padded, low, high, conv_weight, channels):
+    px, py, nchunk, chunk = padded.shape
     low_chunk = jnp.pad(low, ((0, 0), (0, 0), (chunk - channels, 0)))[:, :, None]
     high_chunk = jnp.pad(high, ((0, 0), (0, 0), (0, chunk - channels)))[:, :, None]
-    full = jnp.concatenate([low_chunk, padded_xy.reshape(px, py, nchunk, chunk), high_chunk], axis=2)
+    parts = (
+        jnp.concatenate([low_chunk, padded[:, :, :-1]], axis=2),
+        padded,
+        jnp.concatenate([padded[:, :, 1:], high_chunk], axis=2),
+    )
     slabs = [
-        full[dx : dx + px - 2, dy : dy + py - 2, p : p + nchunk, :]
+        parts[p][dx : dx + px - 2, dy : dy + py - 2]
         for dx in range(3)
         for dy in range(3)
         for p in range(3)
     ]
     stacked = jnp.concatenate(slabs, axis=3)
     return jnp.dot(stacked, banded_weight(conv_weight, channels), preferred_element_type=jnp.float32)
-
 
 def body(
     features,
@@ -74,15 +75,18 @@
 ):
     channels, extent_x, extent_y, extent_z = features.shape
     volume = extent_x * extent_y * extent_z
-    cells = features.transpose(1, 2, 3, 0).reshape(extent_x, extent_y, extent_z * channels)
+    chunk = 4 * channels
+    cells = (
+        features.reshape(channels, extent_x, extent_y, extent_z // 4, 4)
+        .transpose(1, 2, 3, 4, 0)
+        .reshape(extent_x, extent_y, extent_z // 4, chunk)
+    )
     padded = extended(cells, (("gx", 0), ("gy", 1)), 1)
     count_z = lax.axis_size("gz")
     low = lax.ppermute(
-        padded[:, :, -channels:], "gz", [(i, i + 1) for i in range(count_z - 1)]
+        padded[:, :, -1, chunk - channels :], "gz", [(i, i + 1) for i in range(count_z - 1)]
     )
-    high = lax.ppermute(
-        padded[:, :, :channels], "gz", [(i + 1, i) for i in range(count_z - 1)]
-    )
+    high = lax.ppermute(padded[:, :, 0, :channels], "gz", [(i + 1, i) for i in range(count_z - 1)])
     total = conv_lane_dense(padded, low, high, conv_weight, channels).reshape(volume, channels)
     fields = jnp.maximum(total + conv_bias[None, :], 0.0).astype(jnp.bfloat16)
     pair_count = pair_edge.shape[0]

time: 105 us -> 104 us (level)
  local copies, waits for them, and re-layouts: 23.8 us -> 21.9 us
  other arithmetic: 4.25 us -> 5.6 us
    unnamed x9 -> x25, other arithmetic: 1.11 us -> 2.47 us
    slice x3, local copies, waits for them, and re-layouts: 1.91 us -> 0.72 us  [extended(): head = lax.slice_in_dim(cells, 0, width, axis=dim)]
    unnamed x41 -> x25, local copies, waits for them, and re-layouts: 1.61 us -> 2.28 us
  transfers between devices with their start and end apart: 7 -> 7, of which waited for: 2 -> 2; matrix products, arithmetic and copies ran while one was open for 23% -> 22% of each run, Pallas kernels for 0% -> 0%
where the time goes in v6:
time: 104 us; the launch traced here: 103 us
  starting transfers between devices  30.8 us (30%)
  local copies, waits for them, and re-layouts  21.9 us (21%)
  waiting for transfers between devices  18 us (17%)
  blocking collectives  14.2 us (14%)
  matrix products  12.2 us (12%)
  other arithmetic  5.6 us (5%)
    all_to_all x1, starting transfers between devices, body(): lax.all_to_all(send, ('gx', 'gy'), split_axis=0, concat_axis=0, tiled=True)  15.4 us
    all_to_all x1, blocking collectives, body(): lax.all_to_all(owner_scores.reshape(groups, capacity), ('gx', 'gy'), spli...  14.2 us
    all_to_all x1, waiting for transfers between devices, body(): lax.all_to_all(send, ('gx', 'gy'), split_axis=0, concat_axis=0, tiled=True)  13.2 us
    convert_element_type x2, local copies, waits for them, and re-layouts, banded_weight(): return full.reshape(27 * 4 * channels, 4 * channels).astype(jnp.bfloat16)  11.5 us
    dot_general x1, matrix products, banded_weight(): jnp.einsum('pizd,xydco->xypiczo', band_selector(), taps, precision=lax.Pr...  6.1 us
    ppermute x1, starting transfers between devices, body(): lax.ppermute(padded[:, :, -1, chunk - channels:], 'gz', [(i, i + 1) for i...  5.68 us
    ppermute x2, starting transfers between devices, extended(): lax.ppermute(tail, axis, [(i, (i + 1) % count) for i in range(ends)])  5.23 us
    ppermute x1, waiting for transfers between devices, body(): lax.ppermute(padded[:, :, 0, :channels], 'gz', [(i + 1, i) for i in range...  4.8 us
  transfers between devices with their start and end apart: 7, of which 2 were waited for; matrix products, arithmetic and copies ran while one was open for 22% of the time, Pallas kernels for 0%

profile of v6, /device:TPU:192, one launch (start us, length us, event | category | flops | bytes accessed | tf_op | source)
XLA Modules:
  0.0 103.4 jit_solution(11100984683880231532)
XLA Ops:
  0.0 2.1 %copy.86 = bf16[32,2,16,128]{0,2,3,1:T(8,128)(2,1)S(1)} copy(bf16[32,2,16,128]{3,2,1,0:T(8,128)(2,1)} %param.12) | data formatting | bytes 524288 | tf_op args[0]
  2.1 0.2 fusion.73
  2.3 0.2 copy.87
  2.6 0.3 slice.123
  2.9 1.7 %collective-permute-start = (bf16[1,16,32,128]{3,2,1,0:T(8,128)(2,1)S(1)}, bf16[1,16,32,128]{3,2,1,0:T(8,128)(2,1)S(1)}, u32[]{:S(2)}, u32[]{:S(2)}) collective-permute-start(bf16[1,16,32,128]{3,2,1,0:T(8,128)(2,1)S(1)} %slice.123), channel_id=1, source_target_pairs={{0,64},{64,128},{128,192},{192,256},{256,320},{320,384},{384,448},... | collective-permute-start | bytes 393224 | tf_op jit(solution)/shard_map/ppermute | solution.py:19
  4.6 0.2 copy.89
  4.9 0.3 slice.125
  5.2 1.3 %collective-permute-start.1 = (bf16[1,16,32,128]{3,2,1,0:T(8,128)(2,1)S(1)}, bf16[1,16,32,128]{3,2,1,0:T(8,128)(2,1)S(1)}, u32[]{:S(2)}, u32[]{:S(2)}) collective-permute-start(bf16[1,16,32,128]{3,2,1,0:T(8,128)(2,1)S(1)} %slice.125), channel_id=1, source_target_pairs={{64,0},{128,64},{192,128},{256,192},{320,256},{384,320},{448,384},... | collective-permute-start | bytes 393224 | tf_op jit(solution)/shard_map/ppermute | solution.py:21
  6.5 1.1 %copy.94 = bf16[3,3,3,32,32]{3,2,4,1,0:T(4,128)(2,1)S(1)} copy(bf16[3,3,3,32,32]{4,3,2,1,0:T(8,128)(2,1)} %bitcast.66) | data formatting | bytes 110592 | tf_op jit(solution)/shard_map/reshape | solution.py:40
  7.6 6.1 %fusion.2 = bf16[3,3,3,4,32,4,32]{6,5,4,1,0,3,2:T(4,128)(2,1)} fusion(f32[3,4,4,3,1,1,1]{3,2,6,5,4,1,0:T(4,128)S(1)} %copy-done.1, bf16[3,3,3,32,32]{3,2,4,1,0:T(4,128)(2,1)S(1)} %copy.94), kind=kOutput, calls=%fused_computation.6 | convolution fusion | flops 16367616 | bytes 940608 | tf_op jit(solution)/shard_map/pizd,xydco->xypiczo/dot_general | solution.py:41
  13.7 0.1 fusion.63
  13.8 0.6 copy.88
  14.4 0.5 reshape.55
  14.9 0.2 reduce_window_sum.11
  15.1 0.2 select_reduce_fusion.2
  15.4 3.5 %collective-permute-start.2 = (bf16[4,1,32,128]{3,2,1,0:T(8,128)(2,1)S(1)}, bf16[4,1,32,128]{3,2,1,0:T(8,128)(2,1)S(1)}, u32[]{:S(2)}, u32[]{:S(2)}) collective-permute-start(bf16[4,1,32,128]{3,2,1,0:T(8,128)(2,1)S(1)} %get-tuple-element.11), channel_id=1, source_target_pairs={{0,8},{8,16},{16,24},{24,32},{32,40},{40,48},{48,56},{1,9},{9,17},... | collective-permute-start | bytes 98312 | tf_op jit(solution)/shard_map/ppermute | solution.py:19
  18.8 1.3 %collective-permute-start.3 = (bf16[4,1,32,128]{3,2,1,0:T(8,128)(2,1)S(1)}, bf16[4,1,32,128]{3,2,1,0:T(8,128)(2,1)S(1)}, u32[]{:S(2)}, u32[]{:S(2)}) collective-permute-start(bf16[4,1,32,128]{3,2,1,0:T(8,128)(2,1)S(1)} %get-tuple-element.12), channel_id=1, source_target_pairs={{8,0},{16,8},{24,16},{32,24},{40,32},{48,40},{56,48},{9,1},{17,9},... | collective-permute-start | bytes 98312 | tf_op jit(solution)/shard_map/ppermute | solution.py:21
  20.2 6.9 %copy.95 = bf16[3,3,3,4,32,4,32]{6,5,4,3,2,1,0:T(4,128)(2,1)} copy(bf16[3,3,3,4,32,4,32]{6,5,4,1,0,3,2:T(4,128)(2,1)} %fusion.2) | data formatting | bytes 1769472 | tf_op jit(solution)/shard_map/convert_element_type | solution.py:42
  27.0 4.6 %reshape.80 = bf16[3456,128,1,1]{1,0,2,3:T(8,128)(2,1)S(1)} reshape(bf16[3,3,3,4,32,4,32]{6,5,4,3,2,1,0:T(4,128)(2,1)} %copy.95) | data formatting | bytes 1769472 | tf_op jit(solution)/shard_map/convert_element_type | solution.py:42
  31.7 1.3 %scatter_custom_fusion.1 = bf16[320]{0:T(512)(128)(2,1)S(1)} fusion(s32[128]{0:T(128)S(1)} %get-tuple-element.14, bf16[128]{0:T(256)(128)(2,1)S(1)} %convert_element_type.71, bf16[]{:T(256)} %constant.25.clone.1), kind=kCustom, calls=%fused_computation.131 | custom fusion | bytes 642 | tf_op jit(solution)/shard_map/scatter | solution.py:116
  33.0 0.1 reshape.84
  33.2 0.1 pad_maximum_fusion.7
  33.3 5.7 %collective-permute-start.4 = (bf16[4,18,32]{2,0,1:T(4,128)(2,1)S(1)}, bf16[4,18,32]{2,0,1:T(4,128)(2,1)S(1)}, u32[]{:S(2)}, u32[]{:S(2)}) collective-permute-start(bf16[4,18,32]{2,0,1:T(4,128)(2,1)S(1)} %bitcast.68), channel_id=1, source_target_pairs={{0,1},{1,2},{2,3},{3,4},{4,5},{5,6},{6,7},{8,9},{9,10},{10,11},{11... | collective-permute-start | bytes 13832 | tf_op jit(solution)/shard_map/ppermute | solution.py:86
  39.1 0.3 fusion.74
  39.4 1.9 %collective-permute-start.5 = (bf16[4,18,32]{2,0,1:T(4,128)(2,1)S(1)}, bf16[4,18,32]{2,0,1:T(4,128)(2,1)S(1)}, u32[]{:S(2)}, u32[]{:S(2)}) collective-permute-start(bf16[4,18,32]{2,0,1:T(4,128)(2,1)S(1)} %bitcast.69), channel_id=1, source_target_pairs={{1,0},{2,1},{3,2},{4,3},{5,4},{6,5},{7,6},{9,8},{10,9},{11,10},{12... | collective-permute-start | bytes 13832 | tf_op jit(solution)/shard_map/ppermute | solution.py:89
  41.3 0.1 pad_bitcast_fusion.1
  41.5 4.8 %collective-permute-done.5 = bf16[4,18,32]{2,0,1:T(4,128)(2,1)S(1)} collective-permute-done((bf16[4,18,32]{2,0,1:T(4,128)(2,1)S(1)}, bf16[4,18,32]{2,0,1:T(4,128)(2,1)S(1)}, u32[]{:S(2)}, u32[]{:S(2)}) %collective-permute-start.5) | collective-permute-done | bytes 4640 | tf_op jit(solution)/shard_map/ppermute | solution.py:89
  46.3 0.1 fusion.40
  46.5 0.1 fusion.24
  46.6 0.1 fusion.42
  46.8 0.1 fusion.26
  46.9 0.1 fusion.44
  47.1 0.1 fusion.28
  47.2 0.1 fusion.46
  47.4 0.1 fusion.30
  47.5 0.1 fusion.48
  47.7 0.1 fusion.32
  47.8 0.1 fusion.50
  48.0 0.1 fusion.34
  48.1 0.1 fusion.52
  48.3 0.1 fusion.36
  48.5 0.1 fusion.38
  48.7 0.1 fusion.22
  48.8 0.1 fusion.55
  49.0 0.1 fusion.53
  49.1 2.0 %fusion.8 = f32[2,16,32,128]{3,2,1,0:T(8,128)S(1)} fusion(bf16[2,16,32,3456]{3,2,1,0:T(8,128)(2,1)S(1)} %fusion.53, bf16[3456,128,1,1]{1,0,2,3:T(8,128)(2,1)S(1)} %reshape.80), kind=kOutput, calls=%fused_computation.33 | convolution fusion | flops 905969664 | bytes 8486912 | tf_op jit(solution)/shard_map/dot_general | solution.py:61
  51.1 0.5 reshape.57
  51.6 3.4 %fusion.5 = bf16[4,8,8,128]{3,2,1,0:T(8,128)(2,1)S(1)} fusion(s32[4096]{0:T(1024)S(1)} %bitcast.72, f32[4096,32]{1,0:T(8,128)S(1)} %reshape.57, f32[32]{0:T(128)S(1)} %copy-done.9), kind=kOutput, calls=%fused_computation.28 | convolution fusion | flops 273088512 | bytes 606336 | tf_op jit(solution)/shard_map/dot_general | solution.py:96
  55.1 0.1 copy.97
  55.2 1.1 %scatter_custom_fusion = bf16[320,256]{1,0:T(8,128)(2,1)S(1)} fusion(s32[128]{0:T(128)S(1)} %get-tuple-element.14, bf16[128,256]{1,0:T(8,128)(2,1)S(1)} %copy.97, bf16[]{:T(256)} %constant.7.clone.1), kind=kCustom, calls=%fused_computation.107 | custom fusion | bytes 163842 | tf_op jit(solution)/shard_map/scatter | solution.py:115
  56.4 0.8 fusion.20
  57.2 15.4 %all-to-all-start = ((bf16[64,6,256]{2,1,0:T(8,128)(2,1)}), bf16[64,6,256]{2,1,0:T(8,128)(2,1)S(1)}, u32[]{:S(2)}, u32[]{:S(2)}) async-start(bf16[64,6,256]{2,1,0:T(8,128)(2,1)} %fusion.20), calls=%async_computation | async-start | bytes 524288 | tf_op jit(solution)/shard_map/all_to_all | solution.py:122
  72.6 13.2 %all-to-all-done = bf16[64,6,256]{2,1,0:T(8,128)(2,1)S(1)} async-done(((bf16[64,6,256]{2,1,0:T(8,128)(2,1)}), bf16[64,6,256]{2,1,0:T(8,128)(2,1)S(1)}, u32[]{:S(2)}, u32[]{:S(2)}) %all-to-all-start) | async-done | bytes 196640 | tf_op jit(solution)/shard_map/all_to_all | solution.py:122
  85.9 0.1 fusion.66
  86.0 0.1 reshape.61
  86.2 0.3 multiply_convert_fusion.1
  86.5 0.4 convolution_bitcast_fusion
  86.9 0.1 select_reduce_fusion.1
  87.0 0.1 all_to_all.10
  87.1 14.2 %all_to_all.14 = f32[64,1,5]{2,1,0:T(1,128)S(1)} all-to-all(f32[64,1,5]{2,1,0:T(1,128)S(1)} %bitcast.67), channel_id=1, replica_groups=mesh['gx'=8,'gy'=8,'gz'=8] {'gx','gy'}, dimensions={0} | all-to-all | bytes 2560 | tf_op jit(solution)/shard_map/all_to_all | solution.py:140
  101.4 0.5 broadcast.42
  101.9 0.7 reduce.7
  102.6 0.1 broadcast_in_dim.58
  102.8 0.6 select_reduce_fusion
  (50 shorter events, 1.1 us)
Async XLA Ops:
  0.0 86.5 %copy-start = (bf16[512,512]{1,0:T(8,128)(2,1)S(1)}, bf16[512,512]{1,0:T(8,128)(2,1)}, u32[]{:S(2)}) copy-start(bf16[512,512]{1,0:T(8,128)(2,1)} %param.20) | copy-start | bytes 1572868
  0.0 7.6 %copy-start.1 = (f32[3,4,4,3,1,1,1]{3,2,6,5,4,1,0:T(4,128)S(1)}, f32[3,4,4,3,1,1,1]{3,2,6,5,4,1,0:T(4,128)}, u32[]{:S(2)}) copy-start(f32[3,4,4,3,1,1,1]{3,2,6,5,4,1,0:T(4,128)} %constant.38) | copy-start | bytes 1732
  0.0 13.7 %copy-start.2 = (s32[128,1]{0,1:T(1,128)S(1)}, s32[128,1]{0,1:T(1,128)}, u32[]{:S(2)}) copy-start(s32[128,1]{0,1:T(1,128)} %param.16) | copy-start | bytes 1540
  2.9 12.4 %collective-permute-start = (bf16[1,16,32,128]{3,2,1,0:T(8,128)(2,1)S(1)}, bf16[1,16,32,128]{3,2,1,0:T(8,128)(2,1)S(1)}, u32[]{:S(2)}, u32[]{:S(2)}) collective-permute-start(bf16[1,16,32,128]{3,2,1,0:T(8,128)(2,1)S(1)} %slice.123), channel_id=1, source_target_pairs={{0,64},{64,128},{128,192},{192,256},{256,320},{320,384},{384,448},... | collective-permute-start | bytes 393224 | tf_op jit(solution)/shard_map/ppermute | solution.py:19
  5.2 10.1 %collective-permute-start.1 = (bf16[1,16,32,128]{3,2,1,0:T(8,128)(2,1)S(1)}, bf16[1,16,32,128]{3,2,1,0:T(8,128)(2,1)S(1)}, u32[]{:S(2)}, u32[]{:S(2)}) collective-permute-start(bf16[1,16,32,128]{3,2,1,0:T(8,128)(2,1)S(1)} %slice.125), channel_id=1, source_target_pairs={{64,0},{128,64},{192,128},{256,192},{320,256},{384,320},{448,384},... | collective-permute-start | bytes 393224 | tf_op jit(solution)/shard_map/ppermute | solution.py:21
  14.4 17.3 %copy-start.8 = (s32[128]{0:T(128)S(1)}, s32[128]{0:T(128)}, u32[]{:S(2)}) copy-start(s32[128]{0:T(128)} %param.17) | copy-start | bytes 1540
  15.4 17.8 %collective-permute-start.2 = (bf16[4,1,32,128]{3,2,1,0:T(8,128)(2,1)S(1)}, bf16[4,1,32,128]{3,2,1,0:T(8,128)(2,1)S(1)}, u32[]{:S(2)}, u32[]{:S(2)}) collective-permute-start(bf16[4,1,32,128]{3,2,1,0:T(8,128)(2,1)S(1)} %get-tuple-element.11), channel_id=1, source_target_pairs={{0,8},{8,16},{16,24},{24,32},{32,40},{40,48},{48,56},{1,9},{9,17},... | collective-permute-start | bytes 98312 | tf_op jit(solution)/shard_map/ppermute | solution.py:19
  18.8 14.3 %collective-permute-start.3 = (bf16[4,1,32,128]{3,2,1,0:T(8,128)(2,1)S(1)}, bf16[4,1,32,128]{3,2,1,0:T(8,128)(2,1)S(1)}, u32[]{:S(2)}, u32[]{:S(2)}) collective-permute-start(bf16[4,1,32,128]{3,2,1,0:T(8,128)(2,1)S(1)} %get-tuple-element.12), channel_id=1, source_target_pairs={{8,0},{16,8},{24,16},{32,24},{40,32},{48,40},{56,48},{9,1},{17,9},... | collective-permute-start | bytes 98312 | tf_op jit(solution)/shard_map/ppermute | solution.py:21
  33.3 8.0 %collective-permute-start.4 = (bf16[4,18,32]{2,0,1:T(4,128)(2,1)S(1)}, bf16[4,18,32]{2,0,1:T(4,128)(2,1)S(1)}, u32[]{:S(2)}, u32[]{:S(2)}) collective-permute-start(bf16[4,18,32]{2,0,1:T(4,128)(2,1)S(1)} %bitcast.68), channel_id=1, source_target_pairs={{0,1},{1,2},{2,3},{3,4},{4,5},{5,6},{6,7},{8,9},{9,10},{10,11},{11... | collective-permute-start | bytes 13832 | tf_op jit(solution)/shard_map/ppermute | solution.py:86
  39.4 6.9 %collective-permute-start.5 = (bf16[4,18,32]{2,0,1:T(4,128)(2,1)S(1)}, bf16[4,18,32]{2,0,1:T(4,128)(2,1)S(1)}, u32[]{:S(2)}, u32[]{:S(2)}) collective-permute-start(bf16[4,18,32]{2,0,1:T(4,128)(2,1)S(1)} %bitcast.69), channel_id=1, source_target_pairs={{1,0},{2,1},{3,2},{4,3},{5,4},{6,5},{7,6},{9,8},{10,9},{11,10},{12... | collective-permute-start | bytes 13832 | tf_op jit(solution)/shard_map/ppermute | solution.py:89
  49.1 2.5 %copy-start.5 = (s32[2,16,128]{2,1,0:T(8,128)S(1)}, s32[2,16,128]{2,1,0:T(8,128)}, u32[]{:S(2)}) copy-start(s32[2,16,128]{2,1,0:T(8,128)} %param.13) | copy-start | bytes 49156
  49.1 2.5 %copy-start.9 = (f32[32]{0:T(128)S(1)}, f32[32]{0:T(128)}, u32[]{:S(2)}) copy-start(f32[32]{0:T(128)} %param.15) | copy-start | bytes 388
  51.1 21.5 %copy-start.3 = (bf16[512]{0:T(512)(128)(2,1)S(1)}, bf16[512]{0:T(512)(128)(2,1)}, u32[]{:S(2)}) copy-start(bf16[512]{0:T(512)(128)(2,1)} %param.22) | copy-start | bytes 3076
  51.1 35.0 %copy-start.4 = (bf16[256,512]{1,0:T(8,128)(2,1)S(1)}, bf16[256,512]{1,0:T(8,128)(2,1)}, u32[]{:S(2)}) copy-start(bf16[256,512]{1,0:T(8,128)(2,1)} %param.18) | copy-start | bytes 786436
  51.1 35.0 %copy-start.6 = (f32[512]{0:T(512)S(1)}, f32[512]{0:T(512)}, u32[]{:S(2)}) copy-start(f32[512]{0:T(512)} %param.19) | copy-start | bytes 6148
  51.6 34.9 %copy-start.7 = (f32[512]{0:T(512)S(1)}, f32[512]{0:T(512)}, u32[]{:S(2)}) copy-start(f32[512]{0:T(512)} %param.21) | copy-start | bytes 6148
  57.2 28.6 %all-to-all-start = ((bf16[64,6,256]{2,1,0:T(8,128)(2,1)}), bf16[64,6,256]{2,1,0:T(8,128)(2,1)S(1)}, u32[]{:S(2)}, u32[]{:S(2)}) async-start(bf16[64,6,256]{2,1,0:T(8,128)(2,1)} %fusion.20), calls=%async_computation | async-start | bytes 524288 | tf_op jit(solution)/shard_map/all_to_all | solution.py:122

commit v7 on v6

--- a/solution.py
+++ b/solution.py
@@ -1,5 +1,4 @@
 import jax
-import numpy as np
 import jax.numpy as jnp
 from jax import lax
 from jax.sharding import PartitionSpec as P
@@ -25,21 +24,26 @@
     return cells
 
 
-def band_selector():
-    sel = np.zeros((3, 4, 4, 3), np.float32)
-    sel[0, 3, 0, 0] = 1.0
-    for zi in range(4):
-        for zo in range(4):
-            if abs(zi - zo) <= 1:
-                sel[1, zi, zo, zi - zo + 1] = 1.0
-    sel[2, 0, 3, 2] = 1.0
-    return sel
+def banded_weight(conv_weight, channels):
+    taps = conv_weight.reshape(3, 3, 3, channels, channels).transpose(0, 1, 2, 4, 3)
+    empty = jnp.zeros((3, 3, channels, channels), conv_weight.dtype)
 
+    def block(part, zi, zo):
+        shift = zi - zo if part == 1 else (-1 if (part, zi, zo) == (0, 3, 0) else None)
+        if part == 2 and (zi, zo) == (0, 3):
+            shift = 1
+        if shift is None or abs(shift) > 1:
+            return empty
+        return taps[:, :, shift + 1]
 
-def banded_weight(conv_weight, channels):
-    taps = conv_weight.astype(jnp.float32).reshape(3, 3, 3, channels, channels).transpose(0, 1, 2, 4, 3)
-    full = jnp.einsum("pizd,xydco->xypiczo", band_selector(), taps, precision=lax.Precision.HIGHEST)
-    return full.reshape(27 * 4 * channels, 4 * channels).astype(jnp.bfloat16)
+    parts = [
+        jnp.concatenate(
+            [jnp.concatenate([block(part, zi, zo) for zo in range(4)], axis=3) for zi in range(4)],
+            axis=2,
+        )
+        for part in range(3)
+    ]
+    return jnp.stack(parts, axis=2).reshape(27 * 4 * channels, 4 * channels)
 
 
 def conv_lane_dense(padded, low, high, conv_weight, channels):

time: 104 us -> 88.2 us (0.85)
  local copies, waits for them, and re-layouts: 21.9 us -> 11.1 us
  matrix products: 12.2 us -> 6.13 us
  starting transfers between devices: 30.8 us -> 28.7 us
  waiting for transfers between devices: 18 us -> 20 us
  other arithmetic: 5.6 us -> 7.04 us
    convert_element_type x2 -> x0, local copies, waits for them, and re-layouts: 11.5 us -> none  [banded_weight(): return full.reshape(27 * 4 * channels, 4 * channels).astype(jnp.bfloat16)]
    dot_general x1 -> x0, matrix products: 6.1 us -> none  [banded_weight(): jnp.einsum('pizd,xydco->xypiczo', band_selector(), taps, precision=lax.Pr...]
    ppermute x2, waiting for transfers between devices: 0.01 us -> 2.14 us  [extended(): lax.ppermute(head, axis, [((i + 1) % count, i) for i in range(ends)])]
    all_to_all x1, starting transfers between devices: 15.4 us -> 13.3 us  [body(): lax.all_to_all(send, ('gx', 'gy'), split_axis=0, concat_axis=0, tiled=True)]
    another operation x0 -> x3, other arithmetic: none -> 1.44 us  [banded_weight(): return jnp.stack(parts, axis=2).reshape(27 * 4 * channels, 4 * channels)]
  transfers between devices with their start and end apart: 7 -> 7, of which waited for: 2 -> 4; matrix products, arithmetic and copies ran while one was open for 22% -> 8% of each run, Pallas kernels for 0% -> 0%
where the time goes in v7:
time: 88.2 us; the launch traced here: 87.8 us
  starting transfers between devices  28.7 us (33%)
  waiting for transfers between devices  20 us (23%)
  blocking collectives  14.2 us (16%)
  local copies, waits for them, and re-layouts  11.1 us (13%)
  other arithmetic  7.04 us (8%)
  matrix products  6.13 us (7%)
    all_to_all x1, blocking collectives, body(): lax.all_to_all(owner_scores.reshape(groups, capacity), ('gx', 'gy'), spli...  14.2 us
    all_to_all x1, starting transfers between devices, body(): lax.all_to_all(send, ('gx', 'gy'), split_axis=0, concat_axis=0, tiled=True)  13.3 us
    all_to_all x1, waiting for transfers between devices, body(): lax.all_to_all(send, ('gx', 'gy'), split_axis=0, concat_axis=0, tiled=True)  13.2 us
    ppermute x1, starting transfers between devices, body(): lax.ppermute(padded[:, :, -1, chunk - channels:], 'gz', [(i, i + 1) for i...  5.49 us
    ppermute x2, starting transfers between devices, extended(): lax.ppermute(tail, axis, [(i, (i + 1) % count) for i in range(ends)])  5.23 us
    ppermute x1, waiting for transfers between devices, body(): lax.ppermute(padded[:, :, 0, :channels], 'gz', [(i + 1, i) for i in range...  4.62 us
    dot_general x1, matrix products, body(): lax.dot_general(onehot, fields, (((0,), (0,)), ((), ())), preferred_eleme...  3.44 us
    ppermute x2, starting transfers between devices, extended(): lax.ppermute(head, axis, [((i + 1) % count, i) for i in range(ends)])  2.57 us
  transfers between devices with their start and end apart: 7, of which 4 were waited for; matrix products, arithmetic and copies ran while one was open for 8% of the time, Pallas kernels for 0%

profile of v7, /device:TPU:192, one launch (start us, length us, event | category | flops | bytes accessed | tf_op | source)
XLA Modules:
  0.0 87.8 jit_solution(259621745158114784)
XLA Ops:
  0.0 2.1 %copy.91 = bf16[32,2,16,128]{0,2,3,1:T(8,128)(2,1)S(1)} copy(bf16[32,2,16,128]{3,2,1,0:T(8,128)(2,1)} %param.11) | data formatting | bytes 524288 | tf_op args[0]
  2.1 0.2 fusion.76
  2.3 0.2 copy.92
  2.6 0.3 slice.141
  2.9 1.7 %collective-permute-start = (bf16[1,16,32,128]{3,2,1,0:T(8,128)(2,1)S(1)}, bf16[1,16,32,128]{3,2,1,0:T(8,128)(2,1)S(1)}, u32[]{:S(2)}, u32[]{:S(2)}) collective-permute-start(bf16[1,16,32,128]{3,2,1,0:T(8,128)(2,1)S(1)} %slice.141), channel_id=1, source_target_pairs={{0,64},{64,128},{128,192},{192,256},{256,320},{320,384},{384,448},... | collective-permute-start | bytes 393224 | tf_op jit(solution)/shard_map/ppermute | solution.py:18
  4.6 0.2 copy.94
  4.9 0.9 %slice.143 = bf16[1,16,32,128]{3,2,1,0:T(8,128)(2,1)} reshape(bf16[1,16,32,4,32]{4,3,2,1,0:T(4,128)(2,1)S(1)} %copy.94) | data formatting | bytes 262144 | tf_op jit(solution)/shard_map/slice | solution.py:14
  5.8 1.3 %collective-permute-start.1 = (bf16[1,16,32,128]{3,2,1,0:T(8,128)(2,1)}, bf16[1,16,32,128]{3,2,1,0:T(8,128)(2,1)S(1)}, u32[]{:S(2)}, u32[]{:S(2)}) collective-permute-start(bf16[1,16,32,128]{3,2,1,0:T(8,128)(2,1)} %slice.143), channel_id=1, source_target_pairs={{64,0},{128,64},{192,128},{256,192},{320,256},{384,320},{448,384},... | collective-permute-start | bytes 393224 | tf_op jit(solution)/shard_map/ppermute | solution.py:20
  7.1 1.1 %copy.99 = bf16[3,3,3,32,32]{3,4,1,0,2:T(8,128)(2,1)S(1)} copy(bf16[3,3,3,32,32]{4,3,2,1,0:T(8,128)(2,1)} %bitcast.75) | data formatting | bytes 110592 | tf_op jit(solution)/shard_map/reshape | solution.py:28
  8.3 0.2 reduce_window_sum.11
  8.5 0.2 select_reduce_fusion.2
  8.7 0.3 maximum_bitcast_fusion
  9.1 0.6 copy.93
  9.6 0.5 reshape.56
  10.2 0.1 fusion.14
  10.4 0.2 collective-permute-done.1
  10.6 3.5 %collective-permute-start.2 = (bf16[4,1,32,128]{3,2,1,0:T(8,128)(2,1)S(1)}, bf16[4,1,32,128]{3,2,1,0:T(8,128)(2,1)S(1)}, u32[]{:S(2)}, u32[]{:S(2)}) collective-permute-start(bf16[4,1,32,128]{3,2,1,0:T(8,128)(2,1)S(1)} %get-tuple-element.11), channel_id=1, source_target_pairs={{0,8},{8,16},{16,24},{24,32},{32,40},{40,48},{48,56},{1,9},{9,17},... | collective-permute-start | bytes 98312 | tf_op jit(solution)/shard_map/ppermute | solution.py:18
  14.1 1.3 %collective-permute-start.3 = (bf16[4,1,32,128]{3,2,1,0:T(8,128)(2,1)S(1)}, bf16[4,1,32,128]{3,2,1,0:T(8,128)(2,1)S(1)}, u32[]{:S(2)}, u32[]{:S(2)}) collective-permute-start(bf16[4,1,32,128]{3,2,1,0:T(8,128)(2,1)S(1)} %get-tuple-element.12), channel_id=1, source_target_pairs={{8,0},{16,8},{24,16},{32,24},{40,32},{48,40},{56,48},{9,1},{17,9},... | collective-permute-start | bytes 98312 | tf_op jit(solution)/shard_map/ppermute | solution.py:20
  15.4 1.0 %pad_maximum_fusion = bf16[3,3,3,128,128]{4,3,2,1,0:T(8,128)(2,1)} fusion(bf16[3,3,1,128,128]{4,3,2,1,0:T(8,128)(2,1)S(1)} %get-tuple-element.14, bf16[3,3,1,128,128]{4,3,2,1,0:T(8,128)(2,1)S(1)} %maximum_bitcast_fusion, bf16[3,3,1,128,128]{4,3,2,1,0:T(8,128)(2,1)S(1)} %get-tuple-element.13), kind=kLoop, calls=%fused_computation.31 | loop fusion | flops 884736 | bytes 1769472 | tf_op jit(solution)/shard_map/stack | solution.py:46
  16.4 1.3 %scatter_custom_fusion.1 = bf16[320]{0:T(512)(128)(2,1)S(1)} fusion(s32[128]{0:T(128)S(1)} %get-tuple-element.19, bf16[128]{0:T(256)(128)(2,1)S(1)} %convert_element_type.58, bf16[]{:T(256)} %constant.14.clone.1), kind=kCustom, calls=%fused_computation.140 | custom fusion | bytes 642 | tf_op jit(solution)/shard_map/scatter | solution.py:120
  17.7 0.1 reshape.83
  17.9 2.0 %collective-permute-done.3 = bf16[4,1,32,128]{3,2,1,0:T(8,128)(2,1)S(1)} collective-permute-done((bf16[4,1,32,128]{3,2,1,0:T(8,128)(2,1)S(1)}, bf16[4,1,32,128]{3,2,1,0:T(8,128)(2,1)S(1)}, u32[]{:S(2)}, u32[]{:S(2)}) %collective-permute-start.3) | collective-permute-done | bytes 32800 | tf_op jit(solution)/shard_map/ppermute | solution.py:20
  19.9 0.1 pad_maximum_fusion.8
  20.0 5.5 %collective-permute-start.4 = (bf16[4,18,32]{2,0,1:T(4,128)(2,1)S(1)}, bf16[4,18,32]{2,0,1:T(4,128)(2,1)S(1)}, u32[]{:S(2)}, u32[]{:S(2)}) collective-permute-start(bf16[4,18,32]{2,0,1:T(4,128)(2,1)S(1)} %bitcast.77), channel_id=1, source_target_pairs={{0,1},{1,2},{2,3},{3,4},{4,5},{5,6},{6,7},{8,9},{9,10},{10,11},{11... | collective-permute-start | bytes 13832 | tf_op jit(solution)/shard_map/ppermute | solution.py:90
  25.6 0.3 fusion.77
  25.9 2.1 %collective-permute-start.5 = (bf16[4,18,32]{2,0,1:T(4,128)(2,1)S(1)}, bf16[4,18,32]{2,0,1:T(4,128)(2,1)S(1)}, u32[]{:S(2)}, u32[]{:S(2)}) collective-permute-start(bf16[4,18,32]{2,0,1:T(4,128)(2,1)S(1)} %bitcast.78), channel_id=1, source_target_pairs={{1,0},{2,1},{3,2},{4,3},{5,4},{6,5},{7,6},{9,8},{10,9},{11,10},{12... | collective-permute-start | bytes 13832 | tf_op jit(solution)/shard_map/ppermute | solution.py:93
  28.1 4.6 %collective-permute-done.5 = bf16[4,18,32]{2,0,1:T(4,128)(2,1)S(1)} collective-permute-done((bf16[4,18,32]{2,0,1:T(4,128)(2,1)S(1)}, bf16[4,18,32]{2,0,1:T(4,128)(2,1)S(1)}, u32[]{:S(2)}, u32[]{:S(2)}) %collective-permute-start.5) | collective-permute-done | bytes 4640 | tf_op jit(solution)/shard_map/ppermute | solution.py:93
  32.8 0.1 fusion.43
  33.0 0.1 fusion.27
  33.1 0.1 fusion.45
  33.3 0.1 fusion.29
  33.4 0.1 fusion.47
  33.6 0.1 fusion.31
  33.7 0.1 fusion.49
  33.9 0.1 fusion.33
  34.0 0.1 fusion.51
  34.2 0.1 fusion.35
  34.3 0.1 fusion.53
  34.6 0.1 fusion.37
  34.7 0.1 fusion.55
  34.9 0.1 fusion.39
  35.0 0.1 fusion.41
  35.2 0.1 fusion.25
  35.3 0.1 fusion.58
  35.5 0.1 fusion.56
  35.6 2.0 %fusion.79 = f32[2,16,32,128]{3,2,1,0:T(8,128)S(1)} fusion(bf16[2,16,32,3456]{3,2,1,0:T(8,128)(2,1)S(1)} %fusion.56, bf16[3456,128,1,1]{1,0,3,2:T(8,128)(2,1)S(1)} %bitcast.72), kind=kOutput, calls=%fused_computation.148 | convolution fusion | flops 905969664 | bytes 8486912 | tf_op jit(solution)/shard_map/dot_general | solution.py:65
  37.6 0.5 reshape.59
  38.2 3.4 %fusion.4 = bf16[4,8,8,128]{3,2,1,0:T(8,128)(2,1)S(1)} fusion(s32[4096]{0:T(1024)S(1)} %bitcast.81, f32[4096,32]{1,0:T(8,128)S(1)} %reshape.59, f32[32]{0:T(128)S(1)} %copy-done.9), kind=kOutput, calls=%fused_computation.26 | convolution fusion | flops 273088512 | bytes 606336 | tf_op jit(solution)/shard_map/dot_general | solution.py:100
  41.6 0.1 copy.103
  41.7 1.1 %scatter_custom_fusion = bf16[320,256]{1,0:T(8,128)(2,1)S(1)} fusion(s32[128]{0:T(128)S(1)} %get-tuple-element.19, bf16[128,256]{1,0:T(8,128)(2,1)S(1)} %copy.103, bf16[]{:T(256)} %constant.10.clone.1), kind=kCustom, calls=%fused_computation.113 | custom fusion | bytes 163842 | tf_op jit(solution)/shard_map/scatter | solution.py:119
  42.9 0.8 fusion.23
  43.7 13.3 %all-to-all-start = ((bf16[64,6,256]{2,1,0:T(8,128)(2,1)}), bf16[64,6,256]{2,1,0:T(8,128)(2,1)S(1)}, u32[]{:S(2)}, u32[]{:S(2)}) async-start(bf16[64,6,256]{2,1,0:T(8,128)(2,1)} %fusion.23), calls=%async_computation | async-start | bytes 524288 | tf_op jit(solution)/shard_map/all_to_all | solution.py:126
  57.0 13.2 %all-to-all-done = bf16[64,6,256]{2,1,0:T(8,128)(2,1)S(1)} async-done(((bf16[64,6,256]{2,1,0:T(8,128)(2,1)}), bf16[64,6,256]{2,1,0:T(8,128)(2,1)S(1)}, u32[]{:S(2)}, u32[]{:S(2)}) %all-to-all-start) | async-done | bytes 196640 | tf_op jit(solution)/shard_map/all_to_all | solution.py:126
  70.3 0.1 fusion.69
  70.4 0.1 reshape.63
  70.6 0.3 multiply_convert_fusion.1
  71.0 0.4 convolution_bitcast_fusion
  71.3 0.1 select_reduce_fusion.1
  71.4 0.1 all_to_all.10
  71.6 14.2 %all_to_all.14 = f32[64,1,5]{2,1,0:T(1,128)S(1)} all-to-all(f32[64,1,5]{2,1,0:T(1,128)S(1)} %bitcast.76), channel_id=1, replica_groups=mesh['gx'=8,'gy'=8,'gz'=8] {'gx','gy'}, dimensions={0} | all-to-all | bytes 2560 | tf_op jit(solution)/shard_map/all_to_all | solution.py:144
  85.8 0.5 broadcast.67
  86.3 0.7 reduce.7
  87.0 0.1 broadcast_in_dim.62
  87.2 0.6 select_reduce_fusion
  (55 shorter events, 1.3 us)
Async XLA Ops:
  0.0 70.9 %copy-start = (bf16[512,512]{1,0:T(8,128)(2,1)S(1)}, bf16[512,512]{1,0:T(8,128)(2,1)}, u32[]{:S(2)}) copy-start(bf16[512,512]{1,0:T(8,128)(2,1)} %param.19) | copy-start | bytes 1572868
  0.0 8.2 %copy-start.2 = (s32[128,1]{0,1:T(1,128)S(1)}, s32[128,1]{0,1:T(1,128)}, u32[]{:S(2)}) copy-start(s32[128,1]{0,1:T(1,128)} %param.15) | copy-start | bytes 1540
  2.1 14.2 %copy-start.8 = (s32[128]{0:T(128)S(1)}, s32[128]{0:T(128)}, u32[]{:S(2)}) copy-start(s32[128]{0:T(128)} %param.16) | copy-start | bytes 1540
  2.9 7.4 %collective-permute-start = (bf16[1,16,32,128]{3,2,1,0:T(8,128)(2,1)S(1)}, bf16[1,16,32,128]{3,2,1,0:T(8,128)(2,1)S(1)}, u32[]{:S(2)}, u32[]{:S(2)}) collective-permute-start(bf16[1,16,32,128]{3,2,1,0:T(8,128)(2,1)S(1)} %slice.141), channel_id=1, source_target_pairs={{0,64},{64,128},{128,192},{192,256},{256,320},{320,384},{384,448},... | collective-permute-start | bytes 393224 | tf_op jit(solution)/shard_map/ppermute | solution.py:18
  5.8 4.7 %collective-permute-start.1 = (bf16[1,16,32,128]{3,2,1,0:T(8,128)(2,1)}, bf16[1,16,32,128]{3,2,1,0:T(8,128)(2,1)S(1)}, u32[]{:S(2)}, u32[]{:S(2)}) collective-permute-start(bf16[1,16,32,128]{3,2,1,0:T(8,128)(2,1)} %slice.143), channel_id=1, source_target_pairs={{64,0},{128,64},{192,128},{256,192},{320,256},{384,320},{448,384},... | collective-permute-start | bytes 393224 | tf_op jit(solution)/shard_map/ppermute | solution.py:20
  10.6 7.3 %collective-permute-start.2 = (bf16[4,1,32,128]{3,2,1,0:T(8,128)(2,1)S(1)}, bf16[4,1,32,128]{3,2,1,0:T(8,128)(2,1)S(1)}, u32[]{:S(2)}, u32[]{:S(2)}) collective-permute-start(bf16[4,1,32,128]{3,2,1,0:T(8,128)(2,1)S(1)} %get-tuple-element.11), channel_id=1, source_target_pairs={{0,8},{8,16},{16,24},{24,32},{32,40},{40,48},{48,56},{1,9},{9,17},... | collective-permute-start | bytes 98312 | tf_op jit(solution)/shard_map/ppermute | solution.py:18
  14.1 5.8 %collective-permute-start.3 = (bf16[4,1,32,128]{3,2,1,0:T(8,128)(2,1)S(1)}, bf16[4,1,32,128]{3,2,1,0:T(8,128)(2,1)S(1)}, u32[]{:S(2)}, u32[]{:S(2)}) collective-permute-start(bf16[4,1,32,128]{3,2,1,0:T(8,128)(2,1)S(1)} %get-tuple-element.12), channel_id=1, source_target_pairs={{8,0},{16,8},{24,16},{32,24},{40,32},{48,40},{56,48},{9,1},{17,9},... | collective-permute-start | bytes 98312 | tf_op jit(solution)/shard_map/ppermute | solution.py:20
  20.0 8.0 %collective-permute-start.4 = (bf16[4,18,32]{2,0,1:T(4,128)(2,1)S(1)}, bf16[4,18,32]{2,0,1:T(4,128)(2,1)S(1)}, u32[]{:S(2)}, u32[]{:S(2)}) collective-permute-start(bf16[4,18,32]{2,0,1:T(4,128)(2,1)S(1)} %bitcast.77), channel_id=1, source_target_pairs={{0,1},{1,2},{2,3},{3,4},{4,5},{5,6},{6,7},{8,9},{9,10},{10,11},{11... | collective-permute-start | bytes 13832 | tf_op jit(solution)/shard_map/ppermute | solution.py:90
  25.9 6.9 %collective-permute-start.5 = (bf16[4,18,32]{2,0,1:T(4,128)(2,1)S(1)}, bf16[4,18,32]{2,0,1:T(4,128)(2,1)S(1)}, u32[]{:S(2)}, u32[]{:S(2)}) collective-permute-start(bf16[4,18,32]{2,0,1:T(4,128)(2,1)S(1)} %bitcast.78), channel_id=1, source_target_pairs={{1,0},{2,1},{3,2},{4,3},{5,4},{6,5},{7,6},{9,8},{10,9},{11,10},{12... | collective-permute-start | bytes 13832 | tf_op jit(solution)/shard_map/ppermute | solution.py:93
  33.9 1.7 %copy-start.1 = (bf16[3,3,3,128,128]{4,3,2,1,0:T(8,128)(2,1)S(1)}, bf16[3,3,3,128,128]{4,3,2,1,0:T(8,128)(2,1)}, u32[]{:S(2)}) copy-start(bf16[3,3,3,128,128]{4,3,2,1,0:T(8,128)(2,1)} %pad_maximum_fusion) | copy-start | bytes 2654212
  35.6 2.5 %copy-start.5 = (s32[2,16,128]{2,1,0:T(8,128)S(1)}, s32[2,16,128]{2,1,0:T(8,128)}, u32[]{:S(2)}) copy-start(s32[2,16,128]{2,1,0:T(8,128)} %param.12) | copy-start | bytes 49156
  35.6 2.5 %copy-start.9 = (f32[32]{0:T(128)S(1)}, f32[32]{0:T(128)}, u32[]{:S(2)}) copy-start(f32[32]{0:T(128)} %param.14) | copy-start | bytes 388
  37.6 19.4 %copy-start.3 = (bf16[512]{0:T(512)(128)(2,1)S(1)}, bf16[512]{0:T(512)(128)(2,1)}, u32[]{:S(2)}) copy-start(bf16[512]{0:T(512)(128)(2,1)} %param.21) | copy-start | bytes 3076
  37.6 32.9 %copy-start.6 = (f32[512]{0:T(512)S(1)}, f32[512]{0:T(512)}, u32[]{:S(2)}) copy-start(f32[512]{0:T(512)} %param.18) | copy-start | bytes 6148
  38.1 32.5 %copy-start.4 = (bf16[256,512]{1,0:T(8,128)(2,1)S(1)}, bf16[256,512]{1,0:T(8,128)(2,1)}, u32[]{:S(2)}) copy-start(bf16[256,512]{1,0:T(8,128)(2,1)} %param.17) | copy-start | bytes 786436
  38.1 32.8 %copy-start.7 = (f32[512]{0:T(512)S(1)}, f32[512]{0:T(512)}, u32[]{:S(2)}) copy-start(f32[512]{0:T(512)} %param.20) | copy-start | bytes 6148
  43.7 26.5 %all-to-all-start = ((bf16[64,6,256]{2,1,0:T(8,128)(2,1)}), bf16[64,6,256]{2,1,0:T(8,128)(2,1)S(1)}, u32[]{:S(2)}, u32[]{:S(2)}) async-start(bf16[64,6,256]{2,1,0:T(8,128)(2,1)} %fusion.23), calls=%async_computation | async-start | bytes 524288 | tf_op jit(solution)/shard_map/all_to_all | solution.py:126

commit v8 on v7

--- a/solution.py
+++ b/solution.py
@@ -48,12 +48,13 @@
 
 def conv_lane_dense(padded, low, high, conv_weight, channels):
     px, py, nchunk, chunk = padded.shape
-    low_chunk = jnp.pad(low, ((0, 0), (0, 0), (chunk - channels, 0)))[:, :, None]
-    high_chunk = jnp.pad(high, ((0, 0), (0, 0), (0, chunk - channels)))[:, :, None]
+    weight = banded_weight(conv_weight, channels)
+    blocks = weight.reshape(9, 3, chunk, chunk)
+    empty = jnp.zeros((px, py, 1, chunk), padded.dtype)
     parts = (
-        jnp.concatenate([low_chunk, padded[:, :, :-1]], axis=2),
+        jnp.concatenate([empty, padded[:, :, :-1]], axis=2),
         padded,
-        jnp.concatenate([padded[:, :, 1:], high_chunk], axis=2),
+        jnp.concatenate([padded[:, :, 1:], empty], axis=2),
     )
     slabs = [
         parts[p][dx : dx + px - 2, dy : dy + py - 2]
@@ -61,8 +62,20 @@
         for dy in range(3)
         for p in range(3)
     ]
-    stacked = jnp.concatenate(slabs, axis=3)
-    return jnp.dot(stacked, banded_weight(conv_weight, channels), preferred_element_type=jnp.float32)
+    main = jnp.dot(jnp.concatenate(slabs, axis=3), weight, preferred_element_type=jnp.float32)
+    low_chunk = jnp.pad(low, ((0, 0), (0, 0), (chunk - channels, 0)))
+    high_chunk = jnp.pad(high, ((0, 0), (0, 0), (0, chunk - channels)))
+
+    def edge(halo, part):
+        pieces = [halo[dx : dx + px - 2, dy : dy + py - 2] for dx in range(3) for dy in range(3)]
+        return jnp.dot(
+            jnp.concatenate(pieces, axis=2),
+            blocks[:, part].reshape(9 * chunk, chunk),
+            preferred_element_type=jnp.float32,
+        )
+
+    main = main.at[:, :, 0, :].add(edge(low_chunk, 0))
+    return main.at[:, :, nchunk - 1, :].add(edge(high_chunk, 2))
 
 def body(
     features,

time: 88.2 us -> 86.7 us (0.983)
  local copies, waits for them, and re-layouts: 11.1 us -> 14 us
  waiting for transfers between devices: 20 us -> 17.1 us
  other arithmetic: 7.04 us -> 5.16 us
    ppermute x1, waiting for transfers between devices: 4.62 us -> 1.89 us  [body(): lax.ppermute(padded[:, :, 0, :channels], 'gz', [(i + 1, i) for i in range...]
    unnamed x25 -> x58, local copies, waits for them, and re-layouts: 2.29 us -> 4.75 us
    unnamed x25 -> x8, other arithmetic: 2.47 us -> 0.51 us
    dot_general x1 -> x3, matrix products: 1.99 us -> 2.33 us  [the longest x1 1.99 us: conv_lane_dense(): jnp.dot(jnp.concatenate(slabs, axis=3), weight, preferred_element_type=jn...]
  transfers between devices with their start and end apart: 7 -> 7, of which waited for: 4 -> 3; matrix products, arithmetic and copies ran while one was open for 8% -> 12% of each run, Pallas kernels for 0% -> 0%
where the time goes in v8:
time: 86.7 us; the launch traced here: 86.3 us
  starting transfers between devices  28.6 us (33%)
  waiting for transfers between devices  17.1 us (20%)
  blocking collectives  14.2 us (16%)
  local copies, waits for them, and re-layouts  14 us (16%)
  matrix products  6.47 us (7%)
  other arithmetic  5.16 us (6%)
    all_to_all x1, blocking collectives, body(): lax.all_to_all(owner_scores.reshape(groups, capacity), ('gx', 'gy'), spli...  14.2 us
    all_to_all x1, starting transfers between devices, body(): lax.all_to_all(send, ('gx', 'gy'), split_axis=0, concat_axis=0, tiled=True)  13.4 us
    all_to_all x1, waiting for transfers between devices, body(): lax.all_to_all(send, ('gx', 'gy'), split_axis=0, concat_axis=0, tiled=True)  13.2 us
    ppermute x1, starting transfers between devices, body(): lax.ppermute(padded[:, :, -1, chunk - channels:], 'gz', [(i, i + 1) for i...  5.49 us
    ppermute x2, starting transfers between devices, extended(): lax.ppermute(tail, axis, [(i, (i + 1) % count) for i in range(ends)])  5.23 us
    unnamed x58, local copies, waits for them, and re-layouts  4.75 us
    dot_general x1, matrix products, body(): lax.dot_general(onehot, fields, (((0,), (0,)), ((), ())), preferred_eleme...  3.44 us
    ppermute x2, starting transfers between devices, extended(): lax.ppermute(head, axis, [((i + 1) % count, i) for i in range(ends)])  2.57 us
  transfers between devices with their start and end apart: 7, of which 3 were waited for; matrix products, arithmetic and copies ran while one was open for 12% of the time, Pallas kernels for 0%

profile of v8, /device:TPU:192, one launch (start us, length us, event | category | flops | bytes accessed | tf_op | source)
XLA Modules:
  0.0 86.3 jit_solution(2006706441317308484)
XLA Ops:
  0.0 2.1 %copy.58 = bf16[32,2,16,128]{0,2,3,1:T(8,128)(2,1)S(1)} copy(bf16[32,2,16,128]{3,2,1,0:T(8,128)(2,1)} %param.15) | data formatting | bytes 524288 | tf_op args[0]
  2.1 0.2 fusion.42
  2.3 0.2 copy.59
  2.6 0.3 slice.251
  2.9 1.7 %collective-permute-start = (bf16[1,16,32,128]{3,2,1,0:T(8,128)(2,1)S(1)}, bf16[1,16,32,128]{3,2,1,0:T(8,128)(2,1)S(1)}, u32[]{:S(2)}, u32[]{:S(2)}) collective-permute-start(bf16[1,16,32,128]{3,2,1,0:T(8,128)(2,1)S(1)} %slice.251), channel_id=1, source_target_pairs={{0,64},{64,128},{128,192},{192,256},{256,320},{320,384},{384,448},... | collective-permute-start | bytes 393224 | tf_op jit(solution)/shard_map/ppermute | solution.py:18
  4.6 0.2 copy.61
  4.9 0.9 %slice.253 = bf16[1,16,32,128]{3,2,1,0:T(8,128)(2,1)} reshape(bf16[1,16,32,4,32]{4,3,2,1,0:T(4,128)(2,1)S(1)} %copy.61) | data formatting | bytes 262144 | tf_op jit(solution)/shard_map/slice | solution.py:14
  5.8 1.3 %collective-permute-start.1 = (bf16[1,16,32,128]{3,2,1,0:T(8,128)(2,1)}, bf16[1,16,32,128]{3,2,1,0:T(8,128)(2,1)S(1)}, u32[]{:S(2)}, u32[]{:S(2)}) collective-permute-start(bf16[1,16,32,128]{3,2,1,0:T(8,128)(2,1)} %slice.253), channel_id=1, source_target_pairs={{64,0},{128,64},{192,128},{256,192},{320,256},{384,320},{448,384},... | collective-permute-start | bytes 393224 | tf_op jit(solution)/shard_map/ppermute | solution.py:20
  7.1 1.1 %copy.62 = bf16[3,3,3,32,32]{3,4,1,0,2:T(8,128)(2,1)S(1)} copy(bf16[3,3,3,32,32]{4,3,2,1,0:T(8,128)(2,1)} %bitcast.85) | data formatting | bytes 110592 | tf_op jit(solution)/shard_map/reshape | solution.py:28
  8.3 0.2 reduce_window_sum.11
  8.5 0.2 select_reduce_fusion.2
  8.7 0.3 maximum_bitcast_fusion
  9.1 0.6 copy.60
  9.6 0.5 reshape.136
  10.2 0.2 fusion.11
  10.6 3.5 %collective-permute-start.2 = (bf16[4,1,32,128]{3,2,1,0:T(8,128)(2,1)S(1)}, bf16[4,1,32,128]{3,2,1,0:T(8,128)(2,1)S(1)}, u32[]{:S(2)}, u32[]{:S(2)}) collective-permute-start(bf16[4,1,32,128]{3,2,1,0:T(8,128)(2,1)S(1)} %get-tuple-element.35), channel_id=1, source_target_pairs={{0,8},{8,16},{16,24},{24,32},{32,40},{40,48},{48,56},{1,9},{9,17},... | collective-permute-start | bytes 98312 | tf_op jit(solution)/shard_map/ppermute | solution.py:18
  14.1 1.3 %collective-permute-start.3 = (bf16[4,1,32,128]{3,2,1,0:T(8,128)(2,1)S(1)}, bf16[4,1,32,128]{3,2,1,0:T(8,128)(2,1)S(1)}, u32[]{:S(2)}, u32[]{:S(2)}) collective-permute-start(bf16[4,1,32,128]{3,2,1,0:T(8,128)(2,1)S(1)} %get-tuple-element.36), channel_id=1, source_target_pairs={{8,0},{16,8},{24,16},{32,24},{40,32},{48,40},{56,48},{9,1},{17,9},... | collective-permute-start | bytes 98312 | tf_op jit(solution)/shard_map/ppermute | solution.py:20
  15.4 1.0 %pad_maximum_fusion = bf16[3,3,3,128,128]{4,3,2,1,0:T(8,128)(2,1)} fusion(bf16[3,3,1,128,128]{4,3,2,1,0:T(8,128)(2,1)S(1)} %get-tuple-element.38, bf16[3,3,1,128,128]{4,3,2,1,0:T(8,128)(2,1)S(1)} %maximum_bitcast_fusion, bf16[3,3,1,128,128]{4,3,2,1,0:T(8,128)(2,1)S(1)} %get-tuple-element.41), kind=kLoop, calls=%fused_computation.15 | loop fusion | flops 884736 | bytes 1769472 | tf_op jit(solution)/shard_map/stack | solution.py:46
  16.4 1.3 %scatter_custom_fusion.1 = bf16[320]{0:T(512)(128)(2,1)S(1)} fusion(s32[128]{0:T(128)S(1)} %get-tuple-element.47, bf16[128]{0:T(256)(128)(2,1)S(1)} %convert_element_type.58, bf16[]{:T(256)} %constant.83.clone.1), kind=kCustom, calls=%fused_computation.122 | custom fusion | bytes 642 | tf_op jit(solution)/shard_map/scatter | solution.py:133
  17.7 0.1 reshape.167
  17.9 2.0 %collective-permute-done.3 = bf16[4,1,32,128]{3,2,1,0:T(8,128)(2,1)S(1)} collective-permute-done((bf16[4,1,32,128]{3,2,1,0:T(8,128)(2,1)S(1)}, bf16[4,1,32,128]{3,2,1,0:T(8,128)(2,1)S(1)}, u32[]{:S(2)}, u32[]{:S(2)}) %collective-permute-start.3) | collective-permute-done | bytes 32800 | tf_op jit(solution)/shard_map/ppermute | solution.py:20
  19.9 0.3 fusion.43
  20.2 0.1 slice_dynamic-update-slice_fusion.17
  20.5 0.1 slice_dynamic-update-slice_fusion.15
  20.8 0.1 slice_dynamic-update-slice_fusion.13
  21.0 0.1 slice_dynamic-update-slice_fusion.11
  21.3 0.1 slice_dynamic-update-slice_fusion.9
  21.6 0.1 slice_dynamic-update-slice_fusion.7
  21.9 0.1 slice_dynamic-update-slice_fusion.5
  22.2 0.1 slice_dynamic-update-slice_fusion.3
  22.5 0.1 slice_dynamic-update-slice_fusion.1
  22.7 0.1 pad_maximum_fusion.6
  22.9 5.5 %collective-permute-start.4 = (bf16[4,18,32]{2,1,0:T(8,128)(2,1)S(1)}, bf16[4,18,32]{2,1,0:T(8,128)(2,1)S(1)}, u32[]{:S(2)}, u32[]{:S(2)}) collective-permute-start(bf16[4,18,32]{2,1,0:T(8,128)(2,1)S(1)} %copy.66), channel_id=1, source_target_pairs={{0,1},{1,2},{2,3},{3,4},{4,5},{5,6},{6,7},{8,9},{9,10},{10,11},{11... | collective-permute-start | bytes 13832 | tf_op jit(solution)/shard_map/ppermute | solution.py:103
  28.4 1.9 %collective-permute-start.5 = (bf16[4,18,32]{2,1,0:T(8,128)(2,1)S(1)}, bf16[4,18,32]{2,1,0:T(8,128)(2,1)S(1)}, u32[]{:S(2)}, u32[]{:S(2)}) collective-permute-start(bf16[4,18,32]{2,1,0:T(8,128)(2,1)S(1)} %copy.68), channel_id=1, source_target_pairs={{1,0},{2,1},{3,2},{4,3},{5,4},{6,5},{7,6},{9,8},{10,9},{11,10},{12... | collective-permute-start | bytes 13832 | tf_op jit(solution)/shard_map/ppermute | solution.py:106
  30.4 2.0 %fusion.45 = f32[2,16,32,128]{3,2,1,0:T(8,128)S(1)} fusion(bf16[2,16,32,3456]{3,2,1,0:T(8,128)(2,1)S(1)} %slice_dynamic-update-slice_fusion, bf16[3456,128,1,1]{1,0,3,2:T(8,128)(2,1)S(1)} %bitcast.82), kind=kOutput, calls=%fused_computation.132 | convolution fusion | flops 905969664 | bytes 8486912 | tf_op jit(solution)/shard_map/dot_general | solution.py:65
  32.5 0.1 constant_dynamic-update-slice_fusion.11
  32.6 0.1 constant_dynamic-update-slice_fusion.10
  32.7 0.1 constant_dynamic-update-slice_fusion.8
  32.8 0.1 constant_dynamic-update-slice_fusion.7
  33.0 0.1 constant_dynamic-update-slice_fusion.5
  33.1 0.1 constant_dynamic-update-slice_fusion.4
  33.2 0.2 fusion.46
  33.4 0.1 scatter-add.6
  33.5 1.9 %collective-permute-done.5 = bf16[4,18,32]{2,1,0:T(8,128)(2,1)S(1)} collective-permute-done((bf16[4,18,32]{2,1,0:T(8,128)(2,1)S(1)}, bf16[4,18,32]{2,1,0:T(8,128)(2,1)S(1)}, u32[]{:S(2)}, u32[]{:S(2)}) %collective-permute-start.5) | collective-permute-done | bytes 4640 | tf_op jit(solution)/shard_map/ppermute | solution.py:106
  35.5 0.2 fusion.47
  35.7 0.3 scatter-add.9
  36.0 0.5 reshape.141
  36.5 3.4 %fusion.4 = bf16[4,8,8,128]{3,2,1,0:T(8,128)(2,1)S(1)} fusion(s32[4096]{0:T(1024)S(1)} %bitcast.93, f32[4096,32]{1,0:T(8,128)S(1)} %reshape.141, f32[32]{0:T(128)S(1)} %copy-done.9), kind=kOutput, calls=%fused_computation.10 | convolution fusion | flops 273088512 | bytes 606336 | tf_op jit(solution)/shard_map/dot_general | solution.py:113
  40.0 0.1 copy.70
  40.1 1.1 %scatter_custom_fusion = bf16[320,256]{1,0:T(8,128)(2,1)S(1)} fusion(s32[128]{0:T(128)S(1)} %get-tuple-element.47, bf16[128,256]{1,0:T(8,128)(2,1)S(1)} %copy.70, bf16[]{:T(256)} %constant.78.clone.1), kind=kCustom, calls=%fused_computation.99 | custom fusion | bytes 163842 | tf_op jit(solution)/shard_map/scatter | solution.py:132
  41.3 0.8 fusion.21
  42.1 13.4 %all-to-all-start = ((bf16[64,6,256]{2,1,0:T(8,128)(2,1)}), bf16[64,6,256]{2,1,0:T(8,128)(2,1)S(1)}, u32[]{:S(2)}, u32[]{:S(2)}) async-start(bf16[64,6,256]{2,1,0:T(8,128)(2,1)} %fusion.21), calls=%async_computation | async-start | bytes 524288 | tf_op jit(solution)/shard_map/all_to_all | solution.py:139
  55.5 13.2 %all-to-all-done = bf16[64,6,256]{2,1,0:T(8,128)(2,1)S(1)} async-done(((bf16[64,6,256]{2,1,0:T(8,128)(2,1)}), bf16[64,6,256]{2,1,0:T(8,128)(2,1)S(1)}, u32[]{:S(2)}, u32[]{:S(2)}) %all-to-all-start) | async-done | bytes 196640 | tf_op jit(solution)/shard_map/all_to_all | solution.py:139
  68.8 0.1 fusion.33
  68.9 0.1 reshape.145
  69.1 0.3 multiply_convert_fusion.1
  69.5 0.4 convolution_bitcast_fusion
  69.8 0.1 select_reduce_fusion.1
  69.9 0.1 all_to_all.10
  70.1 14.2 %all_to_all.14 = f32[64,1,5]{2,1,0:T(1,128)S(1)} all-to-all(f32[64,1,5]{2,1,0:T(1,128)S(1)} %bitcast.86), channel_id=1, replica_groups=mesh['gx'=8,'gy'=8,'gz'=8] {'gx','gy'}, dimensions={0} | all-to-all | bytes 2560 | tf_op jit(solution)/shard_map/all_to_all | solution.py:157
  84.3 0.5 broadcast.119
  84.8 0.7 reduce.11
  85.6 0.1 broadcast_in_dim.55
  85.7 0.6 select_reduce_fusion
  (77 shorter events, 2.3 us)
Async XLA Ops:
  0.0 69.4 %copy-start = (bf16[512,512]{1,0:T(8,128)(2,1)S(1)}, bf16[512,512]{1,0:T(8,128)(2,1)}, u32[]{:S(2)}) copy-start(bf16[512,512]{1,0:T(8,128)(2,1)} %param.23) | copy-start | bytes 1572868
  0.0 8.2 %copy-start.2 = (s32[128,1]{0,1:T(1,128)S(1)}, s32[128,1]{0,1:T(1,128)}, u32[]{:S(2)}) copy-start(s32[128,1]{0,1:T(1,128)} %param.19) | copy-start | bytes 1540
  2.3 14.0 %copy-start.8 = (s32[128]{0:T(128)S(1)}, s32[128]{0:T(128)}, u32[]{:S(2)}) copy-start(s32[128]{0:T(128)} %param.20) | copy-start | bytes 1540
  2.9 7.5 %collective-permute-start = (bf16[1,16,32,128]{3,2,1,0:T(8,128)(2,1)S(1)}, bf16[1,16,32,128]{3,2,1,0:T(8,128)(2,1)S(1)}, u32[]{:S(2)}, u32[]{:S(2)}) collective-permute-start(bf16[1,16,32,128]{3,2,1,0:T(8,128)(2,1)S(1)} %slice.251), channel_id=1, source_target_pairs={{0,64},{64,128},{128,192},{192,256},{256,320},{320,384},{384,448},... | collective-permute-start | bytes 393224 | tf_op jit(solution)/shard_map/ppermute | solution.py:18
  5.8 4.7 %collective-permute-start.1 = (bf16[1,16,32,128]{3,2,1,0:T(8,128)(2,1)}, bf16[1,16,32,128]{3,2,1,0:T(8,128)(2,1)S(1)}, u32[]{:S(2)}, u32[]{:S(2)}) collective-permute-start(bf16[1,16,32,128]{3,2,1,0:T(8,128)(2,1)} %slice.253), channel_id=1, source_target_pairs={{64,0},{128,64},{192,128},{256,192},{320,256},{384,320},{448,384},... | collective-permute-start | bytes 393224 | tf_op jit(solution)/shard_map/ppermute | solution.py:20
  10.6 7.3 %collective-permute-start.2 = (bf16[4,1,32,128]{3,2,1,0:T(8,128)(2,1)S(1)}, bf16[4,1,32,128]{3,2,1,0:T(8,128)(2,1)S(1)}, u32[]{:S(2)}, u32[]{:S(2)}) collective-permute-start(bf16[4,1,32,128]{3,2,1,0:T(8,128)(2,1)S(1)} %get-tuple-element.35), channel_id=1, source_target_pairs={{0,8},{8,16},{16,24},{24,32},{32,40},{40,48},{48,56},{1,9},{9,17},... | collective-permute-start | bytes 98312 | tf_op jit(solution)/shard_map/ppermute | solution.py:18
  14.1 5.8 %collective-permute-start.3 = (bf16[4,1,32,128]{3,2,1,0:T(8,128)(2,1)S(1)}, bf16[4,1,32,128]{3,2,1,0:T(8,128)(2,1)S(1)}, u32[]{:S(2)}, u32[]{:S(2)}) collective-permute-start(bf16[4,1,32,128]{3,2,1,0:T(8,128)(2,1)S(1)} %get-tuple-element.36), channel_id=1, source_target_pairs={{8,0},{16,8},{24,16},{32,24},{40,32},{48,40},{56,48},{9,1},{17,9},... | collective-permute-start | bytes 98312 | tf_op jit(solution)/shard_map/ppermute | solution.py:20
  21.2 9.1 %copy-start.1 = (bf16[3,3,3,128,128]{4,3,2,1,0:T(8,128)(2,1)S(1)}, bf16[3,3,3,128,128]{4,3,2,1,0:T(8,128)(2,1)}, u32[]{:S(2)}) copy-start(bf16[3,3,3,128,128]{4,3,2,1,0:T(8,128)(2,1)} %pad_maximum_fusion) | copy-start | bytes 2654212
  22.9 9.5 %collective-permute-start.4 = (bf16[4,18,32]{2,1,0:T(8,128)(2,1)S(1)}, bf16[4,18,32]{2,1,0:T(8,128)(2,1)S(1)}, u32[]{:S(2)}, u32[]{:S(2)}) collective-permute-start(bf16[4,18,32]{2,1,0:T(8,128)(2,1)S(1)} %copy.66), channel_id=1, source_target_pairs={{0,1},{1,2},{2,3},{3,4},{4,5},{5,6},{6,7},{8,9},{9,10},{10,11},{11... | collective-permute-start | bytes 13832 | tf_op jit(solution)/shard_map/ppermute | solution.py:103
  28.4 6.9 %collective-permute-start.5 = (bf16[4,18,32]{2,1,0:T(8,128)(2,1)S(1)}, bf16[4,18,32]{2,1,0:T(8,128)(2,1)S(1)}, u32[]{:S(2)}, u32[]{:S(2)}) collective-permute-start(bf16[4,18,32]{2,1,0:T(8,128)(2,1)S(1)} %copy.68), channel_id=1, source_target_pairs={{1,0},{2,1},{3,2},{4,3},{5,4},{6,5},{7,6},{9,8},{10,9},{11,10},{12... | collective-permute-start | bytes 13832 | tf_op jit(solution)/shard_map/ppermute | solution.py:106
  30.4 6.2 %copy-start.5 = (s32[2,16,128]{2,1,0:T(8,128)S(1)}, s32[2,16,128]{2,1,0:T(8,128)}, u32[]{:S(2)}) copy-start(s32[2,16,128]{2,1,0:T(8,128)} %param.16) | copy-start | bytes 49156
  30.4 6.2 %copy-start.9 = (f32[32]{0:T(128)S(1)}, f32[32]{0:T(128)}, u32[]{:S(2)}) copy-start(f32[32]{0:T(128)} %param.18) | copy-start | bytes 388
  36.0 19.5 %copy-start.3 = (bf16[512]{0:T(512)(128)(2,1)S(1)}, bf16[512]{0:T(512)(128)(2,1)}, u32[]{:S(2)}) copy-start(bf16[512]{0:T(512)(128)(2,1)} %param.25) | copy-start | bytes 3076
  36.0 33.1 %copy-start.6 = (f32[512]{0:T(512)S(1)}, f32[512]{0:T(512)}, u32[]{:S(2)}) copy-start(f32[512]{0:T(512)} %param.22) | copy-start | bytes 6148
  36.5 32.6 %copy-start.4 = (bf16[256,512]{1,0:T(8,128)(2,1)S(1)}, bf16[256,512]{1,0:T(8,128)(2,1)}, u32[]{:S(2)}) copy-start(bf16[256,512]{1,0:T(8,128)(2,1)} %param.21) | copy-start | bytes 786436
  36.5 32.9 %copy-start.7 = (f32[512]{0:T(512)S(1)}, f32[512]{0:T(512)}, u32[]{:S(2)}) copy-start(f32[512]{0:T(512)} %param.24) | copy-start | bytes 6148
  42.1 26.6 %all-to-all-start = ((bf16[64,6,256]{2,1,0:T(8,128)(2,1)}), bf16[64,6,256]{2,1,0:T(8,128)(2,1)S(1)}, u32[]{:S(2)}, u32[]{:S(2)}) async-start(bf16[64,6,256]{2,1,0:T(8,128)(2,1)} %fusion.21), calls=%async_computation | async-start | bytes 524288 | tf_op jit(solution)/shard_map/all_to_all | solution.py:139

commit v9 on v8

--- a/solution.py
+++ b/solution.py
@@ -124,12 +124,14 @@
     size_gy = lax.axis_size("gy")
     groups = size_gx * size_gy
     capacity = max(2, (5 * pair_count + 2 * groups - 1) // (2 * groups))
+    capacity = max(capacity, 7)
     owners = pair_owner[:, 0]
     owner_marks = (owners[:, None] == lax.iota(jnp.int32, groups)[None, :]).astype(jnp.int32)
     earlier = jnp.cumsum(owner_marks, axis=0) - owner_marks
     slot_rank = jnp.sum(earlier * owner_marks, axis=1)
     target = owners * capacity + slot_rank
-    send_rows = jnp.zeros((groups * capacity, row_width), jnp.bfloat16).at[target].set(pair_rows)
+    placing = (lax.iota(jnp.int32, groups * capacity)[:, None] == target[None, :]).astype(jnp.bfloat16)
+    send_rows = jnp.dot(placing, pair_rows, preferred_element_type=jnp.float32).astype(jnp.bfloat16)
     send_ids = jnp.full((groups * capacity,), -1, jnp.bfloat16).at[target].set(
         pair_edge.astype(jnp.bfloat16)
     )

time: 86.7 us -> 86.2 us (level)
  local copies, waits for them, and re-layouts: 14 us -> 11.9 us
  other arithmetic: 5.16 us -> 6.51 us
    scatter x1 -> x0, local copies, waits for them, and re-layouts: 1.08 us -> none  [body(): jnp.zeros((groups * capacity, row_width), jnp.bfloat16).at[target]]
    reshape x1, local copies, waits for them, and re-layouts: 1.09 us -> 0.16 us  [banded_weight(): conv_weight.reshape(3, 3, 3, channels, channels).transpose(0, 1, 2, 4, 3)]
    unnamed x58 -> x60, local copies, waits for them, and re-layouts: 4.75 us -> 4.75 us
where the time goes in v9:
time: 86.2 us; the launch traced here: 85.8 us
  starting transfers between devices  28.6 us (33%)
  waiting for transfers between devices  17.1 us (20%)
  blocking collectives  14.2 us (16%)
  local copies, waits for them, and re-layouts  11.9 us (14%)
  matrix products  6.7 us (8%)
  other arithmetic  6.51 us (8%)
    all_to_all x1, blocking collectives, body(): lax.all_to_all(owner_scores.reshape(groups, capacity), ('gx', 'gy'), spli...  14.2 us
    all_to_all x1, starting transfers between devices, body(): lax.all_to_all(send, ('gx', 'gy'), split_axis=0, concat_axis=0, tiled=True)  13.4 us
    all_to_all x1, waiting for transfers between devices, body(): lax.all_to_all(send, ('gx', 'gy'), split_axis=0, concat_axis=0, tiled=True)  13.2 us
    ppermute x1, starting transfers between devices, body(): lax.ppermute(padded[:, :, -1, chunk - channels:], 'gz', [(i, i + 1) for i...  5.49 us
    ppermute x2, starting transfers between devices, extended(): lax.ppermute(tail, axis, [(i, (i + 1) % count) for i in range(ends)])  5.23 us
    unnamed x60, local copies, waits for them, and re-layouts  4.75 us
    dot_general x1, matrix products, body(): lax.dot_general(onehot, fields, (((0,), (0,)), ((), ())), preferred_eleme...  3.44 us
    ppermute x2, starting transfers between devices, extended(): lax.ppermute(head, axis, [((i + 1) % count, i) for i in range(ends)])  2.57 us
  transfers between devices with their start and end apart: 7, of which 3 were waited for; matrix products, arithmetic and copies ran while one was open for 12% of the time, Pallas kernels for 0%

profile of v9, /device:TPU:192, one launch (start us, length us, event | category | flops | bytes accessed | tf_op | source)
XLA Modules:
  0.0 85.8 jit_solution(7386563847238595233)
XLA Ops:
  0.0 2.1 %copy.43 = bf16[32,2,16,128]{0,2,3,1:T(8,128)(2,1)S(1)} copy(bf16[32,2,16,128]{3,2,1,0:T(8,128)(2,1)} %param.15) | data formatting | bytes 524288 | tf_op args[0]
  2.1 0.2 fusion.41
  2.3 0.2 copy.44
  2.6 0.3 slice.251
  2.9 1.7 %collective-permute-start = (bf16[1,16,32,128]{3,2,1,0:T(8,128)(2,1)S(1)}, bf16[1,16,32,128]{3,2,1,0:T(8,128)(2,1)S(1)}, u32[]{:S(2)}, u32[]{:S(2)}) collective-permute-start(bf16[1,16,32,128]{3,2,1,0:T(8,128)(2,1)S(1)} %slice.251), channel_id=1, source_target_pairs={{0,64},{64,128},{128,192},{192,256},{256,320},{320,384},{384,448},... | collective-permute-start | bytes 393224 | tf_op jit(solution)/shard_map/ppermute | solution.py:18
  4.6 0.2 copy.46
  4.9 0.9 %slice.253 = bf16[1,16,32,128]{3,2,1,0:T(8,128)(2,1)} reshape(bf16[1,16,32,4,32]{4,3,2,1,0:T(4,128)(2,1)S(1)} %copy.46) | data formatting | bytes 262144 | tf_op jit(solution)/shard_map/slice | solution.py:14
  5.8 1.3 %collective-permute-start.1 = (bf16[1,16,32,128]{3,2,1,0:T(8,128)(2,1)}, bf16[1,16,32,128]{3,2,1,0:T(8,128)(2,1)S(1)}, u32[]{:S(2)}, u32[]{:S(2)}) collective-permute-start(bf16[1,16,32,128]{3,2,1,0:T(8,128)(2,1)} %slice.253), channel_id=1, source_target_pairs={{64,0},{128,64},{192,128},{256,192},{320,256},{384,320},{448,384},... | collective-permute-start | bytes 393224 | tf_op jit(solution)/shard_map/ppermute | solution.py:20
  7.1 0.7 fusion.31
  7.9 0.2 reduce_window_sum.11
  8.0 0.8 select_reduce_fusion.2
  8.9 0.2 copy.47
  9.1 0.3 maximum_bitcast_fusion
  9.5 0.6 copy.45
  10.0 0.5 reshape.144
  10.6 0.2 fusion.11
  10.9 3.5 %collective-permute-start.2 = (bf16[4,1,32,128]{3,2,1,0:T(8,128)(2,1)S(1)}, bf16[4,1,32,128]{3,2,1,0:T(8,128)(2,1)S(1)}, u32[]{:S(2)}, u32[]{:S(2)}) collective-permute-start(bf16[4,1,32,128]{3,2,1,0:T(8,128)(2,1)S(1)} %get-tuple-element.35), channel_id=1, source_target_pairs={{0,8},{8,16},{16,24},{24,32},{32,40},{40,48},{48,56},{1,9},{9,17},... | collective-permute-start | bytes 98312 | tf_op jit(solution)/shard_map/ppermute | solution.py:18
  14.4 1.3 %collective-permute-start.3 = (bf16[4,1,32,128]{3,2,1,0:T(8,128)(2,1)S(1)}, bf16[4,1,32,128]{3,2,1,0:T(8,128)(2,1)S(1)}, u32[]{:S(2)}, u32[]{:S(2)}) collective-permute-start(bf16[4,1,32,128]{3,2,1,0:T(8,128)(2,1)S(1)} %get-tuple-element.36), channel_id=1, source_target_pairs={{8,0},{16,8},{24,16},{32,24},{40,32},{48,40},{56,48},{9,1},{17,9},... | collective-permute-start | bytes 98312 | tf_op jit(solution)/shard_map/ppermute | solution.py:20
  15.7 1.0 %pad_maximum_fusion = bf16[3,3,3,128,128]{4,3,2,1,0:T(8,128)(2,1)} fusion(bf16[3,3,1,128,128]{4,3,2,1,0:T(8,128)(2,1)S(1)} %get-tuple-element.38, bf16[3,3,1,128,128]{4,3,2,1,0:T(8,128)(2,1)S(1)} %maximum_bitcast_fusion, bf16[3,3,1,128,128]{4,3,2,1,0:T(8,128)(2,1)S(1)} %get-tuple-element.41), kind=kLoop, calls=%fused_computation.15 | loop fusion | flops 884736 | bytes 1769472 | tf_op jit(solution)/shard_map/stack | solution.py:46
  16.8 1.3 %scatter_custom_fusion = bf16[448]{0:T(512)(128)(2,1)S(1)} fusion(s32[128]{0:T(128)S(1)} %get-tuple-element.47, bf16[128]{0:T(256)(128)(2,1)S(1)} %convert_element_type.63, bf16[]{:T(256)} %constant.81.clone.1), kind=kCustom, calls=%fused_computation.122 | custom fusion | bytes 898 | tf_op jit(solution)/shard_map/scatter | solution.py:135
  18.1 0.2 reshape.167
  18.3 2.0 %collective-permute-done.3 = bf16[4,1,32,128]{3,2,1,0:T(8,128)(2,1)S(1)} collective-permute-done((bf16[4,1,32,128]{3,2,1,0:T(8,128)(2,1)S(1)}, bf16[4,1,32,128]{3,2,1,0:T(8,128)(2,1)S(1)}, u32[]{:S(2)}, u32[]{:S(2)}) %collective-permute-start.3) | collective-permute-done | bytes 32800 | tf_op jit(solution)/shard_map/ppermute | solution.py:20
  20.3 0.3 fusion.42
  20.6 0.1 slice_dynamic-update-slice_fusion.17
  20.9 0.1 slice_dynamic-update-slice_fusion.15
  21.1 0.1 slice_dynamic-update-slice_fusion.13
  21.4 0.1 slice_dynamic-update-slice_fusion.11
  21.7 0.1 slice_dynamic-update-slice_fusion.9
  22.0 0.1 slice_dynamic-update-slice_fusion.7
  22.3 0.1 slice_dynamic-update-slice_fusion.5
  22.6 0.1 slice_dynamic-update-slice_fusion.3
  22.8 0.1 slice_dynamic-update-slice_fusion.1
  23.1 0.1 pad_maximum_fusion.6
  23.3 5.5 %collective-permute-start.4 = (bf16[4,18,32]{2,1,0:T(8,128)(2,1)S(1)}, bf16[4,18,32]{2,1,0:T(8,128)(2,1)S(1)}, u32[]{:S(2)}, u32[]{:S(2)}) collective-permute-start(bf16[4,18,32]{2,1,0:T(8,128)(2,1)S(1)} %copy.51), channel_id=1, source_target_pairs={{0,1},{1,2},{2,3},{3,4},{4,5},{5,6},{6,7},{8,9},{9,10},{10,11},{11... | collective-permute-start | bytes 13832 | tf_op jit(solution)/shard_map/ppermute | solution.py:103
  28.8 1.9 %collective-permute-start.5 = (bf16[4,18,32]{2,1,0:T(8,128)(2,1)S(1)}, bf16[4,18,32]{2,1,0:T(8,128)(2,1)S(1)}, u32[]{:S(2)}, u32[]{:S(2)}) collective-permute-start(bf16[4,18,32]{2,1,0:T(8,128)(2,1)S(1)} %copy.53), channel_id=1, source_target_pairs={{1,0},{2,1},{3,2},{4,3},{5,4},{6,5},{7,6},{9,8},{10,9},{11,10},{12... | collective-permute-start | bytes 13832 | tf_op jit(solution)/shard_map/ppermute | solution.py:106
  30.8 2.0 %fusion.44 = f32[2,16,32,128]{3,2,1,0:T(8,128)S(1)} fusion(bf16[2,16,32,3456]{3,2,1,0:T(8,128)(2,1)S(1)} %slice_dynamic-update-slice_fusion, bf16[3456,128,1,1]{1,0,3,2:T(8,128)(2,1)S(1)} %bitcast.84), kind=kOutput, calls=%fused_computation.133 | convolution fusion | flops 905969664 | bytes 8486912 | tf_op jit(solution)/shard_map/dot_general | solution.py:65
  32.9 0.1 constant_dynamic-update-slice_fusion.11
  32.9 0.1 constant_dynamic-update-slice_fusion.10
  33.1 0.1 constant_dynamic-update-slice_fusion.8
  33.2 0.1 constant_dynamic-update-slice_fusion.7
  33.4 0.1 constant_dynamic-update-slice_fusion.5
  33.5 0.1 constant_dynamic-update-slice_fusion.4
  33.5 0.2 fusion.45
  33.8 0.1 scatter-add.6
  33.9 1.9 %collective-permute-done.5 = bf16[4,18,32]{2,1,0:T(8,128)(2,1)S(1)} collective-permute-done((bf16[4,18,32]{2,1,0:T(8,128)(2,1)S(1)}, bf16[4,18,32]{2,1,0:T(8,128)(2,1)S(1)}, u32[]{:S(2)}, u32[]{:S(2)}) %collective-permute-start.5) | collective-permute-done | bytes 4640 | tf_op jit(solution)/shard_map/ppermute | solution.py:106
  35.9 0.2 fusion.46
  36.1 0.3 scatter-add.9
  36.4 0.5 reshape.149
  36.9 3.4 %fusion.4 = bf16[4,8,8,128]{3,2,1,0:T(8,128)(2,1)S(1)} fusion(s32[4096]{0:T(1024)S(1)} %bitcast.95, f32[4096,32]{1,0:T(8,128)S(1)} %reshape.149, f32[32]{0:T(128)S(1)} %copy-done.10), kind=kOutput, calls=%fused_computation.10 | convolution fusion | flops 273088512 | bytes 606336 | tf_op jit(solution)/shard_map/dot_general | solution.py:113
  40.4 0.2 convolution_convert_fusion
  40.7 0.8 fusion.21
  41.5 13.4 %all-to-all-start = ((bf16[64,8,256]{2,1,0:T(8,128)(2,1)}), bf16[64,8,256]{2,1,0:T(8,128)(2,1)S(1)}, u32[]{:S(2)}, u32[]{:S(2)}) async-start(bf16[64,8,256]{2,1,0:T(8,128)(2,1)} %fusion.21), calls=%async_computation | async-start | bytes 524288 | tf_op jit(solution)/shard_map/all_to_all | solution.py:141
  55.0 13.2 %all-to-all-done = bf16[64,8,256]{2,1,0:T(8,128)(2,1)S(1)} async-done(((bf16[64,8,256]{2,1,0:T(8,128)(2,1)}), bf16[64,8,256]{2,1,0:T(8,128)(2,1)S(1)}, u32[]{:S(2)}, u32[]{:S(2)}) %all-to-all-start) | async-done | bytes 262176 | tf_op jit(solution)/shard_map/all_to_all | solution.py:141
  68.3 0.1 fusion.32
  68.4 0.1 reshape.153
  68.6 0.4 multiply_convert_fusion.1
  68.9 0.4 convolution_bitcast_fusion
  69.3 0.1 select_reduce_fusion.1
  69.4 0.1 all_to_all.10
  69.5 14.2 %all_to_all.14 = f32[64,1,7]{2,1,0:T(1,128)S(1)} all-to-all(f32[64,1,7]{2,1,0:T(1,128)S(1)} %bitcast.88), channel_id=1, replica_groups=mesh['gx'=8,'gy'=8,'gz'=8] {'gx','gy'}, dimensions={0} | all-to-all | bytes 3584 | tf_op jit(solution)/shard_map/all_to_all | solution.py:159
  83.8 0.5 broadcast.113
  84.3 0.7 reduce.11
  85.0 0.1 broadcast_in_dim.52
  85.2 0.7 select_reduce_fusion
  (79 shorter events, 2.2 us)
Async XLA Ops:
  0.0 68.9 %copy-start = (bf16[512,512]{1,0:T(8,128)(2,1)S(1)}, bf16[512,512]{1,0:T(8,128)(2,1)}, u32[]{:S(2)}) copy-start(bf16[512,512]{1,0:T(8,128)(2,1)} %param.23) | copy-start | bytes 1572868
  0.0 8.9 %copy-start.3 = (s32[128,1]{0,1:T(1,128)S(1)}, s32[128,1]{0,1:T(1,128)}, u32[]{:S(2)}) copy-start(s32[128,1]{0,1:T(1,128)} %param.19) | copy-start | bytes 1540
  0.0 8.9 %copy-start.2 = (bf16[27,32,32]{2,1,0:T(8,128)(2,1)S(1)}, bf16[27,32,32]{2,1,0:T(8,128)(2,1)}, u32[]{:S(2)}) copy-start(bf16[27,32,32]{2,1,0:T(8,128)(2,1)} %param.17) | copy-start | bytes 165892
  2.3 14.4 %copy-start.9 = (s32[128]{0:T(128)S(1)}, s32[128]{0:T(128)}, u32[]{:S(2)}) copy-start(s32[128]{0:T(128)} %param.20) | copy-start | bytes 1540
  2.9 7.9 %collective-permute-start = (bf16[1,16,32,128]{3,2,1,0:T(8,128)(2,1)S(1)}, bf16[1,16,32,128]{3,2,1,0:T(8,128)(2,1)S(1)}, u32[]{:S(2)}, u32[]{:S(2)}) collective-permute-start(bf16[1,16,32,128]{3,2,1,0:T(8,128)(2,1)S(1)} %slice.251), channel_id=1, source_target_pairs={{0,64},{64,128},{128,192},{192,256},{256,320},{320,384},{384,448},... | collective-permute-start | bytes 393224 | tf_op jit(solution)/shard_map/ppermute | solution.py:18
  5.8 5.1 %collective-permute-start.1 = (bf16[1,16,32,128]{3,2,1,0:T(8,128)(2,1)}, bf16[1,16,32,128]{3,2,1,0:T(8,128)(2,1)S(1)}, u32[]{:S(2)}, u32[]{:S(2)}) collective-permute-start(bf16[1,16,32,128]{3,2,1,0:T(8,128)(2,1)} %slice.253), channel_id=1, source_target_pairs={{64,0},{128,64},{192,128},{256,192},{320,256},{384,320},{448,384},... | collective-permute-start | bytes 393224 | tf_op jit(solution)/shard_map/ppermute | solution.py:20
  10.9 7.3 %collective-permute-start.2 = (bf16[4,1,32,128]{3,2,1,0:T(8,128)(2,1)S(1)}, bf16[4,1,32,128]{3,2,1,0:T(8,128)(2,1)S(1)}, u32[]{:S(2)}, u32[]{:S(2)}) collective-permute-start(bf16[4,1,32,128]{3,2,1,0:T(8,128)(2,1)S(1)} %get-tuple-element.35), channel_id=1, source_target_pairs={{0,8},{8,16},{16,24},{24,32},{32,40},{40,48},{48,56},{1,9},{9,17},... | collective-permute-start | bytes 98312 | tf_op jit(solution)/shard_map/ppermute | solution.py:18
  14.4 5.8 %collective-permute-start.3 = (bf16[4,1,32,128]{3,2,1,0:T(8,128)(2,1)S(1)}, bf16[4,1,32,128]{3,2,1,0:T(8,128)(2,1)S(1)}, u32[]{:S(2)}, u32[]{:S(2)}) collective-permute-start(bf16[4,1,32,128]{3,2,1,0:T(8,128)(2,1)S(1)} %get-tuple-element.36), channel_id=1, source_target_pairs={{8,0},{16,8},{24,16},{32,24},{40,32},{48,40},{56,48},{9,1},{17,9},... | collective-permute-start | bytes 98312 | tf_op jit(solution)/shard_map/ppermute | solution.py:20
  21.6 9.1 %copy-start.1 = (bf16[3,3,3,128,128]{4,3,2,1,0:T(8,128)(2,1)S(1)}, bf16[3,3,3,128,128]{4,3,2,1,0:T(8,128)(2,1)}, u32[]{:S(2)}) copy-start(bf16[3,3,3,128,128]{4,3,2,1,0:T(8,128)(2,1)} %pad_maximum_fusion) | copy-start | bytes 2654212
  23.3 9.5 %collective-permute-start.4 = (bf16[4,18,32]{2,1,0:T(8,128)(2,1)S(1)}, bf16[4,18,32]{2,1,0:T(8,128)(2,1)S(1)}, u32[]{:S(2)}, u32[]{:S(2)}) collective-permute-start(bf16[4,18,32]{2,1,0:T(8,128)(2,1)S(1)} %copy.51), channel_id=1, source_target_pairs={{0,1},{1,2},{2,3},{3,4},{4,5},{5,6},{6,7},{8,9},{9,10},{10,11},{11... | collective-permute-start | bytes 13832 | tf_op jit(solution)/shard_map/ppermute | solution.py:103
  28.8 6.9 %collective-permute-start.5 = (bf16[4,18,32]{2,1,0:T(8,128)(2,1)S(1)}, bf16[4,18,32]{2,1,0:T(8,128)(2,1)S(1)}, u32[]{:S(2)}, u32[]{:S(2)}) collective-permute-start(bf16[4,18,32]{2,1,0:T(8,128)(2,1)S(1)} %copy.53), channel_id=1, source_target_pairs={{1,0},{2,1},{3,2},{4,3},{5,4},{6,5},{7,6},{9,8},{10,9},{11,10},{12... | collective-permute-start | bytes 13832 | tf_op jit(solution)/shard_map/ppermute | solution.py:106
  30.8 6.2 %copy-start.6 = (s32[2,16,128]{2,1,0:T(8,128)S(1)}, s32[2,16,128]{2,1,0:T(8,128)}, u32[]{:S(2)}) copy-start(s32[2,16,128]{2,1,0:T(8,128)} %param.16) | copy-start | bytes 49156
  30.8 6.2 %copy-start.10 = (f32[32]{0:T(128)S(1)}, f32[32]{0:T(128)}, u32[]{:S(2)}) copy-start(f32[32]{0:T(128)} %param.18) | copy-start | bytes 388
  36.4 18.6 %copy-start.4 = (bf16[512]{0:T(512)(128)(2,1)S(1)}, bf16[512]{0:T(512)(128)(2,1)}, u32[]{:S(2)}) copy-start(bf16[512]{0:T(512)(128)(2,1)} %param.25) | copy-start | bytes 3076
  36.4 32.1 %copy-start.7 = (f32[512]{0:T(512)S(1)}, f32[512]{0:T(512)}, u32[]{:S(2)}) copy-start(f32[512]{0:T(512)} %param.22) | copy-start | bytes 6148
  36.9 31.7 %copy-start.5 = (bf16[256,512]{1,0:T(8,128)(2,1)S(1)}, bf16[256,512]{1,0:T(8,128)(2,1)}, u32[]{:S(2)}) copy-start(bf16[256,512]{1,0:T(8,128)(2,1)} %param.21) | copy-start | bytes 786436
  36.9 32.0 %copy-start.8 = (f32[512]{0:T(512)S(1)}, f32[512]{0:T(512)}, u32[]{:S(2)}) copy-start(f32[512]{0:T(512)} %param.24) | copy-start | bytes 6148
  41.5 26.6 %all-to-all-start = ((bf16[64,8,256]{2,1,0:T(8,128)(2,1)}), bf16[64,8,256]{2,1,0:T(8,128)(2,1)S(1)}, u32[]{:S(2)}, u32[]{:S(2)}) async-start(bf16[64,8,256]{2,1,0:T(8,128)(2,1)} %fusion.21), calls=%async_computation | async-start | bytes 524288 | tf_op jit(solution)/shard_map/all_to_all | solution.py:141

commit v10 on v9

--- a/solution.py
+++ b/solution.py
@@ -155,12 +155,14 @@
     ).astype(jnp.bfloat16)
     edge_scores = jnp.dot(second, mlp_out, preferred_element_type=jnp.float32)
     owner_picks = flat_ids[:, None] == lax.iota(jnp.int32, edge_count)[None, :]
-    owner_scores = jnp.sum(jnp.where(owner_picks, edge_scores[None, :], 0.0), axis=1)
+    owner_scores = jnp.dot(
+        owner_picks.astype(jnp.float32), edge_scores, precision=lax.Precision.HIGHEST
+    )
     returned = lax.all_to_all(
         owner_scores.reshape(groups, capacity), ("gx", "gy"), split_axis=0, concat_axis=0, tiled=True
     ).reshape(groups * capacity)
     back_picks = target[:, None] == lax.iota(jnp.int32, groups * capacity)[None, :]
-    return jnp.sum(jnp.where(back_picks, returned[None, :], 0.0), axis=1)
+    return jnp.dot(back_picks.astype(jnp.float32), returned, precision=lax.Precision.HIGHEST)
 
 
 def solution(mesh):

time: 86.2 us -> 86.6 us (level)
  matrix products: 6.7 us -> 7.8 us
    dot_general x0 -> x2, matrix products: none -> 1.1 us  [the longest x1 0.82 us: body(): jnp.dot(back_picks.astype(jnp.float32), returned, precision=lax.Precision...]
where the time goes in v10:
time: 86.6 us; the launch traced here: 86.2 us
  starting transfers between devices  28.6 us (33%)
  waiting for transfers between devices  17.1 us (20%)
  blocking collectives  14.2 us (16%)
  local copies, waits for them, and re-layouts  11.9 us (14%)
  matrix products  7.8 us (9%)
  other arithmetic  5.75 us (7%)
    all_to_all x1, blocking collectives, body(): lax.all_to_all(owner_scores.reshape(groups, capacity), ('gx', 'gy'), spli...  14.2 us
    all_to_all x1, starting transfers between devices, body(): lax.all_to_all(send, ('gx', 'gy'), split_axis=0, concat_axis=0, tiled=True)  13.4 us
    all_to_all x1, waiting for transfers between devices, body(): lax.all_to_all(send, ('gx', 'gy'), split_axis=0, concat_axis=0, tiled=True)  13.2 us
    ppermute x1, starting transfers between devices, body(): lax.ppermute(padded[:, :, -1, chunk - channels:], 'gz', [(i, i + 1) for i...  5.49 us
    ppermute x2, starting transfers between devices, extended(): lax.ppermute(tail, axis, [(i, (i + 1) % count) for i in range(ends)])  5.23 us
    unnamed x60, local copies, waits for them, and re-layouts  4.75 us
    dot_general x1, matrix products, body(): lax.dot_general(onehot, fields, (((0,), (0,)), ((), ())), preferred_eleme...  3.44 us
    ppermute x2, starting transfers between devices, extended(): lax.ppermute(head, axis, [((i + 1) % count, i) for i in range(ends)])  2.57 us
  transfers between devices with their start and end apart: 7, of which 3 were waited for; matrix products, arithmetic and copies ran while one was open for 12% of the time, Pallas kernels for 0%

profile of v10, /device:TPU:192, one launch (start us, length us, event | category | flops | bytes accessed | tf_op | source)
XLA Modules:
  0.0 86.2 jit_solution(5925642818314350141)
XLA Ops:
  0.0 2.1 %copy.29 = bf16[32,2,16,128]{0,2,3,1:T(8,128)(2,1)S(1)} copy(bf16[32,2,16,128]{3,2,1,0:T(8,128)(2,1)} %param.15) | data formatting | bytes 524288 | tf_op args[0]
  2.1 0.2 fusion.44
  2.3 0.2 copy.30
  2.6 0.3 slice.251
  2.9 1.7 %collective-permute-start = (bf16[1,16,32,128]{3,2,1,0:T(8,128)(2,1)S(1)}, bf16[1,16,32,128]{3,2,1,0:T(8,128)(2,1)S(1)}, u32[]{:S(2)}, u32[]{:S(2)}) collective-permute-start(bf16[1,16,32,128]{3,2,1,0:T(8,128)(2,1)S(1)} %slice.251), channel_id=1, source_target_pairs={{0,64},{64,128},{128,192},{192,256},{256,320},{320,384},{384,448},... | collective-permute-start | bytes 393224 | tf_op jit(solution)/shard_map/ppermute | solution.py:18
  4.6 0.2 copy.32
  4.9 0.9 %slice.253 = bf16[1,16,32,128]{3,2,1,0:T(8,128)(2,1)} reshape(bf16[1,16,32,4,32]{4,3,2,1,0:T(4,128)(2,1)S(1)} %copy.32) | data formatting | bytes 262144 | tf_op jit(solution)/shard_map/slice | solution.py:14
  5.8 1.3 %collective-permute-start.1 = (bf16[1,16,32,128]{3,2,1,0:T(8,128)(2,1)}, bf16[1,16,32,128]{3,2,1,0:T(8,128)(2,1)S(1)}, u32[]{:S(2)}, u32[]{:S(2)}) collective-permute-start(bf16[1,16,32,128]{3,2,1,0:T(8,128)(2,1)} %slice.253), channel_id=1, source_target_pairs={{64,0},{128,64},{192,128},{256,192},{320,256},{384,320},{448,384},... | collective-permute-start | bytes 393224 | tf_op jit(solution)/shard_map/ppermute | solution.py:20
  7.1 0.7 fusion.34
  7.9 0.2 reduce_window_sum.11
  8.0 0.8 select_reduce_fusion
  8.9 0.2 copy.33
  9.1 0.3 maximum_bitcast_fusion
  9.5 0.6 copy.31
  10.0 0.5 reshape.145
  10.6 0.2 fusion.11
  11.0 3.5 %collective-permute-start.2 = (bf16[4,1,32,128]{3,2,1,0:T(8,128)(2,1)S(1)}, bf16[4,1,32,128]{3,2,1,0:T(8,128)(2,1)S(1)}, u32[]{:S(2)}, u32[]{:S(2)}) collective-permute-start(bf16[4,1,32,128]{3,2,1,0:T(8,128)(2,1)S(1)} %get-tuple-element.35), channel_id=1, source_target_pairs={{0,8},{8,16},{16,24},{24,32},{32,40},{40,48},{48,56},{1,9},{9,17},... | collective-permute-start | bytes 98312 | tf_op jit(solution)/shard_map/ppermute | solution.py:18
  14.4 1.3 %collective-permute-start.3 = (bf16[4,1,32,128]{3,2,1,0:T(8,128)(2,1)S(1)}, bf16[4,1,32,128]{3,2,1,0:T(8,128)(2,1)S(1)}, u32[]{:S(2)}, u32[]{:S(2)}) collective-permute-start(bf16[4,1,32,128]{3,2,1,0:T(8,128)(2,1)S(1)} %get-tuple-element.36), channel_id=1, source_target_pairs={{8,0},{16,8},{24,16},{32,24},{40,32},{48,40},{56,48},{9,1},{17,9},... | collective-permute-start | bytes 98312 | tf_op jit(solution)/shard_map/ppermute | solution.py:20
  15.7 1.0 %pad_maximum_fusion = bf16[3,3,3,128,128]{4,3,2,1,0:T(8,128)(2,1)} fusion(bf16[3,3,1,128,128]{4,3,2,1,0:T(8,128)(2,1)S(1)} %get-tuple-element.38, bf16[3,3,1,128,128]{4,3,2,1,0:T(8,128)(2,1)S(1)} %maximum_bitcast_fusion, bf16[3,3,1,128,128]{4,3,2,1,0:T(8,128)(2,1)S(1)} %get-tuple-element.41), kind=kLoop, calls=%fused_computation.16 | loop fusion | flops 884736 | bytes 1769472 | tf_op jit(solution)/shard_map/stack | solution.py:46
  16.8 1.3 %scatter_custom_fusion = bf16[448]{0:T(512)(128)(2,1)S(1)} fusion(s32[128]{0:T(128)S(1)} %get-tuple-element.47, bf16[128]{0:T(256)(128)(2,1)S(1)} %convert_element_type.65, bf16[]{:T(256)} %constant.80.clone.1), kind=kCustom, calls=%fused_computation.124 | custom fusion | bytes 898 | tf_op jit(solution)/shard_map/scatter | solution.py:135
  18.1 0.2 reshape.173
  18.3 2.0 %collective-permute-done.3 = bf16[4,1,32,128]{3,2,1,0:T(8,128)(2,1)S(1)} collective-permute-done((bf16[4,1,32,128]{3,2,1,0:T(8,128)(2,1)S(1)}, bf16[4,1,32,128]{3,2,1,0:T(8,128)(2,1)S(1)}, u32[]{:S(2)}, u32[]{:S(2)}) %collective-permute-start.3) | collective-permute-done | bytes 32800 | tf_op jit(solution)/shard_map/ppermute | solution.py:20
  20.3 0.3 fusion.45
  20.6 0.1 slice_dynamic-update-slice_fusion.17
  20.9 0.1 slice_dynamic-update-slice_fusion.15
  21.1 0.1 slice_dynamic-update-slice_fusion.13
  21.4 0.1 slice_dynamic-update-slice_fusion.11
  21.7 0.1 slice_dynamic-update-slice_fusion.9
  22.0 0.1 slice_dynamic-update-slice_fusion.7
  22.3 0.1 slice_dynamic-update-slice_fusion.5
  22.6 0.1 slice_dynamic-update-slice_fusion.3
  22.8 0.1 slice_dynamic-update-slice_fusion.1
  23.1 0.1 pad_maximum_fusion.6
  23.3 5.5 %collective-permute-start.4 = (bf16[4,18,32]{2,1,0:T(8,128)(2,1)S(1)}, bf16[4,18,32]{2,1,0:T(8,128)(2,1)S(1)}, u32[]{:S(2)}, u32[]{:S(2)}) collective-permute-start(bf16[4,18,32]{2,1,0:T(8,128)(2,1)S(1)} %copy.37), channel_id=1, source_target_pairs={{0,1},{1,2},{2,3},{3,4},{4,5},{5,6},{6,7},{8,9},{9,10},{10,11},{11... | collective-permute-start | bytes 13832 | tf_op jit(solution)/shard_map/ppermute | solution.py:103
  28.8 1.9 %collective-permute-start.5 = (bf16[4,18,32]{2,1,0:T(8,128)(2,1)S(1)}, bf16[4,18,32]{2,1,0:T(8,128)(2,1)S(1)}, u32[]{:S(2)}, u32[]{:S(2)}) collective-permute-start(bf16[4,18,32]{2,1,0:T(8,128)(2,1)S(1)} %copy.39), channel_id=1, source_target_pairs={{1,0},{2,1},{3,2},{4,3},{5,4},{6,5},{7,6},{9,8},{10,9},{11,10},{12... | collective-permute-start | bytes 13832 | tf_op jit(solution)/shard_map/ppermute | solution.py:106
  30.8 2.0 %fusion.47 = f32[2,16,32,128]{3,2,1,0:T(8,128)S(1)} fusion(bf16[2,16,32,3456]{3,2,1,0:T(8,128)(2,1)S(1)} %slice_dynamic-update-slice_fusion, bf16[3456,128,1,1]{1,0,3,2:T(8,128)(2,1)S(1)} %bitcast.90), kind=kOutput, calls=%fused_computation.135 | convolution fusion | flops 905969664 | bytes 8486912 | tf_op jit(solution)/shard_map/dot_general | solution.py:65
  32.9 0.1 constant_dynamic-update-slice_fusion.11
  32.9 0.1 constant_dynamic-update-slice_fusion.10
  33.1 0.1 constant_dynamic-update-slice_fusion.8
  33.2 0.1 constant_dynamic-update-slice_fusion.7
  33.4 0.1 constant_dynamic-update-slice_fusion.5
  33.5 0.1 constant_dynamic-update-slice_fusion.4
  33.5 0.2 fusion.48
  33.8 0.1 scatter-add.6
  33.9 1.9 %collective-permute-done.5 = bf16[4,18,32]{2,1,0:T(8,128)(2,1)S(1)} collective-permute-done((bf16[4,18,32]{2,1,0:T(8,128)(2,1)S(1)}, bf16[4,18,32]{2,1,0:T(8,128)(2,1)S(1)}, u32[]{:S(2)}, u32[]{:S(2)}) %collective-permute-start.5) | collective-permute-done | bytes 4640 | tf_op jit(solution)/shard_map/ppermute | solution.py:106
  35.9 0.2 fusion.49
  36.1 0.3 scatter-add.9
  36.4 0.5 reshape.150
  36.9 3.4 %fusion.4 = bf16[4,8,8,128]{3,2,1,0:T(8,128)(2,1)S(1)} fusion(s32[4096]{0:T(1024)S(1)} %bitcast.102, f32[4096,32]{1,0:T(8,128)S(1)} %reshape.150, f32[32]{0:T(128)S(1)} %copy-done.10), kind=kOutput, calls=%fused_computation.10 | convolution fusion | flops 273088512 | bytes 606336 | tf_op jit(solution)/shard_map/dot_general | solution.py:113
  40.4 0.2 convolution_convert_fusion
  40.7 0.8 fusion.21
  41.5 13.4 %all-to-all-start = ((bf16[64,8,256]{2,1,0:T(8,128)(2,1)}), bf16[64,8,256]{2,1,0:T(8,128)(2,1)S(1)}, u32[]{:S(2)}, u32[]{:S(2)}) async-start(bf16[64,8,256]{2,1,0:T(8,128)(2,1)} %fusion.21), calls=%async_computation | async-start | bytes 524288 | tf_op jit(solution)/shard_map/all_to_all | solution.py:141
  55.0 13.2 %all-to-all-done = bf16[64,8,256]{2,1,0:T(8,128)(2,1)S(1)} async-done(((bf16[64,8,256]{2,1,0:T(8,128)(2,1)}), bf16[64,8,256]{2,1,0:T(8,128)(2,1)S(1)}, u32[]{:S(2)}, u32[]{:S(2)}) %all-to-all-start) | async-done | bytes 262176 | tf_op jit(solution)/shard_map/all_to_all | solution.py:141
  68.3 0.1 fusion.35
  68.4 0.1 reshape.155
  68.6 0.4 multiply_convert_fusion.1
  69.0 0.4 convolution_bitcast_fusion.1
  69.3 0.3 fusion.26
  69.6 0.2 all_to_all.10
  69.8 14.2 %all_to_all.14 = f32[64,1,7]{2,1,0:T(1,128)S(1)} all-to-all(f32[64,1,7]{2,1,0:T(1,128)S(1)} %bitcast.94), channel_id=1, replica_groups=mesh['gx'=8,'gy'=8,'gz'=8] {'gx','gy'}, dimensions={0} | all-to-all | bytes 3584 | tf_op jit(solution)/shard_map/all_to_all | solution.py:161
  84.0 0.5 broadcast.112
  84.5 0.7 reduce.11
  85.3 0.1 reshape.171
  85.4 0.8 convolution_bitcast_fusion
  (79 shorter events, 2.2 us)
Async XLA Ops:
  0.0 68.9 %copy-start = (bf16[512,512]{1,0:T(8,128)(2,1)S(1)}, bf16[512,512]{1,0:T(8,128)(2,1)}, u32[]{:S(2)}) copy-start(bf16[512,512]{1,0:T(8,128)(2,1)} %param.23) | copy-start | bytes 1572868
  0.0 8.9 %copy-start.3 = (s32[128,1]{0,1:T(1,128)S(1)}, s32[128,1]{0,1:T(1,128)}, u32[]{:S(2)}) copy-start(s32[128,1]{0,1:T(1,128)} %param.19) | copy-start | bytes 1540
  0.0 8.9 %copy-start.2 = (bf16[27,32,32]{2,1,0:T(8,128)(2,1)S(1)}, bf16[27,32,32]{2,1,0:T(8,128)(2,1)}, u32[]{:S(2)}) copy-start(bf16[27,32,32]{2,1,0:T(8,128)(2,1)} %param.17) | copy-start | bytes 165892
  2.3 14.4 %copy-start.9 = (s32[128]{0:T(128)S(1)}, s32[128]{0:T(128)}, u32[]{:S(2)}) copy-start(s32[128]{0:T(128)} %param.20) | copy-start | bytes 1540
  2.9 7.9 %collective-permute-start = (bf16[1,16,32,128]{3,2,1,0:T(8,128)(2,1)S(1)}, bf16[1,16,32,128]{3,2,1,0:T(8,128)(2,1)S(1)}, u32[]{:S(2)}, u32[]{:S(2)}) collective-permute-start(bf16[1,16,32,128]{3,2,1,0:T(8,128)(2,1)S(1)} %slice.251), channel_id=1, source_target_pairs={{0,64},{64,128},{128,192},{192,256},{256,320},{320,384},{384,448},... | collective-permute-start | bytes 393224 | tf_op jit(solution)/shard_map/ppermute | solution.py:18
  5.8 5.1 %collective-permute-start.1 = (bf16[1,16,32,128]{3,2,1,0:T(8,128)(2,1)}, bf16[1,16,32,128]{3,2,1,0:T(8,128)(2,1)S(1)}, u32[]{:S(2)}, u32[]{:S(2)}) collective-permute-start(bf16[1,16,32,128]{3,2,1,0:T(8,128)(2,1)} %slice.253), channel_id=1, source_target_pairs={{64,0},{128,64},{192,128},{256,192},{320,256},{384,320},{448,384},... | collective-permute-start | bytes 393224 | tf_op jit(solution)/shard_map/ppermute | solution.py:20
  11.0 7.3 %collective-permute-start.2 = (bf16[4,1,32,128]{3,2,1,0:T(8,128)(2,1)S(1)}, bf16[4,1,32,128]{3,2,1,0:T(8,128)(2,1)S(1)}, u32[]{:S(2)}, u32[]{:S(2)}) collective-permute-start(bf16[4,1,32,128]{3,2,1,0:T(8,128)(2,1)S(1)} %get-tuple-element.35), channel_id=1, source_target_pairs={{0,8},{8,16},{16,24},{24,32},{32,40},{40,48},{48,56},{1,9},{9,17},... | collective-permute-start | bytes 98312 | tf_op jit(solution)/shard_map/ppermute | solution.py:18
  14.4 5.8 %collective-permute-start.3 = (bf16[4,1,32,128]{3,2,1,0:T(8,128)(2,1)S(1)}, bf16[4,1,32,128]{3,2,1,0:T(8,128)(2,1)S(1)}, u32[]{:S(2)}, u32[]{:S(2)}) collective-permute-start(bf16[4,1,32,128]{3,2,1,0:T(8,128)(2,1)S(1)} %get-tuple-element.36), channel_id=1, source_target_pairs={{8,0},{16,8},{24,16},{32,24},{40,32},{48,40},{56,48},{9,1},{17,9},... | collective-permute-start | bytes 98312 | tf_op jit(solution)/shard_map/ppermute | solution.py:20
  21.6 9.1 %copy-start.1 = (bf16[3,3,3,128,128]{4,3,2,1,0:T(8,128)(2,1)S(1)}, bf16[3,3,3,128,128]{4,3,2,1,0:T(8,128)(2,1)}, u32[]{:S(2)}) copy-start(bf16[3,3,3,128,128]{4,3,2,1,0:T(8,128)(2,1)} %pad_maximum_fusion) | copy-start | bytes 2654212
  23.3 9.5 %collective-permute-start.4 = (bf16[4,18,32]{2,1,0:T(8,128)(2,1)S(1)}, bf16[4,18,32]{2,1,0:T(8,128)(2,1)S(1)}, u32[]{:S(2)}, u32[]{:S(2)}) collective-permute-start(bf16[4,18,32]{2,1,0:T(8,128)(2,1)S(1)} %copy.37), channel_id=1, source_target_pairs={{0,1},{1,2},{2,3},{3,4},{4,5},{5,6},{6,7},{8,9},{9,10},{10,11},{11... | collective-permute-start | bytes 13832 | tf_op jit(solution)/shard_map/ppermute | solution.py:103
  28.8 6.9 %collective-permute-start.5 = (bf16[4,18,32]{2,1,0:T(8,128)(2,1)S(1)}, bf16[4,18,32]{2,1,0:T(8,128)(2,1)S(1)}, u32[]{:S(2)}, u32[]{:S(2)}) collective-permute-start(bf16[4,18,32]{2,1,0:T(8,128)(2,1)S(1)} %copy.39), channel_id=1, source_target_pairs={{1,0},{2,1},{3,2},{4,3},{5,4},{6,5},{7,6},{9,8},{10,9},{11,10},{12... | collective-permute-start | bytes 13832 | tf_op jit(solution)/shard_map/ppermute | solution.py:106
  30.8 6.2 %copy-start.6 = (s32[2,16,128]{2,1,0:T(8,128)S(1)}, s32[2,16,128]{2,1,0:T(8,128)}, u32[]{:S(2)}) copy-start(s32[2,16,128]{2,1,0:T(8,128)} %param.16) | copy-start | bytes 49156
  30.8 6.2 %copy-start.10 = (f32[32]{0:T(128)S(1)}, f32[32]{0:T(128)}, u32[]{:S(2)}) copy-start(f32[32]{0:T(128)} %param.18) | copy-start | bytes 388
  36.4 18.6 %copy-start.4 = (bf16[512]{0:T(512)(128)(2,1)S(1)}, bf16[512]{0:T(512)(128)(2,1)}, u32[]{:S(2)}) copy-start(bf16[512]{0:T(512)(128)(2,1)} %param.25) | copy-start | bytes 3076
  36.4 32.2 %copy-start.7 = (f32[512]{0:T(512)S(1)}, f32[512]{0:T(512)}, u32[]{:S(2)}) copy-start(f32[512]{0:T(512)} %param.22) | copy-start | bytes 6148
  36.9 31.7 %copy-start.5 = (bf16[256,512]{1,0:T(8,128)(2,1)S(1)}, bf16[256,512]{1,0:T(8,128)(2,1)}, u32[]{:S(2)}) copy-start(bf16[256,512]{1,0:T(8,128)(2,1)} %param.21) | copy-start | bytes 786436
  36.9 32.0 %copy-start.8 = (f32[512]{0:T(512)S(1)}, f32[512]{0:T(512)}, u32[]{:S(2)}) copy-start(f32[512]{0:T(512)} %param.24) | copy-start | bytes 6148
  41.5 26.7 %all-to-all-start = ((bf16[64,8,256]{2,1,0:T(8,128)(2,1)}), bf16[64,8,256]{2,1,0:T(8,128)(2,1)S(1)}, u32[]{:S(2)}, u32[]{:S(2)}) async-start(bf16[64,8,256]{2,1,0:T(8,128)(2,1)} %fusion.21), calls=%async_computation | async-start | bytes 524288 | tf_op jit(solution)/shard_map/all_to_all | solution.py:141

commit v11 on v9

--- a/solution.py
+++ b/solution.py
@@ -109,17 +109,18 @@
     pair_count = pair_edge.shape[0]
     slot_count = pair_count * BINS
     slots_flat = voxel_slot.reshape(volume)
-    onehot = (slots_flat[:, None] == lax.iota(jnp.int32, slot_count)[None, :]).astype(jnp.bfloat16)
+    row_width = BINS * channels
+    bins = slots_flat // pair_count
+    masked = jnp.where(
+        bins[:, None, None] == lax.iota(jnp.int32, BINS)[None, :, None], fields[:, None, :], 0.0
+    ).astype(jnp.bfloat16).reshape(volume, row_width)
+    pair_onehot = (
+        (slots_flat % pair_count)[:, None] == lax.iota(jnp.int32, pair_count)[None, :]
+    ).astype(jnp.bfloat16)
     pooled = lax.dot_general(
-        onehot, fields, (((0,), (0,)), ((), ())), preferred_element_type=jnp.float32
+        pair_onehot, masked, (((0,), (0,)), ((), ())), preferred_element_type=jnp.float32
     ) * (slot_count / volume)
-    row_width = BINS * channels
-    pair_rows = (
-        pooled.reshape(BINS, pair_count, channels)
-        .transpose(1, 0, 2)
-        .reshape(pair_count, row_width)
-        .astype(jnp.bfloat16)
-    )
+    pair_rows = pooled.astype(jnp.bfloat16)
     size_gx = lax.axis_size("gx")
     size_gy = lax.axis_size("gy")
     groups = size_gx * size_gy

time: 86.2 us -> 86.3 us (level)
    dot_general x1 -> x0, matrix products: 3.44 us -> none  [body(): lax.dot_general(onehot, fields, (((0,), (0,)), ((), ())), preferred_eleme...]
    dot_general x1, matrix products: 0.22 us -> 1.86 us  [body(): jnp.dot(placing, pair_rows, preferred_element_type=jnp.float32)]
    dot_general x1, matrix products: 0.36 us -> 1.31 us  [body(): jnp.dot(edge_rows, mlp_in, preferred_element_type=jnp.float32) + mlp_in_bias]
    unnamed x60 -> x58, local copies, waits for them, and re-layouts: 4.75 us -> 4.74 us
where the time goes in v11:
time: 86.3 us; the launch traced here: 85.9 us
  starting transfers between devices  28.6 us (33%)
  waiting for transfers between devices  17.1 us (20%)
  blocking collectives  14.2 us (16%)
  local copies, waits for them, and re-layouts  12.4 us (14%)
  other arithmetic  6.92 us (8%)
  matrix products  5.85 us (7%)
    all_to_all x1, blocking collectives, body(): lax.all_to_all(owner_scores.reshape(groups, capacity), ('gx', 'gy'), spli...  14.2 us
    all_to_all x1, starting transfers between devices, body(): lax.all_to_all(send, ('gx', 'gy'), split_axis=0, concat_axis=0, tiled=True)  13.4 us
    all_to_all x1, waiting for transfers between devices, body(): lax.all_to_all(send, ('gx', 'gy'), split_axis=0, concat_axis=0, tiled=True)  13.2 us
    ppermute x1, starting transfers between devices, body(): lax.ppermute(padded[:, :, -1, chunk - channels:], 'gz', [(i, i + 1) for i...  5.49 us
    ppermute x2, starting transfers between devices, extended(): lax.ppermute(tail, axis, [(i, (i + 1) % count) for i in range(ends)])  5.23 us
    unnamed x58, local copies, waits for them, and re-layouts  4.74 us
    ppermute x2, starting transfers between devices, extended(): lax.ppermute(head, axis, [((i + 1) % count, i) for i in range(ends)])  2.57 us
    dot_general x1, matrix products, conv_lane_dense(): jnp.dot(jnp.concatenate(slabs, axis=3), weight, preferred_element_type=jn...  1.99 us
  transfers between devices with their start and end apart: 7, of which 3 were waited for; matrix products, arithmetic and copies ran while one was open for 12% of the time, Pallas kernels for 0%

profile of v11, /device:TPU:192, one launch (start us, length us, event | category | flops | bytes accessed | tf_op | source)
XLA Modules:
  0.0 85.9 jit_solution(9545299345313838803)
XLA Ops:
  0.0 2.1 %copy.57 = bf16[32,2,16,128]{0,2,3,1:T(8,128)(2,1)S(1)} copy(bf16[32,2,16,128]{3,2,1,0:T(8,128)(2,1)} %param.15) | data formatting | bytes 524288 | tf_op args[0]
  2.1 0.2 fusion.43
  2.4 0.2 copy.58
  2.6 0.3 slice.251
  2.9 1.7 %collective-permute-start = (bf16[1,16,32,128]{3,2,1,0:T(8,128)(2,1)S(1)}, bf16[1,16,32,128]{3,2,1,0:T(8,128)(2,1)S(1)}, u32[]{:S(2)}, u32[]{:S(2)}) collective-permute-start(bf16[1,16,32,128]{3,2,1,0:T(8,128)(2,1)S(1)} %slice.251), channel_id=1, source_target_pairs={{0,64},{64,128},{128,192},{192,256},{256,320},{320,384},{384,448},... | collective-permute-start | bytes 393224 | tf_op jit(solution)/shard_map/ppermute | solution.py:18
  4.7 0.2 copy.60
  4.9 0.9 %slice.253 = bf16[1,16,32,128]{3,2,1,0:T(8,128)(2,1)} reshape(bf16[1,16,32,4,32]{4,3,2,1,0:T(4,128)(2,1)S(1)} %copy.60) | data formatting | bytes 262144 | tf_op jit(solution)/shard_map/slice | solution.py:14
  5.8 1.3 %collective-permute-start.1 = (bf16[1,16,32,128]{3,2,1,0:T(8,128)(2,1)}, bf16[1,16,32,128]{3,2,1,0:T(8,128)(2,1)S(1)}, u32[]{:S(2)}, u32[]{:S(2)}) collective-permute-start(bf16[1,16,32,128]{3,2,1,0:T(8,128)(2,1)} %slice.253), channel_id=1, source_target_pairs={{64,0},{128,64},{192,128},{256,192},{320,256},{384,320},{448,384},... | collective-permute-start | bytes 393224 | tf_op jit(solution)/shard_map/ppermute | solution.py:20
  7.1 0.7 fusion.31
  7.9 0.2 reduce_window_sum.11
  8.0 0.8 select_reduce_fusion.2
  8.9 0.2 copy.61
  9.2 0.3 maximum_bitcast_fusion
  9.5 0.6 copy.59
  10.1 0.5 reshape.238
  10.7 0.2 fusion.10
  11.0 3.5 %collective-permute-start.2 = (bf16[4,1,32,128]{3,2,1,0:T(8,128)(2,1)S(1)}, bf16[4,1,32,128]{3,2,1,0:T(8,128)(2,1)S(1)}, u32[]{:S(2)}, u32[]{:S(2)}) collective-permute-start(bf16[4,1,32,128]{3,2,1,0:T(8,128)(2,1)S(1)} %get-tuple-element.35), channel_id=1, source_target_pairs={{0,8},{8,16},{16,24},{24,32},{32,40},{40,48},{48,56},{1,9},{9,17},... | collective-permute-start | bytes 98312 | tf_op jit(solution)/shard_map/ppermute | solution.py:18
  14.5 1.3 %collective-permute-start.3 = (bf16[4,1,32,128]{3,2,1,0:T(8,128)(2,1)S(1)}, bf16[4,1,32,128]{3,2,1,0:T(8,128)(2,1)S(1)}, u32[]{:S(2)}, u32[]{:S(2)}) collective-permute-start(bf16[4,1,32,128]{3,2,1,0:T(8,128)(2,1)S(1)} %get-tuple-element.36), channel_id=1, source_target_pairs={{8,0},{16,8},{24,16},{32,24},{40,32},{48,40},{56,48},{9,1},{17,9},... | collective-permute-start | bytes 98312 | tf_op jit(solution)/shard_map/ppermute | solution.py:20
  15.8 1.0 %pad_maximum_fusion = bf16[3,3,3,128,128]{4,3,2,1,0:T(8,128)(2,1)} fusion(bf16[3,3,1,128,128]{4,3,2,1,0:T(8,128)(2,1)S(1)} %get-tuple-element.38, bf16[3,3,1,128,128]{4,3,2,1,0:T(8,128)(2,1)S(1)} %maximum_bitcast_fusion, bf16[3,3,1,128,128]{4,3,2,1,0:T(8,128)(2,1)S(1)} %get-tuple-element.41), kind=kLoop, calls=%fused_computation.12 | loop fusion | flops 884736 | bytes 1769472 | tf_op jit(solution)/shard_map/stack | solution.py:46
  16.8 1.3 %scatter_custom_fusion = bf16[448]{0:T(512)(128)(2,1)S(1)} fusion(s32[128]{0:T(128)S(1)} %get-tuple-element.49, bf16[128]{0:T(256)(128)(2,1)S(1)} %convert_element_type.57, bf16[]{:T(256)} %constant.108.clone.1), kind=kCustom, calls=%fused_computation.129 | custom fusion | bytes 898 | tf_op jit(solution)/shard_map/scatter | solution.py:136
  18.2 0.2 reshape.261
  18.3 2.0 %collective-permute-done.3 = bf16[4,1,32,128]{3,2,1,0:T(8,128)(2,1)S(1)} collective-permute-done((bf16[4,1,32,128]{3,2,1,0:T(8,128)(2,1)S(1)}, bf16[4,1,32,128]{3,2,1,0:T(8,128)(2,1)S(1)}, u32[]{:S(2)}, u32[]{:S(2)}) %collective-permute-start.3) | collective-permute-done | bytes 32800 | tf_op jit(solution)/shard_map/ppermute | solution.py:20
  20.4 0.3 fusion.44
  20.7 0.1 slice_dynamic-update-slice_fusion.17
  20.9 0.1 slice_dynamic-update-slice_fusion.15
  21.2 0.1 slice_dynamic-update-slice_fusion.13
  21.5 0.1 slice_dynamic-update-slice_fusion.11
  21.8 0.1 slice_dynamic-update-slice_fusion.9
  22.1 0.1 slice_dynamic-update-slice_fusion.7
  22.4 0.1 slice_dynamic-update-slice_fusion.5
  22.6 0.1 slice_dynamic-update-slice_fusion.3
  22.9 0.1 slice_dynamic-update-slice_fusion.1
  23.2 0.1 pad_maximum_fusion.6
  23.4 5.5 %collective-permute-start.4 = (bf16[4,18,32]{2,1,0:T(8,128)(2,1)S(1)}, bf16[4,18,32]{2,1,0:T(8,128)(2,1)S(1)}, u32[]{:S(2)}, u32[]{:S(2)}) collective-permute-start(bf16[4,18,32]{2,1,0:T(8,128)(2,1)S(1)} %copy.65), channel_id=1, source_target_pairs={{0,1},{1,2},{2,3},{3,4},{4,5},{5,6},{6,7},{8,9},{9,10},{10,11},{11... | collective-permute-start | bytes 13832 | tf_op jit(solution)/shard_map/ppermute | solution.py:103
  28.9 1.9 %collective-permute-start.5 = (bf16[4,18,32]{2,1,0:T(8,128)(2,1)S(1)}, bf16[4,18,32]{2,1,0:T(8,128)(2,1)S(1)}, u32[]{:S(2)}, u32[]{:S(2)}) collective-permute-start(bf16[4,18,32]{2,1,0:T(8,128)(2,1)S(1)} %copy.67), channel_id=1, source_target_pairs={{1,0},{2,1},{3,2},{4,3},{5,4},{6,5},{7,6},{9,8},{10,9},{11,10},{12... | collective-permute-start | bytes 13832 | tf_op jit(solution)/shard_map/ppermute | solution.py:106
  30.8 2.0 %fusion.46 = f32[2,16,32,128]{3,2,1,0:T(8,128)S(1)} fusion(bf16[2,16,32,3456]{3,2,1,0:T(8,128)(2,1)S(1)} %slice_dynamic-update-slice_fusion, bf16[3456,128,1,1]{1,0,3,2:T(8,128)(2,1)S(1)} %bitcast.78), kind=kOutput, calls=%fused_computation.140 | convolution fusion | flops 905969664 | bytes 8486912 | tf_op jit(solution)/shard_map/dot_general | solution.py:65
  33.2 0.1 constant_dynamic-update-slice_fusion.8
  33.3 0.1 constant_dynamic-update-slice_fusion.7
  33.4 0.1 constant_dynamic-update-slice_fusion.5
  33.5 0.1 constant_dynamic-update-slice_fusion.4
  33.6 0.2 fusion.47
  33.8 0.1 scatter-add.6
  33.9 1.9 %collective-permute-done.5 = bf16[4,18,32]{2,1,0:T(8,128)(2,1)S(1)} collective-permute-done((bf16[4,18,32]{2,1,0:T(8,128)(2,1)S(1)}, bf16[4,18,32]{2,1,0:T(8,128)(2,1)S(1)}, u32[]{:S(2)}, u32[]{:S(2)}) %collective-permute-start.5) | collective-permute-done | bytes 4640 | tf_op jit(solution)/shard_map/ppermute | solution.py:106
  36.0 0.2 fusion.48
  36.2 0.3 scatter-add.9
  36.5 0.5 reshape.243
  37.0 0.6 copy.68
  37.5 0.1 maximum_convert_fusion
  37.7 0.3 broadcast_select_fusion
  37.9 1.9 %convolution_convert_fusion = bf16[448,256]{1,0:T(8,128)(2,1)S(1)} fusion(bf16[4096,256]{0,1:T(8,128)(2,1)S(1)} %bitcast.74, s32[4096]{0:T(1024)S(1)} %get-tuple-element.46, s32[128]{0:T(128)S(1)} %multiply_add_fusion), kind=kOutput, calls=%fused_computation.4 | convolution fusion | flops 299081728 | bytes 2343424 | tf_op jit(solution)/shard_map/dot_general | solution.py:135
  39.9 0.8 fusion.20
  40.7 13.4 %all-to-all-start = ((bf16[64,8,256]{2,1,0:T(8,128)(2,1)}), bf16[64,8,256]{2,1,0:T(8,128)(2,1)S(1)}, u32[]{:S(2)}, u32[]{:S(2)}) async-start(bf16[64,8,256]{2,1,0:T(8,128)(2,1)} %fusion.20), calls=%async_computation | async-start | bytes 524288 | tf_op jit(solution)/shard_map/all_to_all | solution.py:142
  54.1 13.2 %all-to-all-done = bf16[64,8,256]{2,1,0:T(8,128)(2,1)S(1)} async-done(((bf16[64,8,256]{2,1,0:T(8,128)(2,1)}), bf16[64,8,256]{2,1,0:T(8,128)(2,1)S(1)}, u32[]{:S(2)}, u32[]{:S(2)}) %all-to-all-start) | async-done | bytes 262176 | tf_op jit(solution)/shard_map/all_to_all | solution.py:142
  67.4 0.1 fusion.32
  67.6 0.1 reshape.247
  67.7 1.3 %multiply_convert_fusion.1 = bf16[64,512]{1,0:T(8,128)(2,1)S(1)} fusion(bf16[256,512]{1,0:T(8,128)(2,1)} %param.21, bf16[448,256]{1,0:T(8,128)(2,1)S(1)} %reshape.246, f32[512]{0:T(512)S(1)} %copy-done.7, s32[448]{0:T(512)S(1)} %reshape.247), kind=kOutput, calls=%fused_computation.73 | convolution fusion | flops 31698944 | bytes 560896 | tf_op jit(solution)/shard_map/dot_general | solution.py:152
  69.0 0.4 convolution_bitcast_fusion
  69.4 0.1 select_reduce_fusion.1
  69.5 0.1 all_to_all.10
  69.6 14.2 %all_to_all.14 = f32[64,1,7]{2,1,0:T(1,128)S(1)} all-to-all(f32[64,1,7]{2,1,0:T(1,128)S(1)} %bitcast.81), channel_id=1, replica_groups=mesh['gx'=8,'gy'=8,'gz'=8] {'gx','gy'}, dimensions={0} | all-to-all | bytes 3584 | tf_op jit(solution)/shard_map/all_to_all | solution.py:160
  83.9 0.5 broadcast.203
  84.4 0.7 reduce.11
  85.1 0.1 broadcast_in_dim.79
  85.3 0.7 select_reduce_fusion
  (80 shorter events, 2.4 us)
Async XLA Ops:
  0.0 69.0 %copy-start = (bf16[512,512]{1,0:T(8,128)(2,1)S(1)}, bf16[512,512]{1,0:T(8,128)(2,1)}, u32[]{:S(2)}) copy-start(bf16[512,512]{1,0:T(8,128)(2,1)} %param.23) | copy-start | bytes 1572868
  0.0 8.9 %copy-start.4 = (s32[128,1]{0,1:T(1,128)S(1)}, s32[128,1]{0,1:T(1,128)}, u32[]{:S(2)}) copy-start(s32[128,1]{0,1:T(1,128)} %param.19) | copy-start | bytes 1540
  0.0 8.9 %copy-start.2 = (bf16[27,32,32]{2,1,0:T(8,128)(2,1)S(1)}, bf16[27,32,32]{2,1,0:T(8,128)(2,1)}, u32[]{:S(2)}) copy-start(bf16[27,32,32]{2,1,0:T(8,128)(2,1)} %param.17) | copy-start | bytes 165892
  0.0 9.1 %copy-start.3 = (s32[2,16,128]{2,1,0:T(8,128)S(1)}, s32[2,16,128]{2,1,0:T(8,128)}, u32[]{:S(2)}) copy-start(s32[2,16,128]{2,1,0:T(8,128)} %param.16) | copy-start | bytes 49156
  2.3 14.5 %copy-start.9 = (s32[128]{0:T(128)S(1)}, s32[128]{0:T(128)}, u32[]{:S(2)}) copy-start(s32[128]{0:T(128)} %param.20) | copy-start | bytes 1540
  2.9 8.0 %collective-permute-start = (bf16[1,16,32,128]{3,2,1,0:T(8,128)(2,1)S(1)}, bf16[1,16,32,128]{3,2,1,0:T(8,128)(2,1)S(1)}, u32[]{:S(2)}, u32[]{:S(2)}) collective-permute-start(bf16[1,16,32,128]{3,2,1,0:T(8,128)(2,1)S(1)} %slice.251), channel_id=1, source_target_pairs={{0,64},{64,128},{128,192},{192,256},{256,320},{320,384},{384,448},... | collective-permute-start | bytes 393224 | tf_op jit(solution)/shard_map/ppermute | solution.py:18
  5.8 5.1 %collective-permute-start.1 = (bf16[1,16,32,128]{3,2,1,0:T(8,128)(2,1)}, bf16[1,16,32,128]{3,2,1,0:T(8,128)(2,1)S(1)}, u32[]{:S(2)}, u32[]{:S(2)}) collective-permute-start(bf16[1,16,32,128]{3,2,1,0:T(8,128)(2,1)} %slice.253), channel_id=1, source_target_pairs={{64,0},{128,64},{192,128},{256,192},{320,256},{384,320},{448,384},... | collective-permute-start | bytes 393224 | tf_op jit(solution)/shard_map/ppermute | solution.py:20
  11.0 7.3 %collective-permute-start.2 = (bf16[4,1,32,128]{3,2,1,0:T(8,128)(2,1)S(1)}, bf16[4,1,32,128]{3,2,1,0:T(8,128)(2,1)S(1)}, u32[]{:S(2)}, u32[]{:S(2)}) collective-permute-start(bf16[4,1,32,128]{3,2,1,0:T(8,128)(2,1)S(1)} %get-tuple-element.35), channel_id=1, source_target_pairs={{0,8},{8,16},{16,24},{24,32},{32,40},{40,48},{48,56},{1,9},{9,17},... | collective-permute-start | bytes 98312 | tf_op jit(solution)/shard_map/ppermute | solution.py:18
  14.5 5.8 %collective-permute-start.3 = (bf16[4,1,32,128]{3,2,1,0:T(8,128)(2,1)S(1)}, bf16[4,1,32,128]{3,2,1,0:T(8,128)(2,1)S(1)}, u32[]{:S(2)}, u32[]{:S(2)}) collective-permute-start(bf16[4,1,32,128]{3,2,1,0:T(8,128)(2,1)S(1)} %get-tuple-element.36), channel_id=1, source_target_pairs={{8,0},{16,8},{24,16},{32,24},{40,32},{48,40},{56,48},{9,1},{17,9},... | collective-permute-start | bytes 98312 | tf_op jit(solution)/shard_map/ppermute | solution.py:20
  21.7 9.1 %copy-start.1 = (bf16[3,3,3,128,128]{4,3,2,1,0:T(8,128)(2,1)S(1)}, bf16[3,3,3,128,128]{4,3,2,1,0:T(8,128)(2,1)}, u32[]{:S(2)}) copy-start(bf16[3,3,3,128,128]{4,3,2,1,0:T(8,128)(2,1)} %pad_maximum_fusion) | copy-start | bytes 2654212
  23.4 9.5 %collective-permute-start.4 = (bf16[4,18,32]{2,1,0:T(8,128)(2,1)S(1)}, bf16[4,18,32]{2,1,0:T(8,128)(2,1)S(1)}, u32[]{:S(2)}, u32[]{:S(2)}) collective-permute-start(bf16[4,18,32]{2,1,0:T(8,128)(2,1)S(1)} %copy.65), channel_id=1, source_target_pairs={{0,1},{1,2},{2,3},{3,4},{4,5},{5,6},{6,7},{8,9},{9,10},{10,11},{11... | collective-permute-start | bytes 13832 | tf_op jit(solution)/shard_map/ppermute | solution.py:103
  28.9 6.9 %collective-permute-start.5 = (bf16[4,18,32]{2,1,0:T(8,128)(2,1)S(1)}, bf16[4,18,32]{2,1,0:T(8,128)(2,1)S(1)}, u32[]{:S(2)}, u32[]{:S(2)}) collective-permute-start(bf16[4,18,32]{2,1,0:T(8,128)(2,1)S(1)} %copy.67), channel_id=1, source_target_pairs={{1,0},{2,1},{3,2},{4,3},{5,4},{6,5},{7,6},{9,8},{10,9},{11,10},{12... | collective-permute-start | bytes 13832 | tf_op jit(solution)/shard_map/ppermute | solution.py:106
  30.8 6.7 %copy-start.6 = (f32[32]{0:T(128)S(1)}, f32[32]{0:T(128)}, u32[]{:S(2)}) copy-start(f32[32]{0:T(128)} %param.18) | copy-start | bytes 388
  33.6 20.5 %copy-start.5 = (bf16[512]{0:T(512)(128)(2,1)S(1)}, bf16[512]{0:T(512)(128)(2,1)}, u32[]{:S(2)}) copy-start(bf16[512]{0:T(512)(128)(2,1)} %param.25) | copy-start | bytes 3076
  35.9 31.8 %copy-start.7 = (f32[512]{0:T(512)S(1)}, f32[512]{0:T(512)}, u32[]{:S(2)}) copy-start(f32[512]{0:T(512)} %param.22) | copy-start | bytes 6148
  36.5 32.6 %copy-start.8 = (f32[512]{0:T(512)S(1)}, f32[512]{0:T(512)}, u32[]{:S(2)}) copy-start(f32[512]{0:T(512)} %param.24) | copy-start | bytes 6148
  40.7 26.6 %all-to-all-start = ((bf16[64,8,256]{2,1,0:T(8,128)(2,1)}), bf16[64,8,256]{2,1,0:T(8,128)(2,1)S(1)}, u32[]{:S(2)}, u32[]{:S(2)}) async-start(bf16[64,8,256]{2,1,0:T(8,128)(2,1)} %fusion.20), calls=%async_computation | async-start | bytes 524288 | tf_op jit(solution)/shard_map/all_to_all | solution.py:142

commit v12 on v9

--- a/solution.py
+++ b/solution.py
@@ -74,8 +74,7 @@
             preferred_element_type=jnp.float32,
         )
 
-    main = main.at[:, :, 0, :].add(edge(low_chunk, 0))
-    return main.at[:, :, nchunk - 1, :].add(edge(high_chunk, 2))
+    return main, edge(low_chunk, 0), edge(high_chunk, 2)
 
 def body(
     features,
@@ -104,14 +103,28 @@
         padded[:, :, -1, chunk - channels :], "gz", [(i, i + 1) for i in range(count_z - 1)]
     )
     high = lax.ppermute(padded[:, :, 0, :channels], "gz", [(i + 1, i) for i in range(count_z - 1)])
-    total = conv_lane_dense(padded, low, high, conv_weight, channels).reshape(volume, channels)
-    fields = jnp.maximum(total + conv_bias[None, :], 0.0).astype(jnp.bfloat16)
+    main, low_fix, high_fix = conv_lane_dense(padded, low, high, conv_weight, channels)
+    bias_lanes = jnp.tile(conv_bias, 4)
+    chunk_index = lax.iota(jnp.int32, main.shape[2])[None, None, :, None]
+    inner = (chunk_index > 0) & (chunk_index < main.shape[2] - 1)
+    fields = jnp.where(inner, jnp.maximum(main + bias_lanes, 0.0), 0.0).astype(jnp.bfloat16)
+    fields = fields.reshape(volume, channels)
+    ends = jnp.stack(
+        [main[:, :, 0] + low_fix, main[:, :, -1] + high_fix], axis=2
+    )
+    end_fields = jnp.maximum(ends + bias_lanes, 0.0).astype(jnp.bfloat16).reshape(-1, channels)
     pair_count = pair_edge.shape[0]
     slot_count = pair_count * BINS
     slots_flat = voxel_slot.reshape(volume)
+    end_slots = voxel_slot.reshape(extent_x, extent_y, extent_z // 4, 4)[:, :, :: extent_z // 4 - 1]
     onehot = (slots_flat[:, None] == lax.iota(jnp.int32, slot_count)[None, :]).astype(jnp.bfloat16)
-    pooled = lax.dot_general(
-        onehot, fields, (((0,), (0,)), ((), ())), preferred_element_type=jnp.float32
+    end_onehot = (
+        end_slots.reshape(-1)[:, None] == lax.iota(jnp.int32, slot_count)[None, :]
+    ).astype(jnp.bfloat16)
+    contract = (((0,), (0,)), ((), ()))
+    pooled = (
+        lax.dot_general(onehot, fields, contract, preferred_element_type=jnp.float32)
+        + lax.dot_general(end_onehot, end_fields, contract, preferred_element_type=jnp.float32)
     ) * (slot_count / volume)
     row_width = BINS * channels
     pair_rows = (

time: 86.2 us -> 87.8 us (1.019)
  matrix products: 6.7 us -> 10.2 us
  other arithmetic: 6.51 us -> 4.24 us
  local copies, waits for them, and re-layouts: 11.9 us -> 13 us
    ppermute x1, waiting for transfers between devices: 1.89 us -> 0.01 us  [body(): lax.ppermute(padded[:, :, 0, :channels], 'gz', [(i + 1, i) for i in range...]
    dot_general x1 -> x2, matrix products: 3.44 us -> 5.17 us  [the longest x1 4.81 us: body(): lax.dot_general(onehot, fields, contract, preferred_element_type=jnp.floa...]
    ppermute x2, waiting for transfers between devices: 1.98 us -> 3.37 us  [extended(): lax.ppermute(head, axis, [((i + 1) % count, i) for i in range(ends)])]
    slice x0 -> x3, local copies, waits for them, and re-layouts: none -> 1.11 us  [the longest x1 1 us: body(): main[:, :, 0] + low_fix]
    dot_general x1, matrix products: 0.36 us -> 1.31 us  [body(): jnp.dot(edge_rows, mlp_in, preferred_element_type=jnp.float32) + mlp_in_bias]
    another operation x2, other arithmetic: 1.34 us -> 0.43 us  [banded_weight(): return jnp.stack(parts, axis=2).reshape(27 * 4 * channels, 4 * channels)]
    unnamed x60 -> x57, local copies, waits for them, and re-layouts: 4.75 us -> 4.84 us
  transfers between devices with their start and end apart: 7 -> 7, of which waited for: 3 -> 3; matrix products, arithmetic and copies ran while one was open for 12% -> 18% of each run, Pallas kernels for 0% -> 0%
where the time goes in v12:
time: 87.8 us; the launch traced here: 87.4 us
  starting transfers between devices  28.3 us (32%)
  waiting for transfers between devices  16.6 us (19%)
  blocking collectives  14.2 us (16%)
  local copies, waits for them, and re-layouts  13 us (15%)
  matrix products  10.2 us (12%)
  other arithmetic  4.24 us (5%)
    all_to_all x1, blocking collectives, body(): lax.all_to_all(owner_scores.reshape(groups, capacity), ('gx', 'gy'), spli...  14.2 us
    all_to_all x1, waiting for transfers between devices, body(): lax.all_to_all(send, ('gx', 'gy'), split_axis=0, concat_axis=0, tiled=True)  13.2 us
    all_to_all x1, starting transfers between devices, body(): lax.all_to_all(send, ('gx', 'gy'), split_axis=0, concat_axis=0, tiled=True)  13.1 us
    ppermute x1, starting transfers between devices, body(): lax.ppermute(padded[:, :, -1, chunk - channels:], 'gz', [(i, i + 1) for i...  5.49 us
    ppermute x2, starting transfers between devices, extended(): lax.ppermute(tail, axis, [(i, (i + 1) % count) for i in range(ends)])  5.23 us
    unnamed x57, local copies, waits for them, and re-layouts  4.84 us
    dot_general x1, matrix products, body(): lax.dot_general(onehot, fields, contract, preferred_element_type=jnp.floa...  4.81 us
    ppermute x2, waiting for transfers between devices, extended(): lax.ppermute(head, axis, [((i + 1) % count, i) for i in range(ends)])  3.37 us
  transfers between devices with their start and end apart: 7, of which 3 were waited for; matrix products, arithmetic and copies ran while one was open for 18% of the time, Pallas kernels for 0%

profile of v12, /device:TPU:192, one launch (start us, length us, event | category | flops | bytes accessed | tf_op | source)
XLA Modules:
  0.0 87.4 jit_solution(11522907679372116491)
XLA Ops:
  0.0 2.1 %copy.52 = bf16[32,2,16,128]{0,2,3,1:T(8,128)(2,1)S(1)} copy(bf16[32,2,16,128]{3,2,1,0:T(8,128)(2,1)} %param.11) | data formatting | bytes 524288 | tf_op args[0]
  2.1 0.2 fusion.43
  2.4 0.2 copy.53
  2.6 0.3 slice.206
  2.9 1.7 %collective-permute-start = (bf16[1,16,32,128]{3,2,1,0:T(8,128)(2,1)S(1)}, bf16[1,16,32,128]{3,2,1,0:T(8,128)(2,1)S(1)}, u32[]{:S(2)}, u32[]{:S(2)}) collective-permute-start(bf16[1,16,32,128]{3,2,1,0:T(8,128)(2,1)S(1)} %slice.206), channel_id=1, source_target_pairs={{0,64},{64,128},{128,192},{192,256},{256,320},{320,384},{384,448},... | collective-permute-start | bytes 393224 | tf_op jit(solution)/shard_map/ppermute | solution.py:18
  4.7 0.2 copy.55
  4.9 0.9 %slice.208 = bf16[1,16,32,128]{3,2,1,0:T(8,128)(2,1)} reshape(bf16[1,16,32,4,32]{4,3,2,1,0:T(4,128)(2,1)S(1)} %copy.55) | data formatting | bytes 262144 | tf_op jit(solution)/shard_map/slice | solution.py:14
  5.9 1.3 %collective-permute-start.1 = (bf16[1,16,32,128]{3,2,1,0:T(8,128)(2,1)}, bf16[1,16,32,128]{3,2,1,0:T(8,128)(2,1)S(1)}, u32[]{:S(2)}, u32[]{:S(2)}) collective-permute-start(bf16[1,16,32,128]{3,2,1,0:T(8,128)(2,1)} %slice.208), channel_id=1, source_target_pairs={{64,0},{128,64},{192,128},{256,192},{320,256},{384,320},{448,384},... | collective-permute-start | bytes 393224 | tf_op jit(solution)/shard_map/ppermute | solution.py:20
  7.1 0.6 copy.54
  7.8 0.2 reduce_window_sum.11
  8.0 0.2 select_reduce_fusion.2
  8.2 0.5 reshape.95
  8.7 0.2 copy.56
  8.9 0.2 fusion.13
  9.2 0.3 maximum_bitcast_fusion
  9.5 0.1 pad_maximum_fusion
  9.7 0.9 collective-permute-done.1
  10.6 3.5 %collective-permute-start.2 = (bf16[4,1,32,128]{3,2,1,0:T(8,128)(2,1)S(1)}, bf16[4,1,32,128]{3,2,1,0:T(8,128)(2,1)S(1)}, u32[]{:S(2)}, u32[]{:S(2)}) collective-permute-start(bf16[4,1,32,128]{3,2,1,0:T(8,128)(2,1)S(1)} %get-tuple-element.13), channel_id=1, source_target_pairs={{0,8},{8,16},{16,24},{24,32},{32,40},{40,48},{48,56},{1,9},{9,17},... | collective-permute-start | bytes 98312 | tf_op jit(solution)/shard_map/ppermute | solution.py:18
  14.1 1.3 %collective-permute-start.3 = (bf16[4,1,32,128]{3,2,1,0:T(8,128)(2,1)S(1)}, bf16[4,1,32,128]{3,2,1,0:T(8,128)(2,1)S(1)}, u32[]{:S(2)}, u32[]{:S(2)}) collective-permute-start(bf16[4,1,32,128]{3,2,1,0:T(8,128)(2,1)S(1)} %get-tuple-element.14), channel_id=1, source_target_pairs={{8,0},{16,8},{24,16},{32,24},{40,32},{48,40},{56,48},{9,1},{17,9},... | collective-permute-start | bytes 98312 | tf_op jit(solution)/shard_map/ppermute | solution.py:20
  15.5 0.1 copy.59
  15.6 0.1 copy.60
  15.7 0.1 eq.114
  15.9 1.3 %scatter_custom_fusion = bf16[448]{0:T(512)(128)(2,1)S(1)} fusion(s32[128]{0:T(128)S(1)} %get-tuple-element.25, bf16[128]{0:T(256)(128)(2,1)S(1)} %convert_element_type.73, bf16[]{:T(256)} %constant.15.clone.1), kind=kCustom, calls=%fused_computation.129 | custom fusion | bytes 898 | tf_op jit(solution)/shard_map/scatter | solution.py:148
  17.2 0.2 reshape.117
  17.4 2.5 %collective-permute-done.3 = bf16[4,1,32,128]{3,2,1,0:T(8,128)(2,1)S(1)} collective-permute-done((bf16[4,1,32,128]{3,2,1,0:T(8,128)(2,1)S(1)}, bf16[4,1,32,128]{3,2,1,0:T(8,128)(2,1)S(1)}, u32[]{:S(2)}, u32[]{:S(2)}) %collective-permute-start.3) | collective-permute-done | bytes 32800 | tf_op jit(solution)/shard_map/ppermute | solution.py:20
  20.0 0.3 fusion.44
  20.3 0.1 slice_dynamic-update-slice_fusion.17
  20.5 0.1 slice_dynamic-update-slice_fusion.15
  20.8 0.1 slice_dynamic-update-slice_fusion.13
  21.1 0.1 slice_dynamic-update-slice_fusion.11
  21.4 0.1 slice_dynamic-update-slice_fusion.9
  21.6 0.1 slice_dynamic-update-slice_fusion.7
  21.9 0.1 slice_dynamic-update-slice_fusion.5
  22.2 0.1 slice_dynamic-update-slice_fusion.3
  22.5 0.1 slice_dynamic-update-slice_fusion.1
  22.8 0.1 pad_maximum_fusion.7
  22.9 5.5 %collective-permute-start.4 = (bf16[4,18,32]{2,1,0:T(8,128)(2,1)S(1)}, bf16[4,18,32]{2,1,0:T(8,128)(2,1)S(1)}, u32[]{:S(2)}, u32[]{:S(2)}) collective-permute-start(bf16[4,18,32]{2,1,0:T(8,128)(2,1)S(1)} %copy.63), channel_id=1, source_target_pairs={{0,1},{1,2},{2,3},{3,4},{4,5},{5,6},{6,7},{8,9},{9,10},{10,11},{11... | collective-permute-start | bytes 13832 | tf_op jit(solution)/shard_map/ppermute | solution.py:102
  28.5 1.9 %collective-permute-start.5 = (bf16[4,18,32]{2,1,0:T(8,128)(2,1)S(1)}, bf16[4,18,32]{2,1,0:T(8,128)(2,1)S(1)}, u32[]{:S(2)}, u32[]{:S(2)}) collective-permute-start(bf16[4,18,32]{2,1,0:T(8,128)(2,1)S(1)} %copy.65), channel_id=1, source_target_pairs={{1,0},{2,1},{3,2},{4,3},{5,4},{6,5},{7,6},{9,8},{10,9},{11,10},{12... | collective-permute-start | bytes 13832 | tf_op jit(solution)/shard_map/ppermute | solution.py:105
  30.4 2.8 %select_convert_fusion = (bf16[2,16,32,128]{3,2,1,0:T(8,128)(2,1)S(1)}, f32[2,16,32,128]{3,2,1,0:T(8,128)}) fusion(f32[128]{0:T(128)S(1)} %add.86, pred[32]{0:T(512)(128)(4,1)S(1)} %compare_and_fusion, bf16[2,16,32,3456]{3,2,1,0:T(8,128)(2,1)S(1)} %slice_dynamic-update-slice_fusion, bf16[3456,128,1,1]{1,0,3,2:T(8,128)(2,1)S(1)} %bitcast.93), kind=kOutput, calls=%fused_computation.30 | convolution fusion | flops 906493952 | bytes 8749600 | tf_op jit(solution)/shard_map/dot_general | solution.py:65
  33.2 0.4 reshape.98
  33.6 4.8 %fusion = f32[1024,32]{0,1:T(8,128)S(1)} fusion(bf16[4096,32]{1,0:T(8,128)(2,1)S(1)} %reshape.98, s32[4096]{0:T(1024)S(1)} %bitcast.103), kind=kOutput, calls=%fused_computation.2 | convolution fusion | flops 272629760 | bytes 409600 | tf_op jit(solution)/shard_map/dot_general | solution.py:126
  38.5 1.0 %fusion.45 = (f32[2,16,1,128]{3,2,1,0:T(1,128)S(1)}, f32[2,16,1,128]{3,2,1,0:T(1,128)S(1)}) fusion(f32[2,16,32,128]{3,2,1,0:T(8,128)} %get-tuple-element.27), kind=kLoop, calls=%fused_computation.138 | loop fusion | bytes 65536 | tf_op jit(solution)/shard_map/slice | solution.py:113
  39.9 0.1 constant_dynamic-update-slice_fusion.7
  40.1 0.1 constant_dynamic-update-slice_fusion.5
  40.1 0.1 constant_dynamic-update-slice_fusion.4
  40.2 0.2 fusion.6
  40.6 0.2 fusion.5
  40.8 0.1 convert_element_type.67
  40.9 0.4 fusion.4
  41.3 0.2 convolution_convert_fusion
  41.6 0.8 fusion.22
  42.4 13.1 %all-to-all-start = ((bf16[64,8,256]{2,1,0:T(8,128)(2,1)}), bf16[64,8,256]{2,1,0:T(8,128)(2,1)S(1)}, u32[]{:S(2)}, u32[]{:S(2)}) async-start(bf16[64,8,256]{2,1,0:T(8,128)(2,1)} %fusion.22), calls=%async_computation | async-start | bytes 524288 | tf_op jit(solution)/shard_map/all_to_all | solution.py:154
  55.6 13.2 %all-to-all-done = bf16[64,8,256]{2,1,0:T(8,128)(2,1)S(1)} async-done(((bf16[64,8,256]{2,1,0:T(8,128)(2,1)}), bf16[64,8,256]{2,1,0:T(8,128)(2,1)S(1)}, u32[]{:S(2)}, u32[]{:S(2)}) %all-to-all-start) | async-done | bytes 262176 | tf_op jit(solution)/shard_map/all_to_all | solution.py:154
  68.9 0.1 fusion.33
  69.0 0.1 reshape.103
  69.1 1.3 %multiply_convert_fusion.1 = bf16[64,512]{1,0:T(8,128)(2,1)S(1)} fusion(bf16[256,512]{1,0:T(8,128)(2,1)} %param.17, bf16[448,256]{1,0:T(8,128)(2,1)S(1)} %reshape.102, f32[512]{0:T(512)S(1)} %copy-done.6, s32[448]{0:T(512)S(1)} %reshape.103), kind=kOutput, calls=%fused_computation.80 | convolution fusion | flops 31698944 | bytes 560896 | tf_op jit(solution)/shard_map/dot_general | solution.py:164
  70.5 0.4 convolution_bitcast_fusion
  70.8 0.1 select_reduce_fusion.1
  70.9 0.1 all_to_all.10
  71.1 14.2 %all_to_all.14 = f32[64,1,7]{2,1,0:T(1,128)S(1)} all-to-all(f32[64,1,7]{2,1,0:T(1,128)S(1)} %bitcast.98), channel_id=1, replica_groups=mesh['gx'=8,'gy'=8,'gz'=8] {'gx','gy'}, dimensions={0} | all-to-all | bytes 3584 | tf_op jit(solution)/shard_map/all_to_all | solution.py:172
  85.3 0.5 broadcast.87
  85.8 0.7 reduce.7
  86.6 0.1 broadcast_in_dim.64
  86.7 0.7 select_reduce_fusion
  (83 shorter events, 2.6 us)
Async XLA Ops:
  0.0 70.5 %copy-start = (bf16[512,512]{1,0:T(8,128)(2,1)S(1)}, bf16[512,512]{1,0:T(8,128)(2,1)}, u32[]{:S(2)}) copy-start(bf16[512,512]{1,0:T(8,128)(2,1)} %param.19) | copy-start | bytes 1572868
  0.0 7.7 %copy-start.3 = (s32[128,1]{0,1:T(1,128)S(1)}, s32[128,1]{0,1:T(1,128)}, u32[]{:S(2)}) copy-start(s32[128,1]{0,1:T(1,128)} %param.15) | copy-start | bytes 1540
  0.0 8.7 %copy-start.1 = (bf16[27,32,32]{2,1,0:T(8,128)(2,1)S(1)}, bf16[27,32,32]{2,1,0:T(8,128)(2,1)}, u32[]{:S(2)}) copy-start(bf16[27,32,32]{2,1,0:T(8,128)(2,1)} %param.13) | copy-start | bytes 165892
  2.3 13.1 %copy-start.5 = (f32[32]{0:T(128)S(1)}, f32[32]{0:T(128)}, u32[]{:S(2)}) copy-start(f32[32]{0:T(128)} %param.14) | copy-start | bytes 388
  2.3 13.2 %copy-start.2 = (s32[2,16,128]{2,1,0:T(8,128)S(1)}, s32[2,16,128]{2,1,0:T(8,128)}, u32[]{:S(2)}) copy-start(s32[2,16,128]{2,1,0:T(8,128)} %param.12) | copy-start | bytes 49156
  2.4 13.5 %copy-start.8 = (s32[128]{0:T(128)S(1)}, s32[128]{0:T(128)}, u32[]{:S(2)}) copy-start(s32[128]{0:T(128)} %param.16) | copy-start | bytes 1540
  2.9 6.7 %collective-permute-start = (bf16[1,16,32,128]{3,2,1,0:T(8,128)(2,1)S(1)}, bf16[1,16,32,128]{3,2,1,0:T(8,128)(2,1)S(1)}, u32[]{:S(2)}, u32[]{:S(2)}) collective-permute-start(bf16[1,16,32,128]{3,2,1,0:T(8,128)(2,1)S(1)} %slice.206), channel_id=1, source_target_pairs={{0,64},{64,128},{128,192},{192,256},{256,320},{320,384},{384,448},... | collective-permute-start | bytes 393224 | tf_op jit(solution)/shard_map/ppermute | solution.py:18
  5.9 4.7 %collective-permute-start.1 = (bf16[1,16,32,128]{3,2,1,0:T(8,128)(2,1)}, bf16[1,16,32,128]{3,2,1,0:T(8,128)(2,1)S(1)}, u32[]{:S(2)}, u32[]{:S(2)}) collective-permute-start(bf16[1,16,32,128]{3,2,1,0:T(8,128)(2,1)} %slice.208), channel_id=1, source_target_pairs={{64,0},{128,64},{192,128},{256,192},{320,256},{384,320},{448,384},... | collective-permute-start | bytes 393224 | tf_op jit(solution)/shard_map/ppermute | solution.py:20
  10.6 6.8 %collective-permute-start.2 = (bf16[4,1,32,128]{3,2,1,0:T(8,128)(2,1)S(1)}, bf16[4,1,32,128]{3,2,1,0:T(8,128)(2,1)S(1)}, u32[]{:S(2)}, u32[]{:S(2)}) collective-permute-start(bf16[4,1,32,128]{3,2,1,0:T(8,128)(2,1)S(1)} %get-tuple-element.13), channel_id=1, source_target_pairs={{0,8},{8,16},{16,24},{24,32},{32,40},{40,48},{48,56},{1,9},{9,17},... | collective-permute-start | bytes 98312 | tf_op jit(solution)/shard_map/ppermute | solution.py:18
  14.1 5.8 %collective-permute-start.3 = (bf16[4,1,32,128]{3,2,1,0:T(8,128)(2,1)S(1)}, bf16[4,1,32,128]{3,2,1,0:T(8,128)(2,1)S(1)}, u32[]{:S(2)}, u32[]{:S(2)}) collective-permute-start(bf16[4,1,32,128]{3,2,1,0:T(8,128)(2,1)S(1)} %get-tuple-element.14), channel_id=1, source_target_pairs={{8,0},{16,8},{24,16},{32,24},{40,32},{48,40},{56,48},{9,1},{17,9},... | collective-permute-start | bytes 98312 | tf_op jit(solution)/shard_map/ppermute | solution.py:20
  22.9 16.5 %collective-permute-start.4 = (bf16[4,18,32]{2,1,0:T(8,128)(2,1)S(1)}, bf16[4,18,32]{2,1,0:T(8,128)(2,1)S(1)}, u32[]{:S(2)}, u32[]{:S(2)}) collective-permute-start(bf16[4,18,32]{2,1,0:T(8,128)(2,1)S(1)} %copy.63), channel_id=1, source_target_pairs={{0,1},{1,2},{2,3},{3,4},{4,5},{5,6},{6,7},{8,9},{9,10},{10,11},{11... | collective-permute-start | bytes 13832 | tf_op jit(solution)/shard_map/ppermute | solution.py:102
  28.5 12.0 %collective-permute-start.5 = (bf16[4,18,32]{2,1,0:T(8,128)(2,1)S(1)}, bf16[4,18,32]{2,1,0:T(8,128)(2,1)S(1)}, u32[]{:S(2)}, u32[]{:S(2)}) collective-permute-start(bf16[4,18,32]{2,1,0:T(8,128)(2,1)S(1)} %copy.65), channel_id=1, source_target_pairs={{1,0},{2,1},{3,2},{4,3},{5,4},{6,5},{7,6},{9,8},{10,9},{11,10},{12... | collective-permute-start | bytes 13832 | tf_op jit(solution)/shard_map/ppermute | solution.py:105
  33.6 21.9 %copy-start.4 = (bf16[512]{0:T(512)(128)(2,1)S(1)}, bf16[512]{0:T(512)(128)(2,1)}, u32[]{:S(2)}) copy-start(bf16[512]{0:T(512)(128)(2,1)} %param.21) | copy-start | bytes 3076
  33.6 35.5 %copy-start.6 = (f32[512]{0:T(512)S(1)}, f32[512]{0:T(512)}, u32[]{:S(2)}) copy-start(f32[512]{0:T(512)} %param.18) | copy-start | bytes 6148
  33.6 36.8 %copy-start.7 = (f32[512]{0:T(512)S(1)}, f32[512]{0:T(512)}, u32[]{:S(2)}) copy-start(f32[512]{0:T(512)} %param.20) | copy-start | bytes 6148
  42.4 26.4 %all-to-all-start = ((bf16[64,8,256]{2,1,0:T(8,128)(2,1)}), bf16[64,8,256]{2,1,0:T(8,128)(2,1)S(1)}, u32[]{:S(2)}, u32[]{:S(2)}) async-start(bf16[64,8,256]{2,1,0:T(8,128)(2,1)} %fusion.22), calls=%async_computation | async-start | bytes 524288 | tf_op jit(solution)/shard_map/all_to_all | solution.py:154

commit v13 on v9

--- a/solution.py
+++ b/solution.py
@@ -56,13 +56,17 @@
         padded,
         jnp.concatenate([padded[:, :, 1:], empty], axis=2),
     )
-    slabs = [
-        parts[p][dx : dx + px - 2, dy : dy + py - 2]
-        for dx in range(3)
-        for dy in range(3)
-        for p in range(3)
-    ]
-    main = jnp.dot(jnp.concatenate(slabs, axis=3), weight, preferred_element_type=jnp.float32)
+    trio = jnp.concatenate(parts, axis=3)
+    grouped = weight.reshape(9, 3 * chunk, chunk)
+    main = None
+    for dx in range(3):
+        for dy in range(3):
+            term = jnp.dot(
+                trio[dx : dx + px - 2, dy : dy + py - 2],
+                grouped[dx * 3 + dy],
+                preferred_element_type=jnp.float32,
+            )
+            main = term if main is None else main + term
     low_chunk = jnp.pad(low, ((0, 0), (0, 0), (chunk - channels, 0)))
     high_chunk = jnp.pad(high, ((0, 0), (0, 0), (0, chunk - channels)))
 

time: 86.2 us -> 87.9 us (1.020)
  local copies, waits for them, and re-layouts: 11.9 us -> 13.7 us
  other arithmetic: 6.51 us -> 5.15 us
  matrix products: 6.7 us -> 8.05 us
    ppermute x1, waiting for transfers between devices: 1.89 us -> 0.01 us  [body(): lax.ppermute(padded[:, :, 0, :channels], 'gz', [(i + 1, i) for i in range...]
    dot_general x1 -> x9, matrix products: 1.99 us -> 3.34 us  [conv_lane_dense(): jnp.dot(trio[dx:dx + px - 2, dy:dy + py - 2], grouped[dx * 3 + dy], prefe...]
    slice x3, local copies, waits for them, and re-layouts: 0.54 us -> 1.79 us  [extended(): lax.slice_in_dim(cells, cells.shape[dim] - width, cells.shape[dim], axis=...]
    ppermute x1, waiting for transfers between devices: 0.01 us -> 1.06 us  [body(): lax.ppermute(padded[:, :, -1, chunk - channels:], 'gz', [(i, i + 1) for i...]
    concatenate x1, other arithmetic: 0.22 us -> 1.14 us  [banded_weight(): jnp.concatenate([jnp.concatenate([block(part, zi, zo) for zo in range(4)]...]
    another operation x2, other arithmetic: 1.34 us -> 0.42 us  [banded_weight(): return jnp.stack(parts, axis=2).reshape(27 * 4 * channels, 4 * channels)]
    concatenate x1, local copies, waits for them, and re-layouts: 0.02 us -> 0.92 us  [extended(): jnp.concatenate([lax.ppermute(tail, axis, [(i, (i + 1) % count) for i in...]
    ppermute x2, waiting for transfers between devices: 1.98 us -> 2.87 us  [extended(): lax.ppermute(head, axis, [((i + 1) % count, i) for i in range(ends)])]
  transfers between devices with their start and end apart: 7 -> 7, of which waited for: 3 -> 3; matrix products, arithmetic and copies ran while one was open for 12% -> 10% of each run, Pallas kernels for 0% -> 0%
where the time goes in v13:
time: 87.9 us; the launch traced here: 87.5 us
  starting transfers between devices  28.5 us (32%)
  waiting for transfers between devices  17.1 us (19%)
  blocking collectives  14.2 us (16%)
  local copies, waits for them, and re-layouts  13.7 us (16%)
  matrix products  8.05 us (9%)
  other arithmetic  5.15 us (6%)
    all_to_all x1, blocking collectives, body(): lax.all_to_all(owner_scores.reshape(groups, capacity), ('gx', 'gy'), spli...  14.2 us
    all_to_all x1, waiting for transfers between devices, body(): lax.all_to_all(send, ('gx', 'gy'), split_axis=0, concat_axis=0, tiled=True)  13.2 us
    all_to_all x1, starting transfers between devices, body(): lax.all_to_all(send, ('gx', 'gy'), split_axis=0, concat_axis=0, tiled=True)  12.7 us
    ppermute x2, starting transfers between devices, extended(): lax.ppermute(tail, axis, [(i, (i + 1) % count) for i in range(ends)])  5.86 us
    ppermute x1, starting transfers between devices, body(): lax.ppermute(padded[:, :, -1, chunk - channels:], 'gz', [(i, i + 1) for i...  5.49 us
    unnamed x44, local copies, waits for them, and re-layouts  4.5 us
    dot_general x1, matrix products, body(): lax.dot_general(onehot, fields, (((0,), (0,)), ((), ())), preferred_eleme...  3.44 us
    dot_general x9, matrix products, conv_lane_dense(): jnp.dot(trio[dx:dx + px - 2, dy:dy + py - 2], grouped[dx * 3 + dy], prefe...  3.34 us
  transfers between devices with their start and end apart: 7, of which 3 were waited for; matrix products, arithmetic and copies ran while one was open for 10% of the time, Pallas kernels for 0%

profile of v13, /device:TPU:192, one launch (start us, length us, event | category | flops | bytes accessed | tf_op | source)
XLA Modules:
  0.0 87.5 jit_solution(11519150761569825921)
XLA Ops:
  0.0 2.1 %copy.43 = bf16[32,2,16,128]{0,2,3,1:T(8,128)(2,1)S(1)} copy(bf16[32,2,16,128]{3,2,1,0:T(8,128)(2,1)} %param.15) | data formatting | bytes 524288 | tf_op args[0]
  2.1 0.2 fusion.48
  2.3 0.2 copy.44
  2.6 0.9 %slice.219 = bf16[1,16,32,128]{3,2,1,0:T(8,128)(2,1)} reshape(bf16[1,16,32,4,32]{4,3,2,1,0:T(4,128)(2,1)S(1)} %copy.44) | data formatting | bytes 262144 | tf_op jit(solution)/shard_map/slice | solution.py:15
  3.5 2.4 %collective-permute-start = (bf16[1,16,32,128]{3,2,1,0:T(8,128)(2,1)}, bf16[1,16,32,128]{3,2,1,0:T(8,128)(2,1)}, u32[]{:S(2)}, u32[]{:S(2)}) collective-permute-start(bf16[1,16,32,128]{3,2,1,0:T(8,128)(2,1)} %slice.219), channel_id=1, source_target_pairs={{0,64},{64,128},{128,192},{192,256},{256,320},{320,384},{384,448},... | collective-permute-start | bytes 393224 | tf_op jit(solution)/shard_map/ppermute | solution.py:18
  5.9 0.2 copy.46
  6.2 0.9 %slice.221 = bf16[1,16,32,128]{3,2,1,0:T(8,128)(2,1)} reshape(bf16[1,16,32,4,32]{4,3,2,1,0:T(4,128)(2,1)S(1)} %copy.46) | data formatting | bytes 262144 | tf_op jit(solution)/shard_map/slice | solution.py:14
  7.1 1.3 %collective-permute-start.1 = (bf16[1,16,32,128]{3,2,1,0:T(8,128)(2,1)}, bf16[1,16,32,128]{3,2,1,0:T(8,128)(2,1)}, u32[]{:S(2)}, u32[]{:S(2)}) collective-permute-start(bf16[1,16,32,128]{3,2,1,0:T(8,128)(2,1)} %slice.221), channel_id=1, source_target_pairs={{64,0},{128,64},{192,128},{256,192},{320,256},{384,320},{448,384},... | collective-permute-start | bytes 393224 | tf_op jit(solution)/shard_map/ppermute | solution.py:20
  8.5 0.2 reduce_window_sum.11
  8.7 0.2 select_reduce_fusion.2
  8.9 0.2 copy.47
  9.1 0.6 copy-done.1
  9.7 0.3 maximum_bitcast_fusion
  10.1 0.6 copy.45
  10.6 0.5 reshape.141
  11.2 1.1 %fusion.22 = (bf16[3,3,128,128]{3,2,1,0:T(8,128)(2,1)S(1)}, bf16[3,3,1,128,128]{4,3,2,1,0:T(8,128)(2,1)S(1)}, bf16[3,3,1,128,128]{4,3,2,1,0:T(8,128)(2,1)S(1)}, bf16[3,3,128,128]{3,2,1,0:T(8,128)(2,1)S(1)}) fusion(bf16[3,3,32,32]{3,2,1,0:T(8,128)(2,1)} %copy-done.2, bf16[3,3,32,128]{3,2,1,0:T(8,128)(2,1)S(1)} %broadcast.84, ...), kind=kLoop, calls=%fused_computation.38 | loop fusion | flops 2359296 | bytes 1437696 | tf_op jit(solution)/shard_map/concatenate | solution.py:40
  12.4 0.9 %constant_dynamic-update-slice_fusion.2 = bf16[4,16,32,128]{3,2,1,0:T(8,128)(2,1)S(1)} fusion(bf16[1,16,32,128]{3,2,1,0:T(8,128)(2,1)} %collective-permute-done), kind=kLoop, calls=%fused_computation.80 | loop fusion | bytes 262144
  13.3 0.9 %constant_dynamic-update-slice_fusion = bf16[4,16,32,128]{3,2,1,0:T(8,128)(2,1)S(1)} fusion(bf16[4,16,32,128]{3,2,1,0:T(8,128)(2,1)S(1)} %constant_dynamic-update-slice_fusion.1, bf16[1,16,32,128]{3,2,1,0:T(8,128)(2,1)} %collective-permute-done.1), kind=kLoop, calls=%fused_computation.78 | loop fusion | bytes 262144 | tf_op jit(solution)/shard_map/concatenate | solution.py:16
  14.3 0.6 fusion.50
  14.9 3.5 %collective-permute-start.2 = (bf16[4,1,32,128]{3,2,1,0:T(8,128)(2,1)}, bf16[4,1,32,128]{3,2,1,0:T(8,128)(2,1)S(1)}, u32[]{:S(2)}, u32[]{:S(2)}) collective-permute-start(bf16[4,1,32,128]{3,2,1,0:T(8,128)(2,1)} %get-tuple-element.35), channel_id=1, source_target_pairs={{0,8},{8,16},{16,24},{24,32},{32,40},{40,48},{48,56},{1,9},{9,17},... | collective-permute-start | bytes 98312 | tf_op jit(solution)/shard_map/ppermute | solution.py:18
  18.3 1.3 %collective-permute-start.3 = (bf16[4,1,32,128]{3,2,1,0:T(8,128)(2,1)S(1)}, bf16[4,1,32,128]{3,2,1,0:T(8,128)(2,1)S(1)}, u32[]{:S(2)}, u32[]{:S(2)}) collective-permute-start(bf16[4,1,32,128]{3,2,1,0:T(8,128)(2,1)S(1)} %get-tuple-element.36), channel_id=1, source_target_pairs={{8,0},{16,8},{24,16},{32,24},{40,32},{48,40},{56,48},{9,1},{17,9},... | collective-permute-start | bytes 98312 | tf_op jit(solution)/shard_map/ppermute | solution.py:20
  19.6 0.1 pad_maximum_fusion
  19.8 1.3 %scatter_custom_fusion = bf16[448]{0:T(512)(128)(2,1)S(1)} fusion(s32[128]{0:T(128)S(1)} %get-tuple-element.47, bf16[128]{0:T(256)(128)(2,1)S(1)} %convert_element_type.63, bf16[]{:T(256)} %constant.81.clone.1), kind=kCustom, calls=%fused_computation.110 | custom fusion | bytes 898 | tf_op jit(solution)/shard_map/scatter | solution.py:139
  21.1 0.2 reshape.171
  21.3 2.9 %collective-permute-done.3 = bf16[4,1,32,128]{3,2,1,0:T(8,128)(2,1)S(1)} collective-permute-done((bf16[4,1,32,128]{3,2,1,0:T(8,128)(2,1)S(1)}, bf16[4,1,32,128]{3,2,1,0:T(8,128)(2,1)S(1)}, u32[]{:S(2)}, u32[]{:S(2)}) %collective-permute-start.3) | collective-permute-done | bytes 32800 | tf_op jit(solution)/shard_map/ppermute | solution.py:20
  24.2 0.3 fusion.49
  24.5 0.5 fusion.4
  25.0 0.4 fusion.33
  25.4 0.4 fusion.32
  25.7 0.4 fusion.31
  26.1 0.4 fusion.30
  26.5 0.4 fusion.29
  26.8 0.4 fusion.28
  27.2 0.4 fusion.27
  27.6 0.4 fusion.26
  27.9 0.1 pad_maximum_fusion.2
  28.1 1.9 %collective-permute-start.5 = (bf16[4,18,32]{2,1,0:T(8,128)(2,1)S(1)}, bf16[4,18,32]{2,1,0:T(8,128)(2,1)S(1)}, u32[]{:S(2)}, u32[]{:S(2)}) collective-permute-start(bf16[4,18,32]{2,1,0:T(8,128)(2,1)S(1)} %copy.53), channel_id=1, source_target_pairs={{1,0},{2,1},{3,2},{4,3},{5,4},{6,5},{7,6},{9,8},{10,9},{11,10},{12... | collective-permute-start | bytes 13832 | tf_op jit(solution)/shard_map/ppermute | solution.py:110
  30.1 5.5 %collective-permute-start.4 = (bf16[4,18,32]{2,1,0:T(8,128)(2,1)S(1)}, bf16[4,18,32]{2,1,0:T(8,128)(2,1)S(1)}, u32[]{:S(2)}, u32[]{:S(2)}) collective-permute-start(bf16[4,18,32]{2,1,0:T(8,128)(2,1)S(1)} %copy.51), channel_id=1, source_target_pairs={{0,1},{1,2},{2,3},{3,4},{4,5},{5,6},{6,7},{8,9},{9,10},{10,11},{11... | collective-permute-start | bytes 13832 | tf_op jit(solution)/shard_map/ppermute | solution.py:107
  35.6 0.4 fusion.12
  36.0 1.1 %collective-permute-done.4 = bf16[4,18,32]{2,1,0:T(8,128)(2,1)S(1)} collective-permute-done((bf16[4,18,32]{2,1,0:T(8,128)(2,1)S(1)}, bf16[4,18,32]{2,1,0:T(8,128)(2,1)S(1)}, u32[]{:S(2)}, u32[]{:S(2)}) %collective-permute-start.4) | collective-permute-done | bytes 4640 | tf_op jit(solution)/shard_map/ppermute | solution.py:107
  37.5 0.1 constant_dynamic-update-slice_fusion.6
  37.6 0.1 constant_dynamic-update-slice_fusion.4
  37.7 0.1 constant_dynamic-update-slice_fusion.3
  37.8 0.2 fusion.51
  38.1 0.1 scatter-add.6
  38.3 0.2 fusion.52
  38.5 0.3 scatter-add.9
  38.8 0.5 reshape.145
  39.3 3.4 %fusion.15 = bf16[4,8,8,128]{3,2,1,0:T(8,128)(2,1)S(1)} fusion(s32[4096]{0:T(1024)S(1)} %bitcast.169, f32[4096,32]{1,0:T(8,128)S(1)} %reshape.145, f32[32]{0:T(128)S(1)} %copy-done.11), kind=kOutput, calls=%fused_computation.24 | convolution fusion | flops 273088512 | bytes 606336 | tf_op jit(solution)/shard_map/dot_general | solution.py:117
  42.8 0.2 convolution_convert_fusion
  43.1 0.8 fusion.24
  44.0 12.7 %all-to-all-start = ((bf16[64,8,256]{2,1,0:T(8,128)(2,1)}), bf16[64,8,256]{2,1,0:T(8,128)(2,1)S(1)}, u32[]{:S(2)}, u32[]{:S(2)}) async-start(bf16[64,8,256]{2,1,0:T(8,128)(2,1)} %fusion.24), calls=%async_computation | async-start | bytes 524288 | tf_op jit(solution)/shard_map/all_to_all | solution.py:145
  56.6 13.2 %all-to-all-done = bf16[64,8,256]{2,1,0:T(8,128)(2,1)S(1)} async-done(((bf16[64,8,256]{2,1,0:T(8,128)(2,1)}), bf16[64,8,256]{2,1,0:T(8,128)(2,1)S(1)}, u32[]{:S(2)}, u32[]{:S(2)}) %all-to-all-start) | async-done | bytes 262176 | tf_op jit(solution)/shard_map/all_to_all | solution.py:145
  69.9 0.1 fusion.39
  70.1 0.1 reshape.149
  70.2 0.4 multiply_convert_fusion.1
  70.6 0.4 convolution_bitcast_fusion
  71.0 0.1 select_reduce_fusion.1
  71.1 0.1 all_to_all.10
  71.2 14.2 %all_to_all.14 = f32[64,1,7]{2,1,0:T(1,128)S(1)} all-to-all(f32[64,1,7]{2,1,0:T(1,128)S(1)} %bitcast.162), channel_id=1, replica_groups=mesh['gx'=8,'gy'=8,'gz'=8] {'gx','gy'}, dimensions={0} | all-to-all | bytes 3584 | tf_op jit(solution)/shard_map/all_to_all | solution.py:163
  85.5 0.5 broadcast.120
  86.0 0.7 reduce.11
  86.7 0.1 broadcast_in_dim.52
  86.8 0.7 select_reduce_fusion
  (63 shorter events, 1.3 us)
Async XLA Ops:
  0.0 70.6 %copy-start = (bf16[512,512]{1,0:T(8,128)(2,1)S(1)}, bf16[512,512]{1,0:T(8,128)(2,1)}, u32[]{:S(2)}) copy-start(bf16[512,512]{1,0:T(8,128)(2,1)} %param.23) | copy-start | bytes 1572868
  2.3 6.1 %copy-start.4 = (s32[128,1]{0,1:T(1,128)S(1)}, s32[128,1]{0,1:T(1,128)}, u32[]{:S(2)}) copy-start(s32[128,1]{0,1:T(1,128)} %param.19) | copy-start | bytes 1540
  2.3 6.6 %copy-start.3 = (bf16[27,32,32]{2,1,0:T(8,128)(2,1)S(1)}, bf16[27,32,32]{2,1,0:T(8,128)(2,1)}, u32[]{:S(2)}) copy-start(bf16[27,32,32]{2,1,0:T(8,128)(2,1)} %param.17) | copy-start | bytes 165892
  3.5 8.8 %collective-permute-start = (bf16[1,16,32,128]{3,2,1,0:T(8,128)(2,1)}, bf16[1,16,32,128]{3,2,1,0:T(8,128)(2,1)}, u32[]{:S(2)}, u32[]{:S(2)}) collective-permute-start(bf16[1,16,32,128]{3,2,1,0:T(8,128)(2,1)} %slice.219), channel_id=1, source_target_pairs={{0,64},{64,128},{128,192},{192,256},{256,320},{320,384},{384,448},... | collective-permute-start | bytes 393224 | tf_op jit(solution)/shard_map/ppermute | solution.py:18
  7.1 6.2 %collective-permute-start.1 = (bf16[1,16,32,128]{3,2,1,0:T(8,128)(2,1)}, bf16[1,16,32,128]{3,2,1,0:T(8,128)(2,1)}, u32[]{:S(2)}, u32[]{:S(2)}) collective-permute-start(bf16[1,16,32,128]{3,2,1,0:T(8,128)(2,1)} %slice.221), channel_id=1, source_target_pairs={{64,0},{128,64},{192,128},{256,192},{320,256},{384,320},{448,384},... | collective-permute-start | bytes 393224 | tf_op jit(solution)/shard_map/ppermute | solution.py:20
  9.1 0.6 copy-start.1
  9.1 0.6 copy-start.2
  12.3 7.4 %copy-start.10 = (s32[128]{0:T(128)S(1)}, s32[128]{0:T(128)}, u32[]{:S(2)}) copy-start(s32[128]{0:T(128)} %param.20) | copy-start | bytes 1540
  14.9 6.4 %collective-permute-start.2 = (bf16[4,1,32,128]{3,2,1,0:T(8,128)(2,1)}, bf16[4,1,32,128]{3,2,1,0:T(8,128)(2,1)S(1)}, u32[]{:S(2)}, u32[]{:S(2)}) collective-permute-start(bf16[4,1,32,128]{3,2,1,0:T(8,128)(2,1)} %get-tuple-element.35), channel_id=1, source_target_pairs={{0,8},{8,16},{16,24},{24,32},{32,40},{40,48},{48,56},{1,9},{9,17},... | collective-permute-start | bytes 98312 | tf_op jit(solution)/shard_map/ppermute | solution.py:18
  18.3 5.8 %collective-permute-start.3 = (bf16[4,1,32,128]{3,2,1,0:T(8,128)(2,1)S(1)}, bf16[4,1,32,128]{3,2,1,0:T(8,128)(2,1)S(1)}, u32[]{:S(2)}, u32[]{:S(2)}) collective-permute-start(bf16[4,1,32,128]{3,2,1,0:T(8,128)(2,1)S(1)} %get-tuple-element.36), channel_id=1, source_target_pairs={{8,0},{16,8},{24,16},{32,24},{40,32},{48,40},{56,48},{9,1},{17,9},... | collective-permute-start | bytes 98312 | tf_op jit(solution)/shard_map/ppermute | solution.py:20
  28.1 10.1 %collective-permute-start.5 = (bf16[4,18,32]{2,1,0:T(8,128)(2,1)S(1)}, bf16[4,18,32]{2,1,0:T(8,128)(2,1)S(1)}, u32[]{:S(2)}, u32[]{:S(2)}) collective-permute-start(bf16[4,18,32]{2,1,0:T(8,128)(2,1)S(1)} %copy.53), channel_id=1, source_target_pairs={{1,0},{2,1},{3,2},{4,3},{5,4},{6,5},{7,6},{9,8},{10,9},{11,10},{12... | collective-permute-start | bytes 13832 | tf_op jit(solution)/shard_map/ppermute | solution.py:110
  30.1 7.0 %collective-permute-start.4 = (bf16[4,18,32]{2,1,0:T(8,128)(2,1)S(1)}, bf16[4,18,32]{2,1,0:T(8,128)(2,1)S(1)}, u32[]{:S(2)}, u32[]{:S(2)}) collective-permute-start(bf16[4,18,32]{2,1,0:T(8,128)(2,1)S(1)} %copy.51), channel_id=1, source_target_pairs={{0,1},{1,2},{2,3},{3,4},{4,5},{5,6},{6,7},{8,9},{9,10},{10,11},{11... | collective-permute-start | bytes 13832 | tf_op jit(solution)/shard_map/ppermute | solution.py:107
  38.0 1.3 %copy-start.7 = (s32[2,16,128]{2,1,0:T(8,128)S(1)}, s32[2,16,128]{2,1,0:T(8,128)}, u32[]{:S(2)}) copy-start(s32[2,16,128]{2,1,0:T(8,128)} %param.16) | copy-start | bytes 49156
  38.0 1.3 %copy-start.11 = (f32[32]{0:T(128)S(1)}, f32[32]{0:T(128)}, u32[]{:S(2)}) copy-start(f32[32]{0:T(128)} %param.18) | copy-start | bytes 388
  42.8 13.9 %copy-start.5 = (bf16[512]{0:T(512)(128)(2,1)S(1)}, bf16[512]{0:T(512)(128)(2,1)}, u32[]{:S(2)}) copy-start(bf16[512]{0:T(512)(128)(2,1)} %param.25) | copy-start | bytes 3076
  42.8 27.4 %copy-start.6 = (bf16[256,512]{1,0:T(8,128)(2,1)S(1)}, bf16[256,512]{1,0:T(8,128)(2,1)}, u32[]{:S(2)}) copy-start(bf16[256,512]{1,0:T(8,128)(2,1)} %param.21) | copy-start | bytes 786436
  42.8 27.4 %copy-start.8 = (f32[512]{0:T(512)S(1)}, f32[512]{0:T(512)}, u32[]{:S(2)}) copy-start(f32[512]{0:T(512)} %param.22) | copy-start | bytes 6148
  42.8 27.8 %copy-start.9 = (f32[512]{0:T(512)S(1)}, f32[512]{0:T(512)}, u32[]{:S(2)}) copy-start(f32[512]{0:T(512)} %param.24) | copy-start | bytes 6148
  44.0 25.9 %all-to-all-start = ((bf16[64,8,256]{2,1,0:T(8,128)(2,1)}), bf16[64,8,256]{2,1,0:T(8,128)(2,1)S(1)}, u32[]{:S(2)}, u32[]{:S(2)}) async-start(bf16[64,8,256]{2,1,0:T(8,128)(2,1)} %fusion.24), calls=%async_computation | async-start | bytes 524288 | tf_op jit(solution)/shard_map/all_to_all | solution.py:145

commit v14 on v9

--- a/solution.py
+++ b/solution.py
@@ -93,12 +93,21 @@
     channels, extent_x, extent_y, extent_z = features.shape
     volume = extent_x * extent_y * extent_z
     chunk = 4 * channels
-    cells = (
-        features.reshape(channels, extent_x, extent_y, extent_z // 4, 4)
-        .transpose(1, 2, 3, 4, 0)
-        .reshape(extent_x, extent_y, extent_z // 4, chunk)
+
+    def lane_dense(block):
+        return (
+            block.reshape(channels, block.shape[1], extent_y, extent_z // 4, 4)
+            .transpose(1, 2, 3, 4, 0)
+            .reshape(block.shape[1], extent_y, extent_z // 4, chunk)
+        )
+
+    count_x = lax.axis_size("gx")
+    from_below = lax.ppermute(features[:, -1:], "gx", [(i, i + 1) for i in range(count_x - 1)])
+    from_above = lax.ppermute(features[:, :1], "gx", [(i + 1, i) for i in range(count_x - 1)])
+    cells = jnp.concatenate(
+        [lane_dense(from_below), lane_dense(features), lane_dense(from_above)], axis=0
     )
-    padded = extended(cells, (("gx", 0), ("gy", 1)), 1)
+    padded = extended(cells, (("gy", 1),), 1)
     count_z = lax.axis_size("gz")
     low = lax.ppermute(
         padded[:, :, -1, chunk - channels :], "gz", [(i, i + 1) for i in range(count_z - 1)]

time: 86.2 us -> 91.8 us (1.065)
  local copies, waits for them, and re-layouts: 11.9 us -> 15.2 us
  other arithmetic: 6.51 us -> 8.62 us
  waiting for transfers between devices: 17.1 us -> 15.1 us
  starting transfers between devices: 28.6 us -> 30.6 us
    ppermute x0 -> x2, starting transfers between devices: none -> 3.95 us  [the longest x1 2.67 us: body(): lax.ppermute(features[:, -1:], 'gx', [(i, i + 1) for i in range(count_x -...]
    transpose x1 -> x3, local copies, waits for them, and re-layouts: 0.55 us -> 3.13 us  [lane_dense(): return block.reshape(channels, block.shape[1], extent_y, extent_z // 4, 4...]
    ppermute x2 -> x1, waiting for transfers between devices: 1.98 us -> 0.01 us  [extended(): lax.ppermute(head, axis, [((i + 1) % count, i) for i in range(ends)])]
    ppermute x2 -> x1, starting transfers between devices: 2.57 us -> 1.29 us  [extended(): lax.ppermute(head, axis, [((i + 1) % count, i) for i in range(ends)])]
    reshape x1, local copies, waits for them, and re-layouts: 0.16 us -> 1.08 us  [banded_weight(): conv_weight.reshape(3, 3, 3, channels, channels).transpose(0, 1, 2, 4, 3)]
    ppermute x2 -> x1, starting transfers between devices: 5.23 us -> 4.55 us  [extended(): lax.ppermute(tail, axis, [(i, (i + 1) % count) for i in range(ends)])]
  transfers between devices with their start and end apart: 7 -> 7, of which waited for: 3 -> 2; matrix products, arithmetic and copies ran while one was open for 12% -> 15% of each run, Pallas kernels for 0% -> 0%
where the time goes in v14:
time: 91.8 us; the launch traced here: 91.2 us
  starting transfers between devices  30.6 us (33%)
  local copies, waits for them, and re-layouts  15.2 us (17%)
  waiting for transfers between devices  15.1 us (16%)
  blocking collectives  14.2 us (15%)
  other arithmetic  8.62 us (9%)
  matrix products  6.7 us (7%)
    all_to_all x1, blocking collectives, body(): lax.all_to_all(owner_scores.reshape(groups, capacity), ('gx', 'gy'), spli...  14.2 us
    all_to_all x1, starting transfers between devices, body(): lax.all_to_all(send, ('gx', 'gy'), split_axis=0, concat_axis=0, tiled=True)  13.3 us
    all_to_all x1, waiting for transfers between devices, body(): lax.all_to_all(send, ('gx', 'gy'), split_axis=0, concat_axis=0, tiled=True)  13.2 us
    ppermute x1, starting transfers between devices, body(): lax.ppermute(padded[:, :, -1, chunk - channels:], 'gz', [(i, i + 1) for i...  5.49 us
    unnamed x60, local copies, waits for them, and re-layouts  4.74 us
    ppermute x1, starting transfers between devices, extended(): lax.ppermute(tail, axis, [(i, (i + 1) % count) for i in range(ends)])  4.55 us
    dot_general x1, matrix products, body(): lax.dot_general(onehot, fields, (((0,), (0,)), ((), ())), preferred_eleme...  3.44 us
    transpose x3, local copies, waits for them, and re-layouts, lane_dense(): return block.reshape(channels, block.shape[1], extent_y, extent_z // 4, 4...  3.13 us
  transfers between devices with their start and end apart: 7, of which 2 were waited for; matrix products, arithmetic and copies ran while one was open for 15% of the time, Pallas kernels for 0%

profile of v14, /device:TPU:192, one launch (start us, length us, event | category | flops | bytes accessed | tf_op | source)
XLA Modules:
  0.0 91.2 jit_solution(11764096581977372584)
XLA Ops:
  0.0 2.1 %copy.49 = bf16[32,2,16,128]{0,2,3,1:T(8,128)(2,1)S(1)} copy(bf16[32,2,16,128]{3,2,1,0:T(8,128)(2,1)} %param.15) | data formatting | bytes 524288 | tf_op args[0]
  2.1 1.2 %fusion.41 = (bf16[32,1,16,128]{0,2,3,1:T(8,128)(2,1)}, bf16[32,1,16,128]{0,2,3,1:T(8,128)(2,1)}) fusion(bf16[32,2,16,128]{0,2,3,1:T(8,128)(2,1)S(1)} %copy.49), kind=kLoop, calls=%fused_computation.130 | loop fusion | bytes 524288 | tf_op jit(solution)/shard_map/slice | solution.py:106
  3.3 2.7 %collective-permute-start = (bf16[32,1,16,128]{0,2,3,1:T(8,128)(2,1)}, bf16[32,1,16,128]{0,2,3,1:T(8,128)(2,1)}, u32[]{:S(2)}, u32[]{:S(2)}) collective-permute-start(bf16[32,1,16,128]{0,2,3,1:T(8,128)(2,1)} %get-tuple-element.30), channel_id=1, source_target_pairs={{0,64},{64,128},{128,192},{192,256},{256,320},{320,384},{384,448},... | collective-permute-start | bytes 393224 | tf_op jit(solution)/shard_map/ppermute | solution.py:105
  5.9 1.3 %collective-permute-start.1 = (bf16[32,1,16,128]{0,2,3,1:T(8,128)(2,1)}, bf16[32,1,16,128]{0,2,3,1:T(8,128)(2,1)}, u32[]{:S(2)}, u32[]{:S(2)}) collective-permute-start(bf16[32,1,16,128]{0,2,3,1:T(8,128)(2,1)} %get-tuple-element.29), channel_id=1, source_target_pairs={{64,0},{128,64},{192,128},{256,192},{320,256},{384,320},{448,384},... | collective-permute-start | bytes 393224 | tf_op jit(solution)/shard_map/ppermute | solution.py:106
  7.2 0.7 fusion.31
  8.0 0.2 reduce_window_sum.11
  8.1 0.8 select_reduce_fusion.2
  9.0 0.7 fusion.38
  9.6 0.7 multiply_add_fusion
  10.3 1.1 %copy.55 = bf16[3,3,3,32,32]{3,4,1,0,2:T(8,128)(2,1)S(1)} copy(bf16[3,3,3,32,32]{4,3,2,1,0:T(8,128)(2,1)} %bitcast.92) | data formatting | bytes 110592 | tf_op jit(solution)/shard_map/reshape | solution.py:28
  11.5 1.0 %fusion.11 = (bf16[3,3,128,128]{3,2,1,0:T(8,128)(2,1)}, bf16[3,3,1,128,128]{4,3,2,1,0:T(8,128)(2,1)S(1)}, bf16[3,3,1,128,128]{4,3,2,1,0:T(8,128)(2,1)S(1)}, bf16[3,3,128,128]{3,2,1,0:T(8,128)(2,1)}) fusion(bf16[3,3,32,32]{3,2,1,0:T(8,128)(2,1)S(1)} %get-tuple-element.44, bf16[3,3,32,128]{3,2,1,0:T(8,128)(2,1)S(1)} %broadcast.84, ...), kind=kLoop, calls=%fused_computation.32 | loop fusion | flops 2359296 | bytes 1437696 | tf_op jit(solution)/shard_map/concatenate | solution.py:40
  12.5 0.3 maximum_bitcast_fusion
  12.9 0.6 copy.52
  13.4 0.5 reshape.156
  13.9 1.3 %copy.50 = bf16[1,16,32,4,32]{4,3,2,1,0:T(4,128)(2,1)S(1)} copy(bf16[1,16,32,4,32]{4,1,3,2,0:T(8,128)(2,1)} %bitcast.5) | data formatting | bytes 262144 | tf_op jit(solution)/shard_map/transpose | solution.py:100
  15.2 0.3 reshape.154
  15.6 1.3 %copy.54 = bf16[1,16,32,4,32]{4,3,2,1,0:T(4,128)(2,1)S(1)} copy(bf16[1,16,32,4,32]{4,1,3,2,0:T(8,128)(2,1)} %bitcast.9) | data formatting | bytes 262144 | tf_op jit(solution)/shard_map/transpose | solution.py:100
  16.9 0.3 reshape.158
  17.2 1.3 %collective-permute-start.3 = (bf16[4,1,32,128]{3,2,1,0:T(8,128)(2,1)S(1)}, bf16[4,1,32,128]{3,2,1,0:T(8,128)(2,1)S(1)}, u32[]{:S(2)}, u32[]{:S(2)}) collective-permute-start(bf16[4,1,32,128]{3,2,1,0:T(8,128)(2,1)S(1)} %get-tuple-element.36), channel_id=1, source_target_pairs={{8,0},{16,8},{24,16},{32,24},{40,32},{48,40},{56,48},{9,1},{17,9},... | collective-permute-start | bytes 98312 | tf_op jit(solution)/shard_map/ppermute | solution.py:20
  18.5 4.5 %collective-permute-start.2 = (bf16[4,1,32,128]{3,2,1,0:T(8,128)(2,1)S(1)}, bf16[4,1,32,128]{3,2,1,0:T(8,128)(2,1)S(1)}, u32[]{:S(2)}, u32[]{:S(2)}) collective-permute-start(bf16[4,1,32,128]{3,2,1,0:T(8,128)(2,1)S(1)} %get-tuple-element.35), channel_id=1, source_target_pairs={{0,8},{8,16},{16,24},{24,32},{32,40},{40,48},{48,56},{1,9},{9,17},... | collective-permute-start | bytes 98312 | tf_op jit(solution)/shard_map/ppermute | solution.py:18
  23.1 1.0 %pad_maximum_fusion = bf16[3,3,3,128,128]{4,3,2,1,0:T(8,128)(2,1)} fusion(bf16[3,3,1,128,128]{4,3,2,1,0:T(8,128)(2,1)S(1)} %get-tuple-element.38, bf16[3,3,1,128,128]{4,3,2,1,0:T(8,128)(2,1)S(1)} %maximum_bitcast_fusion, bf16[3,3,1,128,128]{4,3,2,1,0:T(8,128)(2,1)S(1)} %get-tuple-element.41), kind=kLoop, calls=%fused_computation.15 | loop fusion | flops 884736 | bytes 1769472 | tf_op jit(solution)/shard_map/stack | solution.py:46
  24.1 1.3 %scatter_custom_fusion = bf16[448]{0:T(512)(128)(2,1)S(1)} fusion(s32[128]{0:T(128)S(1)} %get-tuple-element.47, bf16[128]{0:T(256)(128)(2,1)S(1)} %convert_element_type.63, bf16[]{:T(256)} %constant.81.clone.1), kind=kCustom, calls=%fused_computation.122 | custom fusion | bytes 898 | tf_op jit(solution)/shard_map/scatter | solution.py:144
  25.4 0.2 reshape.181
  25.7 0.3 fusion.42
  26.0 0.1 slice_dynamic-update-slice_fusion.17
  26.2 0.1 slice_dynamic-update-slice_fusion.15
  26.5 0.1 slice_dynamic-update-slice_fusion.13
  26.8 0.1 slice_dynamic-update-slice_fusion.11
  27.1 0.1 slice_dynamic-update-slice_fusion.9
  27.4 0.1 slice_dynamic-update-slice_fusion.7
  27.7 0.1 slice_dynamic-update-slice_fusion.5
  27.9 0.1 slice_dynamic-update-slice_fusion.3
  28.2 0.1 slice_dynamic-update-slice_fusion.1
  28.5 0.1 pad_maximum_fusion.6
  28.7 5.5 %collective-permute-start.4 = (bf16[4,18,32]{2,1,0:T(8,128)(2,1)S(1)}, bf16[4,18,32]{2,1,0:T(8,128)(2,1)S(1)}, u32[]{:S(2)}, u32[]{:S(2)}) collective-permute-start(bf16[4,18,32]{2,1,0:T(8,128)(2,1)S(1)} %copy.59), channel_id=1, source_target_pairs={{0,1},{1,2},{2,3},{3,4},{4,5},{5,6},{6,7},{8,9},{9,10},{10,11},{11... | collective-permute-start | bytes 13832 | tf_op jit(solution)/shard_map/ppermute | solution.py:112
  34.2 2.1 %collective-permute-start.5 = (bf16[4,18,32]{2,1,0:T(8,128)(2,1)S(1)}, bf16[4,18,32]{2,1,0:T(8,128)(2,1)S(1)}, u32[]{:S(2)}, u32[]{:S(2)}) collective-permute-start(bf16[4,18,32]{2,1,0:T(8,128)(2,1)S(1)} %copy.61), channel_id=1, source_target_pairs={{1,0},{2,1},{3,2},{4,3},{5,4},{6,5},{7,6},{9,8},{10,9},{11,10},{12... | collective-permute-start | bytes 13832 | tf_op jit(solution)/shard_map/ppermute | solution.py:115
  36.3 2.0 %fusion.44 = f32[2,16,32,128]{3,2,1,0:T(8,128)S(1)} fusion(bf16[2,16,32,3456]{3,2,1,0:T(8,128)(2,1)S(1)} %slice_dynamic-update-slice_fusion, bf16[3456,128,1,1]{1,0,3,2:T(8,128)(2,1)S(1)} %bitcast.89), kind=kOutput, calls=%fused_computation.133 | convolution fusion | flops 905969664 | bytes 8486912 | tf_op jit(solution)/shard_map/dot_general | solution.py:65
  38.4 0.1 constant_dynamic-update-slice_fusion.11
  38.6 0.1 constant_dynamic-update-slice_fusion.8
  38.7 0.1 constant_dynamic-update-slice_fusion.7
  38.9 0.1 constant_dynamic-update-slice_fusion.5
  39.0 0.1 constant_dynamic-update-slice_fusion.4
  39.1 0.2 fusion.45
  39.3 0.1 scatter-add.6
  39.4 1.9 %collective-permute-done.5 = bf16[4,18,32]{2,1,0:T(8,128)(2,1)S(1)} collective-permute-done((bf16[4,18,32]{2,1,0:T(8,128)(2,1)S(1)}, bf16[4,18,32]{2,1,0:T(8,128)(2,1)S(1)}, u32[]{:S(2)}, u32[]{:S(2)}) %collective-permute-start.5) | collective-permute-done | bytes 4640 | tf_op jit(solution)/shard_map/ppermute | solution.py:115
  41.4 0.2 fusion.46
  41.6 0.3 scatter-add.9
  42.0 0.5 reshape.163
  42.5 3.4 %fusion.4 = bf16[4,8,8,128]{3,2,1,0:T(8,128)(2,1)S(1)} fusion(s32[4096]{0:T(1024)S(1)} %bitcast.100, f32[4096,32]{1,0:T(8,128)S(1)} %reshape.163, f32[32]{0:T(128)S(1)} %copy-done.10), kind=kOutput, calls=%fused_computation.10 | convolution fusion | flops 273088512 | bytes 606336 | tf_op jit(solution)/shard_map/dot_general | solution.py:122
  45.9 0.2 convolution_convert_fusion
  46.2 0.8 fusion.21
  47.1 13.3 %all-to-all-start = ((bf16[64,8,256]{2,1,0:T(8,128)(2,1)}), bf16[64,8,256]{2,1,0:T(8,128)(2,1)S(1)}, u32[]{:S(2)}, u32[]{:S(2)}) async-start(bf16[64,8,256]{2,1,0:T(8,128)(2,1)} %fusion.21), calls=%async_computation | async-start | bytes 524288 | tf_op jit(solution)/shard_map/all_to_all | solution.py:150
  60.4 13.2 %all-to-all-done = bf16[64,8,256]{2,1,0:T(8,128)(2,1)S(1)} async-done(((bf16[64,8,256]{2,1,0:T(8,128)(2,1)}), bf16[64,8,256]{2,1,0:T(8,128)(2,1)S(1)}, u32[]{:S(2)}, u32[]{:S(2)}) %all-to-all-start) | async-done | bytes 262176 | tf_op jit(solution)/shard_map/all_to_all | solution.py:150
  73.7 0.1 fusion.32
  73.8 0.1 reshape.167
  74.0 0.4 multiply_convert_fusion.1
  74.4 0.4 convolution_bitcast_fusion
  74.7 0.1 select_reduce_fusion.1
  74.8 0.1 all_to_all.10
  75.0 14.2 %all_to_all.14 = f32[64,1,7]{2,1,0:T(1,128)S(1)} all-to-all(f32[64,1,7]{2,1,0:T(1,128)S(1)} %bitcast.93), channel_id=1, replica_groups=mesh['gx'=8,'gy'=8,'gz'=8] {'gx','gy'}, dimensions={0} | all-to-all | bytes 3584 | tf_op jit(solution)/shard_map/all_to_all | solution.py:168
  89.2 0.5 broadcast.113
  89.7 0.7 reduce.11
  90.4 0.1 broadcast_in_dim.52
  90.6 0.7 select_reduce_fusion
  (79 shorter events, 2.3 us)
Async XLA Ops:
  0.0 74.3 %copy-start = (bf16[512,512]{1,0:T(8,128)(2,1)S(1)}, bf16[512,512]{1,0:T(8,128)(2,1)}, u32[]{:S(2)}) copy-start(bf16[512,512]{1,0:T(8,128)(2,1)} %param.23) | copy-start | bytes 1572868
  3.3 20.8 %copy-start.9 = (s32[128]{0:T(128)S(1)}, s32[128]{0:T(128)}, u32[]{:S(2)}) copy-start(s32[128]{0:T(128)} %param.20) | copy-start | bytes 1540
  3.3 10.7 %collective-permute-start = (bf16[32,1,16,128]{0,2,3,1:T(8,128)(2,1)}, bf16[32,1,16,128]{0,2,3,1:T(8,128)(2,1)}, u32[]{:S(2)}, u32[]{:S(2)}) collective-permute-start(bf16[32,1,16,128]{0,2,3,1:T(8,128)(2,1)} %get-tuple-element.30), channel_id=1, source_target_pairs={{0,64},{64,128},{128,192},{192,256},{256,320},{320,384},{384,448},... | collective-permute-start | bytes 393224 | tf_op jit(solution)/shard_map/ppermute | solution.py:105
  5.9 9.6 %collective-permute-start.1 = (bf16[32,1,16,128]{0,2,3,1:T(8,128)(2,1)}, bf16[32,1,16,128]{0,2,3,1:T(8,128)(2,1)}, u32[]{:S(2)}, u32[]{:S(2)}) collective-permute-start(bf16[32,1,16,128]{0,2,3,1:T(8,128)(2,1)} %get-tuple-element.29), channel_id=1, source_target_pairs={{64,0},{128,64},{192,128},{256,192},{320,256},{384,320},{448,384},... | collective-permute-start | bytes 393224 | tf_op jit(solution)/shard_map/ppermute | solution.py:106
  17.2 8.4 %collective-permute-start.3 = (bf16[4,1,32,128]{3,2,1,0:T(8,128)(2,1)S(1)}, bf16[4,1,32,128]{3,2,1,0:T(8,128)(2,1)S(1)}, u32[]{:S(2)}, u32[]{:S(2)}) collective-permute-start(bf16[4,1,32,128]{3,2,1,0:T(8,128)(2,1)S(1)} %get-tuple-element.36), channel_id=1, source_target_pairs={{8,0},{16,8},{24,16},{32,24},{40,32},{48,40},{56,48},{9,1},{17,9},... | collective-permute-start | bytes 98312 | tf_op jit(solution)/shard_map/ppermute | solution.py:20
  18.5 7.1 %collective-permute-start.2 = (bf16[4,1,32,128]{3,2,1,0:T(8,128)(2,1)S(1)}, bf16[4,1,32,128]{3,2,1,0:T(8,128)(2,1)S(1)}, u32[]{:S(2)}, u32[]{:S(2)}) collective-permute-start(bf16[4,1,32,128]{3,2,1,0:T(8,128)(2,1)S(1)} %get-tuple-element.35), channel_id=1, source_target_pairs={{0,8},{8,16},{16,24},{24,32},{32,40},{40,48},{48,56},{1,9},{9,17},... | collective-permute-start | bytes 98312 | tf_op jit(solution)/shard_map/ppermute | solution.py:18
  27.0 9.3 %copy-start.3 = (bf16[3,3,3,128,128]{4,3,2,1,0:T(8,128)(2,1)S(1)}, bf16[3,3,3,128,128]{4,3,2,1,0:T(8,128)(2,1)}, u32[]{:S(2)}) copy-start(bf16[3,3,3,128,128]{4,3,2,1,0:T(8,128)(2,1)} %pad_maximum_fusion) | copy-start | bytes 2654212
  28.7 9.6 %collective-permute-start.4 = (bf16[4,18,32]{2,1,0:T(8,128)(2,1)S(1)}, bf16[4,18,32]{2,1,0:T(8,128)(2,1)S(1)}, u32[]{:S(2)}, u32[]{:S(2)}) collective-permute-start(bf16[4,18,32]{2,1,0:T(8,128)(2,1)S(1)} %copy.59), channel_id=1, source_target_pairs={{0,1},{1,2},{2,3},{3,4},{4,5},{5,6},{6,7},{8,9},{9,10},{10,11},{11... | collective-permute-start | bytes 13832 | tf_op jit(solution)/shard_map/ppermute | solution.py:112
  34.2 4.9 %copy-start.2 = (bf16[3,3,128,128]{3,2,1,0:T(8,128)(2,1)S(1)}, bf16[3,3,128,128]{3,2,1,0:T(8,128)(2,1)}, u32[]{:S(2)}) copy-start(bf16[3,3,128,128]{3,2,1,0:T(8,128)(2,1)} %get-tuple-element.42) | copy-start | bytes 884740
  34.2 7.1 %collective-permute-start.5 = (bf16[4,18,32]{2,1,0:T(8,128)(2,1)S(1)}, bf16[4,18,32]{2,1,0:T(8,128)(2,1)S(1)}, u32[]{:S(2)}, u32[]{:S(2)}) collective-permute-start(bf16[4,18,32]{2,1,0:T(8,128)(2,1)S(1)} %copy.61), channel_id=1, source_target_pairs={{1,0},{2,1},{3,2},{4,3},{5,4},{6,5},{7,6},{9,8},{10,9},{11,10},{12... | collective-permute-start | bytes 13832 | tf_op jit(solution)/shard_map/ppermute | solution.py:115
  36.3 5.1 %copy-start.1 = (bf16[3,3,128,128]{3,2,1,0:T(8,128)(2,1)S(1)}, bf16[3,3,128,128]{3,2,1,0:T(8,128)(2,1)}, u32[]{:S(2)}) copy-start(bf16[3,3,128,128]{3,2,1,0:T(8,128)(2,1)} %get-tuple-element.37) | copy-start | bytes 884740
  36.3 6.2 %copy-start.6 = (s32[2,16,128]{2,1,0:T(8,128)S(1)}, s32[2,16,128]{2,1,0:T(8,128)}, u32[]{:S(2)}) copy-start(s32[2,16,128]{2,1,0:T(8,128)} %param.16) | copy-start | bytes 49156
  36.3 6.2 %copy-start.10 = (f32[32]{0:T(128)S(1)}, f32[32]{0:T(128)}, u32[]{:S(2)}) copy-start(f32[32]{0:T(128)} %param.18) | copy-start | bytes 388
  41.9 18.4 %copy-start.4 = (bf16[512]{0:T(512)(128)(2,1)S(1)}, bf16[512]{0:T(512)(128)(2,1)}, u32[]{:S(2)}) copy-start(bf16[512]{0:T(512)(128)(2,1)} %param.25) | copy-start | bytes 3076
  41.9 32.0 %copy-start.5 = (bf16[256,512]{1,0:T(8,128)(2,1)S(1)}, bf16[256,512]{1,0:T(8,128)(2,1)}, u32[]{:S(2)}) copy-start(bf16[256,512]{1,0:T(8,128)(2,1)} %param.21) | copy-start | bytes 786436
  41.9 32.0 %copy-start.7 = (f32[512]{0:T(512)S(1)}, f32[512]{0:T(512)}, u32[]{:S(2)}) copy-start(f32[512]{0:T(512)} %param.22) | copy-start | bytes 6148
  42.4 31.9 %copy-start.8 = (f32[512]{0:T(512)S(1)}, f32[512]{0:T(512)}, u32[]{:S(2)}) copy-start(f32[512]{0:T(512)} %param.24) | copy-start | bytes 6148
  47.1 26.5 %all-to-all-start = ((bf16[64,8,256]{2,1,0:T(8,128)(2,1)}), bf16[64,8,256]{2,1,0:T(8,128)(2,1)S(1)}, u32[]{:S(2)}, u32[]{:S(2)}) async-start(bf16[64,8,256]{2,1,0:T(8,128)(2,1)} %fusion.21), calls=%async_computation | async-start | bytes 524288 | tf_op jit(solution)/shard_map/all_to_all | solution.py:150
